TPU v7x, 32 devices: a whole 2x2x4 slice. The times are simulated.
32 devices in a mesh: dp: 4 (over y, x), seq: 8 (over z, core).
Axes of the slice: x: 2, y: 2, z: 4, core: 2. Of those that a mesh axis runs over, the one named last changes fastest.
Arguments:
- queries: bfloat16 [4, 8, 512, 2048], P('dp', 'seq'), may hold values from -48 to 48
- keys: bfloat16 [4, 8, 512, 2048], P('dp', 'seq'), may hold values from -6 to 6
- values: bfloat16 [4, 8, 512, 2048], P('dp', 'seq'), may hold values from -6 to 6
- out_grad: bfloat16 [4, 8, 512, 2048], P('dp', 'seq'), may hold values from -6 to 6
- out_weight: bfloat16 [2048, 2048], P('dp'), may hold values from -0.125 to 0.125
- row_mask: int32 [4, 4], replicated, may hold values from 0 to 1, as said below
- col_mask: int32 [8, 8], replicated, may hold values from 0 to 1, as said below
Outputs:
- layer_out: bfloat16 [4, 8, 512, 2048], P('dp', 'seq')
- query_grad: bfloat16 [4, 8, 512, 2048], P('dp', 'seq')
- key_grad: bfloat16 [4, 8, 512, 2048], P('dp', 'seq')
- value_grad: bfloat16 [4, 8, 512, 2048], P('dp', 'seq')
- wo_grad: float32 [2048, 2048], P(('dp', 'seq'))
Inputs may be any that keep to these rules, and one draw needn't show every extreme that they name: row_mask[a, b] is 1 for b = a and 0 for b > a. col_mask[r, s] is 1 for s = r and for s = r - 1, and 0 for s > r.
All inputs are finite; a program needn't handle non-finite values.
Results may differ from a plain program's by a relative error of at most 0.012.
Values may be sent and summed in bfloat16 or wider, within the bound.
No kernel may reach another device: no remote copies, remote signals or barrier semaphores. Data moves between devices by JAX's collectives and lax.ppermute only.
A program may use at most 192 MiB of HBM per device.

v0:
```python
import math

import jax
import jax.numpy as jnp
from jax import lax
from jax.sharding import PartitionSpec as P

DH = 128
COLS = 512
BLK = 128


masked_out = -1e30


def split_heads(tensor):
    return tensor.reshape(tensor.shape[:3] + (tensor.shape[3] // DH, DH))


def row_permit(row_mask):
    spread = jnp.repeat(jnp.repeat(row_mask, BLK, axis=0), BLK, axis=1)
    row_index = lax.broadcasted_iota(jnp.int32, (COLS, COLS), 0)
    col_index = lax.broadcasted_iota(jnp.int32, (COLS, COLS), 1)
    return (spread == 1) & (col_index <= row_index)


def row_scores(queries, keys):
    return jnp.einsum(
        "brihd,brjhd->brhij",
        split_heads(queries),
        split_heads(keys),
        preferred_element_type=jnp.float32,
    ) * (1.0 / math.sqrt(DH))


def column_scores(queries, keys):
    return jnp.einsum(
        "brchd,bschd->bchrs",
        split_heads(queries),
        split_heads(keys),
        preferred_element_type=jnp.float32,
    ) * (1.0 / math.sqrt(DH))


def row_forward(queries, keys, values, allowed):
    scores = row_scores(queries, keys)
    highest = jnp.max(jnp.where(allowed, scores, masked_out), axis=-1, keepdims=True)
    attend = jnp.exp(jnp.where(allowed, scores - highest, masked_out))
    totals = jnp.sum(attend, axis=-1, keepdims=True)
    probs = (attend / totals).astype(jnp.bfloat16)
    output = jnp.einsum(
        "brhij,brjhd->brihd", probs, split_heads(values), preferred_element_type=jnp.float32
    )
    log_total = jnp.transpose((highest + jnp.log(totals))[..., 0], (0, 1, 3, 2))
    return (output.reshape(queries.shape).astype(jnp.bfloat16), log_total)


def column_forward(queries, keys, values, allowed):
    scores = column_scores(queries, keys)
    highest = jnp.max(jnp.where(allowed, scores, masked_out), axis=-1, keepdims=True)
    attend = jnp.exp(jnp.where(allowed, scores - highest, masked_out))
    totals = jnp.sum(attend, axis=-1, keepdims=True)
    probs = (attend / totals).astype(jnp.bfloat16)
    output = jnp.einsum(
        "bchrs,bschd->brchd", probs, split_heads(values), preferred_element_type=jnp.float32
    )
    log_total = jnp.transpose((highest + jnp.log(totals))[..., 0], (0, 3, 1, 2))
    return (output.reshape(queries.shape).astype(jnp.bfloat16), log_total)


def row_backward(queries, keys, values, output, grads, log_total, allowed):
    scale = 1.0 / math.sqrt(DH)
    query_heads, key_heads, value_heads = (
        split_heads(queries),
        split_heads(keys),
        split_heads(values),
    )
    out_heads, grad_heads = (split_heads(output), split_heads(grads))
    grad_dot = jnp.einsum(
        "brihd,brihd->brhi", grad_heads, out_heads, preferred_element_type=jnp.float32
    )
    scores = row_scores(queries, keys)
    attend = jnp.exp(
        jnp.where(allowed, scores - jnp.transpose(log_total, (0, 1, 3, 2))[..., None], masked_out)
    )
    value_grad = jnp.einsum(
        "brhij,brihd->brjhd",
        attend.astype(jnp.bfloat16),
        grad_heads,
        preferred_element_type=jnp.float32,
    )
    attend_grad = jnp.einsum(
        "brihd,brjhd->brhij", grad_heads, value_heads, preferred_element_type=jnp.float32
    )
    score_grad = (attend * (attend_grad - grad_dot[..., None])).astype(jnp.bfloat16)
    query_grad = (
        jnp.einsum("brhij,brjhd->brihd", score_grad, key_heads, preferred_element_type=jnp.float32)
        * scale
    )
    key_grad = (
        jnp.einsum(
            "brhij,brihd->brjhd", score_grad, query_heads, preferred_element_type=jnp.float32
        )
        * scale
    )
    return tuple(
        (
            gradient.reshape(queries.shape).astype(jnp.bfloat16)
            for gradient in (query_grad, key_grad, value_grad)
        )
    )


def column_backward(queries, keys, values, output, grads, log_total, allowed):
    scale = 1.0 / math.sqrt(DH)
    query_heads, key_heads, value_heads = (
        split_heads(queries),
        split_heads(keys),
        split_heads(values),
    )
    out_heads, grad_heads = (split_heads(output), split_heads(grads))
    grad_dot = jnp.einsum(
        "brchd,brchd->bchr", grad_heads, out_heads, preferred_element_type=jnp.float32
    )
    scores = column_scores(queries, keys)
    attend = jnp.exp(
        jnp.where(allowed, scores - jnp.transpose(log_total, (0, 2, 3, 1))[..., None], masked_out)
    )
    value_grad = jnp.einsum(
        "bchrs,brchd->bschd",
        attend.astype(jnp.bfloat16),
        grad_heads,
        preferred_element_type=jnp.float32,
    )
    attend_grad = jnp.einsum(
        "brchd,bschd->bchrs", grad_heads, value_heads, preferred_element_type=jnp.float32
    )
    score_grad = (attend * (attend_grad - grad_dot[..., None])).astype(jnp.bfloat16)
    query_grad = (
        jnp.einsum("bchrs,bschd->brchd", score_grad, key_heads, preferred_element_type=jnp.float32)
        * scale
    )
    key_grad = (
        jnp.einsum(
            "bchrs,brchd->bschd", score_grad, query_heads, preferred_element_type=jnp.float32
        )
        * scale
    )
    return tuple(
        (
            gradient.reshape(queries.shape).astype(jnp.bfloat16)
            for gradient in (query_grad, key_grad, value_grad)
        )
    )


def project(attention, out_grad, weight):
    features = attention.shape[3]
    flat_attn = attention.reshape(-1, features)
    flat_grad = out_grad.reshape(-1, features)
    layer_out = jnp.dot(flat_attn, weight, preferred_element_type=jnp.float32).astype(jnp.bfloat16)
    attn_grad = lax.dot_general(
        flat_grad, weight, (((1,), (1,)), ((), ())), preferred_element_type=jnp.float32
    ).astype(jnp.bfloat16)
    return (layer_out.reshape(attention.shape), attn_grad.reshape(attention.shape))


def weight_gradient(attention, out_grad):
    features = attention.shape[3]
    flat_attn = attention.reshape(-1, features)
    flat_grad = out_grad.reshape(-1, features)
    devices_all = lax.axis_size(("dp", "seq"))
    tokens_all = flat_attn.shape[0] * devices_all
    summed = lax.psum_scatter(
        lax.dot_general(
            flat_attn, flat_grad, (((0,), (0,)), ((), ())), preferred_element_type=jnp.float32
        ),
        ("dp", "seq"),
        scatter_dimension=0,
        tiled=True,
    )
    return summed * (1.0 / math.sqrt(tokens_all))


def on_device(queries, keys, values, out_grad, out_weight, row_mask, col_mask):
    row_ok = row_permit(row_mask)
    col_ok = col_mask == 1
    weight = lax.all_gather(out_weight, "dp", axis=0, tiled=True)
    shipped = (
        lax.all_to_all(queries, "seq", split_axis=3, concat_axis=1, tiled=True),
        lax.all_to_all(keys, "seq", split_axis=3, concat_axis=1, tiled=True),
        lax.all_to_all(values, "seq", split_axis=3, concat_axis=1, tiled=True),
    )
    heads_all = queries.shape[3] // DH
    head_count = heads_all // lax.axis_size("seq")
    row_heads = lax.axis_index("seq") * head_count < heads_all // 2
    head_out, head_total = lax.cond(
        row_heads,
        lambda packed: row_forward(packed[0], packed[1], packed[2], row_ok),
        lambda packed: column_forward(packed[0], packed[1], packed[2], col_ok),
        shipped,
    )
    attention = lax.all_to_all(head_out, "seq", split_axis=1, concat_axis=3, tiled=True)
    layer_out, attn_grad = project(attention, out_grad, weight)
    head_grad = lax.all_to_all(attn_grad, "seq", split_axis=3, concat_axis=1, tiled=True)
    head_grads = lax.cond(
        row_heads,
        lambda packed: row_backward(*packed, row_ok),
        lambda packed: column_backward(*packed, col_ok),
        (shipped[0], shipped[1], shipped[2], head_out, head_grad, head_total),
    )
    grads = (
        lax.all_to_all(head_grads[0], "seq", split_axis=1, concat_axis=3, tiled=True),
        lax.all_to_all(head_grads[1], "seq", split_axis=1, concat_axis=3, tiled=True),
        lax.all_to_all(head_grads[2], "seq", split_axis=1, concat_axis=3, tiled=True),
    )
    wo_grad = weight_gradient(attention, out_grad)
    return (layer_out, grads[0], grads[1], grads[2], wo_grad)


def solution(mesh):
    in_specs = (
        P("dp", "seq", None, None),
        P("dp", "seq", None, None),
        P("dp", "seq", None, None),
        P("dp", "seq", None, None),
        P("dp", None),
        P(),
        P(),
    )
    out_specs = (
        P("dp", "seq", None, None),
        P("dp", "seq", None, None),
        P("dp", "seq", None, None),
        P("dp", "seq", None, None),
        P(("dp", "seq"), None),
    )
    return jax.shard_map(
        on_device, mesh=mesh, in_specs=in_specs, out_specs=out_specs, check_vma=False
    )
```

profile of v0, /device:TPU:0, one launch (start us, length us, event | category | flops | bytes accessed | tf_op | source)
XLA Modules:
  0.0 712.1 jit_solution(11204183050144207562)
XLA Ops:
  8.0 10.9 %copy.231 = bf16[1,1,512,2048]{2,1,0,3:T(2,128)(2,1)} copy(bf16[1,1,512,2048]{3,2,1,0:T(8,128)(2,1)} %param.11) | data formatting | bytes 4194304 | tf_op args[0]
  19.5 15.4 %reduce.12 = bf16[2048,512]{1,0:T(8,128)(2,1)} reduce(bf16[2048,1,1,512]{3,2,1,0:T(2,128)(2,1)} %bitcast.213, bf16[]{:T(256)} %broadcast.108), dimensions={1,2}, to_apply=%bitcast.145.reduce_sub_computation | reduce | bytes 4194306
  34.9 6.3 reshape.345
  41.1 6.3 all-to-all-start
  48.2 10.8 %copy.232 = bf16[1,1,512,2048]{2,1,0,3:T(2,128)(2,1)} copy(bf16[1,1,512,2048]{3,2,1,0:T(8,128)(2,1)} %param.12) | data formatting | bytes 4194304 | tf_op args[1]
  59.0 15.5 %reduce.13 = bf16[2048,512]{1,0:T(8,128)(2,1)} reduce(bf16[2048,1,1,512]{3,2,1,0:T(2,128)(2,1)} %bitcast.219, bf16[]{:T(256)} %broadcast.108), dimensions={1,2}, to_apply=%bitcast.147.reduce_sub_computation | reduce | bytes 4194306
  74.5 6.3 reshape.347
  80.8 15.9 %all-to-all-done = bf16[8,2,65536]{2,1,0:T(2,128)(2,1)} async-done(((bf16[8,2,65536]{2,1,0:T(2,128)(2,1)}), bf16[8,2,65536]{2,1,0:T(2,128)(2,1)}, u32[]{:S(2)}, u32[]{:S(2)}) %all-to-all-start) | async-done | bytes 2097184 | tf_op jit(solution)/shard_map/all_to_all | solution.py:190
  96.6 4.4 all-to-all-start.1
  101.0 10.8 %copy.233 = bf16[1,1,512,2048]{2,1,0,3:T(2,128)(2,1)} copy(bf16[1,1,512,2048]{3,2,1,0:T(8,128)(2,1)} %param.13) | data formatting | bytes 4194304 | tf_op args[2]
  111.8 15.4 %reduce.14 = bf16[2048,512]{1,0:T(8,128)(2,1)} reduce(bf16[2048,1,1,512]{3,2,1,0:T(2,128)(2,1)} %bitcast.220, bf16[]{:T(256)} %broadcast.108), dimensions={1,2}, to_apply=%bitcast.149.reduce_sub_computation | reduce | bytes 4194306
  127.1 6.3 reshape.349
  133.4 16.6 %all-to-all-done.1 = bf16[8,2,65536]{2,1,0:T(2,128)(2,1)} async-done(((bf16[8,2,65536]{2,1,0:T(2,128)(2,1)}), bf16[8,2,65536]{2,1,0:T(2,128)(2,1)}, u32[]{:S(2)}, u32[]{:S(2)}) %all-to-all-start.1) | async-done | bytes 2097184 | tf_op jit(solution)/shard_map/all_to_all | solution.py:191
  150.1 4.4 all-to-all-start.2
  156.3 6.7 reshape.346
  163.1 4.1 copy.307
  167.2 6.7 reshape.348
  173.9 4.1 copy.308
  178.0 25.5 %all-to-all-done.2 = bf16[8,2,65536]{2,1,0:T(2,128)(2,1)} async-done(((bf16[8,2,65536]{2,1,0:T(2,128)(2,1)}), bf16[8,2,65536]{2,1,0:T(2,128)(2,1)}, u32[]{:S(2)}, u32[]{:S(2)}) %all-to-all-start.2) | async-done | bytes 2097184 | tf_op jit(solution)/shard_map/all_to_all | solution.py:192
  203.5 6.7 reshape.350
  210.3 4.1 copy.309
  214.4 33.1 %conditional.4 = (f32[1,8,512,2]{2,1,3,0:T(8,128)S(1)}, bf16[1,8,512,2,128]{4,1,3,2,0:T(8,128)(2,1)}) conditional(s32[]{:T(128)} %convert_element_type.105, (pred[8,8]{1,0:T(8,128)(4,1)S(1)}, bf16[1,8,512,256]{2,3,1,0:T(8,128)(2,1)}, bf16[1,8,512,256]{2,3,1,0:T(8,128)(2,1)}, bf16[1,8,512,256]{2,3,1,0:T(8,128)(2,1)}) %tuple.97, ...), branch_computations={%region_0.3_spmd, %region_3.6_spmd} | conditional | flops 2198855680 | bytes 64552976
  215.1 11.0 %select_reduce_fusion.1 = (f32[8,2,512]{2,1,0:T(2,128)S(1)}, f32[8,2,512,512]{2,3,1,0:T(8,128)}) fusion(pred[512,512]{0,1:T(8,128)(4,1)S(1)} %copy.237, bf16[8,512,2,128]{1,3,2,0:T(8,128)(2,1)} %bitcast.12, bf16[8,512,2,128]{1,3,2,0:T(8,128)(2,1)} %bitcast.189), kind=kOutput, calls=%fused_computation.8 | convolution fusion | flops 1086316544 | bytes 21266432 | tf_op jit(solution)/shard_map/cond/branch_1_fun/brihd,brjhd->brhij/dot_general | solution.py:28
  226.0 9.3 %fusion.1 = f32[8,2,512]{2,1,0:T(2,128)S(1)} fusion(f32[8,2,512,512]{2,3,1,0:T(8,128)} %get-tuple-element.236, f32[8,2,512]{2,1,0:T(2,128)S(1)} %get-tuple-element.235, pred[512,512]{0,1:T(8,128)(4,1)S(1)} %copy.237), kind=kLoop, calls=%fused_computation.9 | loop fusion | flops 16769024 | bytes 17104896 | tf_op jit(solution)/shard_map/cond/branch_1_fun/reduce_sum | solution.py:49
  235.4 9.5 %convert_bitcast_fusion.1 = bf16[1,8,512,2,128]{4,2,3,1,0:T(8,128)(2,1)S(1)} fusion(bf16[8,512,2,128]{1,3,2,0:T(8,128)(2,1)} %bitcast.210, f32[8,2,512,512]{2,3,1,0:T(8,128)} %get-tuple-element.236, f32[8,2,512]{2,1,0:T(2,128)S(1)} %fusion.1, f32[8,2,512]{2,1,0:T(2,128)S(1)} %get-tuple-element.235, pred[512,512]{0,1:T(8,128)(4,1)S(1)} %copy.237), kind=kOutput, calls=%fused_computation.11 | convolution fusion | flops 1095761920 | bytes 21299200 | tf_op jit(solution)/shard_map/cond/branch_1_fun/brhij,brjhd->brihd/dot_general | solution.py:51
  244.8 2.7 copy.206
  247.5 4.3 copy.238
  251.8 52.7 %all_to_all.141 = bf16[1,8,512,256]{2,3,0,1:T(8,128)(2,1)S(1)} all-to-all(bf16[1,8,512,256]{2,3,0,1:T(8,128)(2,1)} %bitcast.200), channel_id=1, replica_groups=mesh['dp'=4,'seq'=8] {'seq'}, dimensions={1} | all-to-all | bytes 4194304 | tf_op jit(solution)/shard_map/all_to_all | solution.py:203
  305.9 8.2 %fusion.21 = f32[2048,2048]{1,0:T(8,128)} fusion(bf16[512,2048]{0,1:T(8,128)(2,1)S(1)} %bitcast.224, bf16[1,1,512,2048]{3,2,1,0:T(8,128)(2,1)S(1)} %copy-done), kind=kOutput, calls=%fused_computation.42 | convolution fusion | flops 4294967296 | bytes 20971520 | tf_op jit(solution)/shard_map/dot_general | solution.py:175
  314.1 9.1 %fusion.20 = bf16[1,1,512,2048]{3,2,1,0:T(8,128)(2,1)} fusion(bf16[2048,2048]{1,0:T(8,128)(2,1)} %all-gather.2.cloned.1.call-done, bf16[1,1,512,2048]{3,2,1,0:T(8,128)(2,1)S(1)} %copy-done), kind=kOutput, calls=%fused_computation.41 | convolution fusion | flops 4296015872 | bytes 12582912 | tf_op jit(solution)/shard_map/dot_general | solution.py:162
  323.2 10.8 %copy.239 = bf16[1,1,512,2048]{2,1,0,3:T(2,128)(2,1)} copy(bf16[1,1,512,2048]{3,2,1,0:T(8,128)(2,1)} %fusion.20) | data formatting | bytes 4194304 | tf_op jit(solution)/shard_map/reshape | solution.py:165
  334.0 14.1 %reduce.15 = bf16[2048,512]{1,0:T(8,128)(2,1)S(1)} reduce(bf16[2048,1,1,512]{3,2,1,0:T(2,128)(2,1)} %bitcast.214, bf16[]{:T(256)} %broadcast.108), dimensions={1,2}, to_apply=%bitcast.151.reduce_sub_computation | reduce | bytes 4194306
  348.1 3.8 reshape.351
  351.9 84.2 %all_to_all.142 = bf16[8,2,65536]{2,1,0:T(2,128)(2,1)S(1)} all-to-all(bf16[8,2,65536]{2,1,0:T(2,128)(2,1)} %reshape.351), channel_id=1, replica_groups=mesh['dp'=4,'seq'=8] {'seq'}, dimensions={0} | all-to-all | bytes 4194304 | tf_op jit(solution)/shard_map/all_to_all | solution.py:205
  436.0 4.4 reshape.352
  440.4 4.3 copy.310
  444.6 83.8 %conditional.10 = (bf16[1,8,512,2,128]{4,1,3,2,0:T(8,128)(2,1)}, bf16[1,8,512,2,128]{4,1,3,2,0:T(8,128)(2,1)}, bf16[1,8,512,2,128]{4,1,3,2,0:T(8,128)(2,1)}) conditional(s32[]{:T(128)} %convert_element_type.105, (pred[8,8]{1,0:T(8,128)(4,1)S(1)}, bf16[1,8,512,256]{2,3,1,0:T(8,128)(2,1)}, bf16[1,8,512,256]{2,3,1,0:T(8,128)(2,1)S(1)}, ...), branch_computations={%region_6.7_spmd, %region_7.8_spmd} | conditional | flops 5417984000 | bytes 135004224 | solution.py:206
  452.5 9.7 %fusion.28 = f32[8,2,512,512]{3,2,1,0:T(8,128)} fusion(bf16[8,512,2,128]{1,3,2,0:T(8,128)(2,1)} %bitcast.38, bf16[8,512,2,128]{1,3,2,0:T(8,128)(2,1)S(1)} %bitcast.191), kind=kOutput, calls=%fused_computation.53 | convolution fusion | flops 1073741824 | bytes 20971520 | tf_op jit(solution)/shard_map/cond/branch_1_fun/brihd,brjhd->brhij/dot_general | solution.py:28
  462.2 6.4 copy.276
  468.6 6.2 copy.305
  474.8 8.8 %multiply_reduce_fusion = f32[8,2,512]{1,2,0:T(8,128)} fusion(f32[8,2,512,128]{3,1,2,0:T(2,128)} %copy.276, bf16[8,512,2,128]{3,2,1,0:T(2,128)(2,1)} %copy.305), kind=kLoop, calls=%fused_computation.31 | loop fusion | flops 3137536 | bytes 6324224 | tf_op jit(solution)/shard_map/cond
  485.9 12.7 %multiply_convert_fusion.1 = bf16[8,2,512,512]{3,2,1,0:T(8,128)(2,1)} fusion(f32[8,2,512,512]{3,2,1,0:T(8,128)} %fusion.28, bf16[8,512,2,128]{1,3,2,0:T(8,128)(2,1)} %bitcast.198, bf16[8,512,2,128]{1,3,2,0:T(8,128)(2,1)} %bitcast.212, f32[8,2,512]{2,1,0:T(2,128)S(1)} %copy.277, f32[8,2,512]{2,1,0:T(2,128)S(1)} %bitcast.229, ...), kind=kOutput, calls=%fused_computation.23 | convolution fusion | flops 1098907648 | bytes 29687808 | tf_op jit(solution)/shard_map/cond/branch_1_fun/brihd,brjhd->brhij/dot_general | solution.py:92
  498.5 5.8 multiply_bitcast_fusion.3
  504.4 2.7 copy.228
  507.0 6.6 multiply_bitcast_fusion.2
  513.7 2.7 copy.229
  516.4 9.3 %fusion.14 = bf16[1,8,512,2,128]{4,2,3,1,0:T(8,128)(2,1)S(1)} fusion(bf16[8,512,2,128]{1,3,2,0:T(8,128)(2,1)S(1)} %bitcast.199, f32[8,2,512,512]{3,2,1,0:T(8,128)} %fusion.28, f32[8,2,512]{2,1,0:T(2,128)S(1)} %bitcast.230, pred[512,512]{1,0:T(8,128)(4,1)S(1)} %get-tuple-element.70), kind=kOutput, calls=%fused_computation.34 | convolution fusion | flops 1090519040 | bytes 21266432 | tf_op jit(solution)/shard_map/cond/branch_1_fun/brhij,brihd->brjhd/dot_general | solution.py:86
  525.6 2.6 copy.230
  528.5 3.2 copy.247
  534.3 3.6 all-to-all-start.5
  537.9 4.5 copy.249
  542.5 4.4 reshape.337
  546.8 40.4 %all-to-all-done.5 = bf16[1,8,512,256]{3,2,0,1:T(8,128)(2,1)S(1)} async-done(((bf16[1,8,512,256]{3,2,0,1:T(8,128)(2,1)}), bf16[1,8,512,256]{3,2,0,1:T(8,128)(2,1)S(1)}, u32[]{:S(2)}, u32[]{:S(2)}) %all-to-all-start.5) | async-done | bytes 2097184 | tf_op jit(solution)/shard_map/all_to_all | solution.py:213
  587.2 4.4 all-to-all-start.6
  591.6 4.5 copy.251
  596.1 4.4 reshape.338
  600.5 40.2 %all-to-all-done.6 = bf16[1,8,512,256]{3,2,0,1:T(8,128)(2,1)} async-done(((bf16[1,8,512,256]{3,2,0,1:T(8,128)(2,1)}), bf16[1,8,512,256]{3,2,0,1:T(8,128)(2,1)}, u32[]{:S(2)}, u32[]{:S(2)}) %all-to-all-start.6) | async-done | bytes 2097184 | tf_op jit(solution)/shard_map/all_to_all | solution.py:214
  640.7 4.6 all-to-all-start.7
  645.3 9.9 %fusion.19 = bf16[1,1,512,2048]{3,2,1,0:T(8,128)(2,1)} fusion(bf16[512,2048]{0,1:T(8,128)(2,1)} %bitcast.225, bf16[2048,2048]{1,0:T(8,128)(2,1)} %all-gather.2.cloned.1.call-done), kind=kOutput, calls=%fused_computation.40 | convolution fusion | flops 4296015872 | bytes 12582912 | tf_op jit(solution)/shard_map/dot_general | solution.py:161
  657.5 3.9 copy.253
  661.4 2.9 copy.250
  666.7 27.6 %all-to-all-done.7 = bf16[1,8,512,256]{3,2,0,1:T(8,128)(2,1)} async-done(((bf16[1,8,512,256]{3,2,0,1:T(8,128)(2,1)}), bf16[1,8,512,256]{3,2,0,1:T(8,128)(2,1)}, u32[]{:S(2)}, u32[]{:S(2)}) %all-to-all-start.7) | async-done | bytes 2097184 | tf_op jit(solution)/shard_map/all_to_all | solution.py:215
  694.3 3.9 copy.252
  698.2 4.1 copy.255
  (35 shorter events, 16.4 us)
Async XLA Ops:
  8.0 297.9 %copy-start = (bf16[1,1,512,2048]{3,2,1,0:T(8,128)(2,1)S(1)}, bf16[1,1,512,2048]{3,2,1,0:T(8,128)(2,1)}, u32[]{:S(2)}) copy-start(bf16[1,1,512,2048]{3,2,1,0:T(8,128)(2,1)} %param.14) | copy-start | bytes 6291460
  41.1 55.5 %all-to-all-start = ((bf16[8,2,65536]{2,1,0:T(2,128)(2,1)}), bf16[8,2,65536]{2,1,0:T(2,128)(2,1)}, u32[]{:S(2)}, u32[]{:S(2)}) async-start(bf16[8,2,65536]{2,1,0:T(2,128)(2,1)} %reshape.345), calls=%async_computation | async-start | bytes 4194304 | tf_op jit(solution)/shard_map/all_to_all | solution.py:190
  47.5 266.7 %all-gather.2.cloned.1.call-start = ((), (), s32[]{:S(2)}) async-start(), calls=%async_computation.9 | async-start | bytes 10485760 | tf_op jit(solution)/shard_map/all_gather | solution.py:188
  96.6 53.4 %all-to-all-start.1 = ((bf16[8,2,65536]{2,1,0:T(2,128)(2,1)}), bf16[8,2,65536]{2,1,0:T(2,128)(2,1)}, u32[]{:S(2)}, u32[]{:S(2)}) async-start(bf16[8,2,65536]{2,1,0:T(2,128)(2,1)} %reshape.347), calls=%async_computation.1 | async-start | bytes 4194304 | tf_op jit(solution)/shard_map/all_to_all | solution.py:191
  133.4 21.1 %copy-start.9 = (s32[4,4]{1,0:T(4,128)S(1)}, s32[4,4]{1,0:T(4,128)}, u32[]{:S(2)}) copy-start(s32[4,4]{1,0:T(4,128)} %param.16) | copy-start | bytes 196
  133.4 21.1 %copy-start.8 = (s32[8,8]{1,0:T(8,128)S(1)}, s32[8,8]{1,0:T(8,128)}, u32[]{:S(2)}) copy-start(s32[8,8]{1,0:T(8,128)} %param.17) | copy-start | bytes 772
  150.1 53.4 %all-to-all-start.2 = ((bf16[8,2,65536]{2,1,0:T(2,128)(2,1)}), bf16[8,2,65536]{2,1,0:T(2,128)(2,1)}, u32[]{:S(2)}, u32[]{:S(2)}) async-start(bf16[8,2,65536]{2,1,0:T(2,128)(2,1)} %reshape.349), calls=%async_computation.2 | async-start | bytes 4194304 | tf_op jit(solution)/shard_map/all_to_all | solution.py:192
  154.5 547.8 %reduce-scatter.2.cloned.1.call-start = ((), (), s32[]{:S(2)}) async-start(), calls=%async_computation.10 | async-start | bytes 17301504 | tf_op jit(solution)/shard_map/reduce_scatter | solution.py:174
  304.6 1.3 copy-start.7
  440.4 4.3 copy-start.2
  513.6 2.7 copy-start.4
  534.3 52.9 %all-to-all-start.5 = ((bf16[1,8,512,256]{3,2,0,1:T(8,128)(2,1)}), bf16[1,8,512,256]{3,2,0,1:T(8,128)(2,1)S(1)}, u32[]{:S(2)}, u32[]{:S(2)}) async-start(bf16[1,8,512,256]{3,2,0,1:T(8,128)(2,1)} %reshape.336), calls=%async_computation.5 | async-start | bytes 4194304 | tf_op jit(solution)/shard_map/all_to_all | solution.py:213
  587.2 53.4 %all-to-all-start.6 = ((bf16[1,8,512,256]{3,2,0,1:T(8,128)(2,1)}), bf16[1,8,512,256]{3,2,0,1:T(8,128)(2,1)}, u32[]{:S(2)}, u32[]{:S(2)}) async-start(bf16[1,8,512,256]{3,2,0,1:T(8,128)(2,1)} %reshape.337), calls=%async_computation.6 | async-start | bytes 4194304 | tf_op jit(solution)/shard_map/all_to_all | solution.py:214
  640.7 53.7 %all-to-all-start.7 = ((bf16[1,8,512,256]{3,2,0,1:T(8,128)(2,1)}), bf16[1,8,512,256]{3,2,0,1:T(8,128)(2,1)}, u32[]{:S(2)}, u32[]{:S(2)}) async-start(bf16[1,8,512,256]{3,2,0,1:T(8,128)(2,1)} %reshape.338), calls=%async_computation.7 | async-start | bytes 4194304 | tf_op jit(solution)/shard_map/all_to_all | solution.py:215
  698.2 5.9 copy-start.1
Sparse Core Ops, SparseCore 0:
  50.1 89.0 all-gather.1
Sparse Core Ops, SparseCore 1:
  314.2 225.1 reduce-scatter.1
where the time goes:
time: 724 us; the launch traced here: 712 us
  local copies, waits for them, and re-layouts  184 us (25%)
  waiting for transfers between devices  167 us (23%)
  blocking collectives  137 us (19%)
  matrix products  91.7 us (13%)
  other arithmetic  80.3 us (11%)
  starting transfers between devices  27.7 us (4%)
  between operations  16.1 us (2%)
  loops' own time  8.47 us (1%)
    unnamed x32, local copies, waits for them, and re-layouts  113 us
    all_to_all x1, blocking collectives, on_device(): lax.all_to_all(attn_grad, 'seq', split_axis=3, concat_axis=1, tiled=True)  84.2 us
    unnamed x4, other arithmetic  60.3 us
    all_to_all x1, blocking collectives, on_device(): lax.all_to_all(head_out, 'seq', split_axis=1, concat_axis=3, tiled=True)  52.7 us
    all_to_all x1, waiting for transfers between devices, on_device(): lax.all_to_all(head_grads[0], 'seq', split_axis=1, concat_axis=3, tiled=T...  40.4 us
    all_to_all x1, waiting for transfers between devices, on_device(): lax.all_to_all(head_grads[1], 'seq', split_axis=1, concat_axis=3, tiled=T...  40.2 us
    all_to_all x1, waiting for transfers between devices, on_device(): lax.all_to_all(head_grads[2], 'seq', split_axis=1, concat_axis=3, tiled=T...  27.6 us
    all_to_all x1, waiting for transfers between devices, on_device(): lax.all_to_all(values, 'seq', split_axis=3, concat_axis=1, tiled=True)  25.5 us
  transfers between devices with their start and end apart: 8, of which 6 were waited for; matrix products, arithmetic and copies ran while one was open for 45% of the time, Pallas kernels for 0%

commit v1 on v0

v1 whole, which is shorter than its diff:
```python
import math

import jax
import jax.numpy as jnp
from jax import lax
from jax.sharding import PartitionSpec as P

DH = 128
COLS = 512
BLK = 128

masked_out = -1e30
scale = 1.0 / math.sqrt(DH)


def row_permit(row_mask):
    spread = jnp.repeat(jnp.repeat(row_mask, BLK, axis=0), BLK, axis=1)
    row_index = lax.broadcasted_iota(jnp.int32, (COLS, COLS), 0)
    col_index = lax.broadcasted_iota(jnp.int32, (COLS, COLS), 1)
    return (spread == 1) & (col_index <= row_index)


def softmax_parts(scores, allowed):
    highest = jnp.max(jnp.where(allowed, scores, masked_out), axis=-1, keepdims=True)
    attend = jnp.exp(jnp.where(allowed, scores - highest, masked_out))
    totals = jnp.sum(attend, axis=-1, keepdims=True)
    probs = (attend / totals).astype(jnp.bfloat16)
    return probs, highest + jnp.log(totals)


def row_forward(q, k, v, allowed):
    scores = jnp.einsum("ihd,jhd->hij", q, k, preferred_element_type=jnp.float32) * scale
    probs, log_total = softmax_parts(scores, allowed[None])
    out = jnp.einsum("hij,jhd->ihd", probs, v, preferred_element_type=jnp.float32)
    return out.astype(jnp.bfloat16), scores, log_total


def row_backward(q, k, v, out, grad, scores, log_total, allowed):
    grad_dot = jnp.einsum("ihd,ihd->hi", grad, out, preferred_element_type=jnp.float32)
    back = jnp.where(allowed[None], jnp.exp(scores - log_total), 0.0)
    value_grad = jnp.einsum(
        "hij,ihd->jhd", back.astype(jnp.bfloat16), grad, preferred_element_type=jnp.float32
    )
    prob_grad = jnp.einsum("ihd,jhd->hij", grad, v, preferred_element_type=jnp.float32)
    score_grad = (back * (prob_grad - grad_dot[..., None])).astype(jnp.bfloat16)
    query_grad = jnp.einsum("hij,jhd->ihd", score_grad, k, preferred_element_type=jnp.float32)
    key_grad = jnp.einsum("hij,ihd->jhd", score_grad, q, preferred_element_type=jnp.float32)
    return tuple(
        g.astype(jnp.bfloat16) for g in (query_grad * scale, key_grad * scale, value_grad)
    )


def column_forward(q, k, v, allowed):
    scores = jnp.einsum("rchd,schd->chrs", q, k, preferred_element_type=jnp.float32) * scale
    probs, log_total = softmax_parts(scores, allowed)
    out = jnp.einsum("chrs,schd->rchd", probs, v, preferred_element_type=jnp.float32)
    return out.astype(jnp.bfloat16), scores, log_total


def column_backward(q, k, v, out, grad, scores, log_total, allowed):
    grad_dot = jnp.einsum("rchd,rchd->chr", grad, out, preferred_element_type=jnp.float32)
    back = jnp.where(allowed, jnp.exp(scores - log_total), 0.0)
    value_grad = jnp.einsum(
        "chrs,rchd->schd", back.astype(jnp.bfloat16), grad, preferred_element_type=jnp.float32
    )
    prob_grad = jnp.einsum("rchd,schd->chrs", grad, v, preferred_element_type=jnp.float32)
    score_grad = (back * (prob_grad - grad_dot[..., None])).astype(jnp.bfloat16)
    query_grad = jnp.einsum("chrs,schd->rchd", score_grad, k, preferred_element_type=jnp.float32)
    key_grad = jnp.einsum("chrs,rchd->schd", score_grad, q, preferred_element_type=jnp.float32)
    return tuple(
        g.astype(jnp.bfloat16) for g in (query_grad * scale, key_grad * scale, value_grad)
    )


def on_device(queries, keys, values, out_grad, out_weight, row_mask, col_mask):
    tokens, features = queries.shape[2], queries.shape[3]
    half = features // 2
    heads_half = half // DH
    rows = lax.axis_size("seq")
    cols_each = tokens // rows

    weight = lax.all_gather(out_weight, "dp", axis=0, tiled=True)

    packed = jnp.stack([t[0, 0, :, half:] for t in (queries, keys, values)])
    shipped = lax.all_to_all(packed[None], "seq", split_axis=2, concat_axis=0, tiled=True)
    col_q, col_k, col_v = (
        shipped[:, i].reshape(rows, cols_each, heads_half, DH) for i in range(3)
    )
    col_ok = col_mask == 1
    col_out, col_scores, col_total = column_forward(col_q, col_k, col_v, col_ok)
    col_back = lax.all_to_all(
        col_out.reshape(rows, cols_each, half), "seq", split_axis=0, concat_axis=1, tiled=True
    )

    row_ok = row_permit(row_mask)
    split = lambda t: t[0, 0, :, :half].reshape(tokens, heads_half, DH)
    row_q, row_k, row_v = split(queries), split(keys), split(values)
    row_out, row_scores, row_total = row_forward(row_q, row_k, row_v, row_ok)

    flat_grad = out_grad[0, 0]
    attn_grad = lax.dot_general(
        flat_grad, weight, (((1,), (1,)), ((), ())), preferred_element_type=jnp.float32
    ).astype(jnp.bfloat16)
    grad_cols = lax.all_to_all(
        attn_grad[None, :, half:], "seq", split_axis=1, concat_axis=0, tiled=True
    ).reshape(rows, cols_each, heads_half, DH)
    col_grads = column_backward(
        col_q, col_k, col_v, col_out, grad_cols, col_scores, col_total, col_ok
    )
    col_grads_back = lax.all_to_all(
        jnp.stack([g.reshape(rows, cols_each, half) for g in col_grads]),
        "seq",
        split_axis=1,
        concat_axis=2,
        tiled=True,
    )

    row_grads = row_backward(
        row_q,
        row_k,
        row_v,
        row_out,
        attn_grad[:, :half].reshape(tokens, heads_half, DH),
        row_scores,
        row_total,
        row_ok,
    )

    attention = jnp.concatenate([row_out.reshape(tokens, half), col_back[0]], axis=1)
    layer_out = jnp.dot(attention, weight, preferred_element_type=jnp.float32).astype(
        jnp.bfloat16
    )

    devices_all = lax.axis_size(("dp", "seq"))
    partial = lax.dot_general(
        attention, flat_grad, (((0,), (0,)), ((), ())), preferred_element_type=jnp.float32
    )
    wo_grad = lax.psum_scatter(partial, ("dp", "seq"), scatter_dimension=0, tiled=True) * (
        1.0 / math.sqrt(tokens * devices_all)
    )

    grads = [
        jnp.concatenate([row_grads[i].reshape(tokens, half), col_grads_back[i, 0]], axis=1)[
            None, None
        ]
        for i in range(3)
    ]
    return (layer_out[None, None], grads[0], grads[1], grads[2], wo_grad)


def solution(mesh):
    in_specs = (
        P("dp", "seq", None, None),
        P("dp", "seq", None, None),
        P("dp", "seq", None, None),
        P("dp", "seq", None, None),
        P("dp", None),
        P(),
        P(),
    )
    out_specs = (
        P("dp", "seq", None, None),
        P("dp", "seq", None, None),
        P("dp", "seq", None, None),
        P("dp", "seq", None, None),
        P(("dp", "seq"), None),
    )
    return jax.shard_map(
        on_device, mesh=mesh, in_specs=in_specs, out_specs=out_specs, check_vma=False
    )
```

time: 724 us -> 482 us (0.67)
  blocking collectives: 137 us -> 0 us
  local copies, waits for them, and re-layouts: 184 us -> 86.6 us
  waiting for transfers between devices: 167 us -> 257 us
  other arithmetic: 80.3 us -> 25.5 us
  matrix products: 91.7 us -> 70.7 us
  loops' own time: 8.47 us -> 0 us
    all_to_all x2 -> x0, blocking collectives: 137 us -> none  [the longest x1 84.2 us: on_device(): lax.all_to_all(attn_grad, 'seq', split_axis=3, concat_axis=1, tiled=True)]
    reduce_scatter x1, waiting for transfers between devices: 0.01 us -> 96.5 us  [on_device(): lax.psum_scatter(partial, ('dp', 'seq'), scatter_dimension=0, tiled=True)]
    unnamed x32 -> x74, local copies, waits for them, and re-layouts: 113 us -> 27.9 us
    all_to_all x6 -> x4, waiting for transfers between devices: 166 us -> 88.9 us  [the longest x1 82.1 us: on_device(): lax.all_to_all(jnp.stack([g.reshape(rows, cols_each, half) for g in col_g...]
    all_gather x1, waiting for transfers between devices: 0.02 us -> 71.1 us  [on_device(): weight = lax.all_gather(out_weight, 'dp', axis=0, tiled=True)]
    unnamed x4 -> x3, other arithmetic: 60.3 us -> 10.7 us
    dot_general x10 -> x15, matrix products: 91.7 us -> 70.7 us  [the longest x1 9.73 us: on_device(): lax.dot_general(attention, flat_grad, (((0,), (0,)), ((), ())), preferred...]
    cond x7 -> x0, local copies, waits for them, and re-layouts: 20.6 us -> none
  transfers between devices with their start and end apart: 8 -> 6, of which waited for: 6 -> 5; matrix products, arithmetic and copies ran while one was open for 45% -> 30% of each run, Pallas kernels for 0% -> 0%
where the time goes in v1:
time: 482 us; the launch traced here: 475 us
  waiting for transfers between devices  257 us (53%)
  local copies, waits for them, and re-layouts  86.6 us (18%)
  matrix products  70.7 us (15%)
  other arithmetic  25.5 us (5%)
  starting transfers between devices  20.5 us (4%)
  between operations  14.8 us (3%)
    reduce_scatter x1, waiting for transfers between devices, on_device(): lax.psum_scatter(partial, ('dp', 'seq'), scatter_dimension=0, tiled=True)  96.5 us
    all_to_all x1, waiting for transfers between devices, on_device(): lax.all_to_all(jnp.stack([g.reshape(rows, cols_each, half) for g in col_g...  82.1 us
    all_gather x1, waiting for transfers between devices, on_device(): weight = lax.all_gather(out_weight, 'dp', axis=0, tiled=True)  71.1 us
    unnamed x74, local copies, waits for them, and re-layouts  27.9 us
    unnamed x3, other arithmetic  10.7 us
    dot_general x1, matrix products, on_device(): lax.dot_general(attention, flat_grad, (((0,), (0,)), ((), ())), preferred...  9.73 us
  transfers between devices with their start and end apart: 6, of which 5 were waited for; matrix products, arithmetic and copies ran while one was open for 30% of the time, Pallas kernels for 0%

profile of v1, /device:TPU:0, one launch (start us, length us, event | category | flops | bytes accessed | tf_op | source)
XLA Modules:
  0.0 475.2 jit_solution(15149277100078210538)
XLA Ops:
  7.9 2.9 fusion.43
  10.9 1.9 fusion.41
  13.1 4.7 copy.147
  17.9 6.7 %all-to-all-start = ((bf16[1,3,512,1024]{3,1,0,2:T(4,128)(2,1)}), bf16[1,3,512,1024]{3,1,0,2:T(4,128)(2,1)}, u32[]{:S(2)}, u32[]{:S(2)}) async-start(bf16[1,3,512,1024]{3,1,0,2:T(4,128)(2,1)} %copy.147), calls=%async_computation | async-start | bytes 8388608 | tf_op jit(solution)/shard_map/all_to_all | solution.py:85
  24.9 1.6 copy.202
  26.5 2.7 copy.201
  29.1 71.1 %all-gather.2.cloned.1.call-done = bf16[2048,2048]{1,0:T(8,128)(2,1)} async-done(((bf16[512,2048]{1,0:T(8,128)(2,1)}), bf16[2048,2048]{1,0:T(8,128)(2,1)}) %all-gather.2.cloned.1.call-update) | async-done | bytes 8388624 | tf_op jit(solution)/shard_map/all_gather | solution.py:82
  100.2 8.1 %convolution_convert_fusion = bf16[512,2048]{1,0:T(8,128)(2,1)S(1)} fusion(bf16[2048,2048]{1,0:T(8,128)(2,1)} %all-gather.2.cloned.1.call-done, bf16[1,1,512,2048]{3,2,1,0:T(8,128)(2,1)S(1)} %copy-done), kind=kOutput, calls=%fused_computation.16 | convolution fusion | flops 4296015872 | bytes 12582912 | tf_op jit(solution)/shard_map/dot_general | solution.py:101
  108.3 1.2 slice_bitcast_fusion.1
  109.5 2.9 copy.233
  113.0 9.0 %reduce.6 = bf16[512,1024]{1,0:T(8,128)(2,1)} reduce(bf16[512,1,1024]{2,1,0:T(2,128)(2,1)} %bitcast.142, bf16[]{:T(256)} %broadcast.37), dimensions={1}, to_apply=%bitcast.127.reduce_sub_computation | reduce | bytes 2097154
  122.0 2.6 reshape.105
  124.6 4.9 %all-to-all-start.2 = ((bf16[8,2,32768]{2,1,0:T(2,128)(2,1)}), bf16[8,2,32768]{2,1,0:T(2,128)(2,1)}, u32[]{:S(2)}, u32[]{:S(2)}) async-start(bf16[8,2,32768]{2,1,0:T(2,128)(2,1)} %reshape.105), calls=%async_computation.2 | async-start | bytes 2097152 | tf_op jit(solution)/shard_map/all_to_all | solution.py:104
  129.5 6.1 %select_reduce_fusion = (f32[8,512]{1,0:T(8,128)S(1)}, f32[8,512,512]{1,2,0:T(8,128)}) fusion(pred[512,512]{0,1:T(8,128)(4,1)S(1)} %fusion.20, bf16[512,8,128]{0,2,1:T(8,128)(2,1)} %bitcast.152, bf16[512,8,128]{0,2,1:T(8,128)(2,1)S(1)} %bitcast.140), kind=kOutput, calls=%fused_computation.4 | convolution fusion | flops 543158272 | bytes 10764288 | tf_op jit(solution)/shard_map/ihd,jhd->hij/dot_general | solution.py:32
  135.6 3.4 copy.231
  139.4 1.3 copy.204
  141.2 1.1 copy-done.6
  142.3 2.6 fusion.27
  144.9 2.7 copy.151
  148.0 2.4 copy.153
  150.5 5.7 %all-to-all-done.2 = bf16[8,2,32768]{2,1,0:T(2,128)(2,1)} async-done(((bf16[8,2,32768]{2,1,0:T(2,128)(2,1)}), bf16[8,2,32768]{2,1,0:T(2,128)(2,1)}, u32[]{:S(2)}, u32[]{:S(2)}) %all-to-all-start.2) | async-done | bytes 1048608 | tf_op jit(solution)/shard_map/all_to_all | solution.py:104
  156.1 6.1 %reshape.106 = bf16[512,1,1024]{2,1,0:T(2,128)(2,1)} reshape(bf16[8,2,32768]{2,1,0:T(2,128)(2,1)} %all-to-all-done.2) | data formatting | bytes 2097152
  162.3 7.8 %bitcast_reduce_fusion = bf16[512,1024]{1,0:T(8,128)(2,1)S(1)} fusion(bf16[512,1,1024]{2,1,0:T(2,128)(2,1)} %reshape.106), kind=kLoop, calls=%fused_computation.83 | loop fusion | bytes 2097152 | tf_op jit(solution)/shard_map/all_to_all | solution.py:104
  171.6 2.7 multiply_reduce_fusion
  174.3 1.1 copy.154
  175.5 2.3 reshape.92
  177.8 4.3 all-to-all-start.1
  182.1 5.1 %fusion = f32[8,512]{1,0:T(8,128)S(1)} fusion(f32[8,512,512]{1,2,0:T(8,128)} %get-tuple-element.22, f32[8,512]{1,0:T(8,128)S(1)} %get-tuple-element.21, pred[512,512]{0,1:T(8,128)(4,1)} %copy-done.15), kind=kLoop, calls=%fused_computation.5 | loop fusion | flops 8384512 | bytes 8683520 | tf_op jit(solution)/shard_map/reduce_sum | solution.py:26
  187.2 2.5 copy.145
  189.7 1.5 copy.207
  191.2 1.0 copy-done.2
  192.1 1.5 bitcast_convert_fusion.1
  193.7 2.9 copy.190
  196.6 8.6 %multiply_reduce_fusion.1 = (f32[8,512]{1,0:T(8,128)}, bf16[8,512,128]{1,2,0:T(8,128)(2,1)}) fusion(f32[8,512,128]{1,2,0:T(8,128)} %copy.190, bf16[512,8,128]{0,2,1:T(8,128)(2,1)} %bitcast.154, f32[8,512,512]{1,2,0:T(8,128)} %get-tuple-element.22, f32[8,512]{1,0:T(8,128)S(1)} %fusion, f32[8,512]{1,0:T(8,128)S(1)} %get-tuple-element.21, ...), kind=kOutput, calls=%fused_computation.27 | convolution fusion | flops 549449728 | bytes 12894208 | tf_op jit(solution)/shard_map/hij,jhd->ihd/dot_general | solution.py:34
  205.1 2.3 copy.155
  207.4 1.2 all-to-all-done.1
  208.6 9.7 %fusion.10 = f32[2048,2048]{1,0:T(8,128)} fusion(bf16[1,1,512,2048]{3,2,1,0:T(8,128)(2,1)S(1)} %copy-done, bf16[512,1024]{1,0:T(8,128)(2,1)} %bitcast.19, bf16[512,1024]{1,0:T(8,128)(2,1)} %copy.155), kind=kOutput, calls=%fused_computation.23 | convolution fusion | flops 4299161600 | bytes 20971520 | tf_op jit(solution)/shard_map/dot_general | solution.py:135
  219.7 2.6 fusion.22
  222.3 2.8 copy.163
  225.3 1.7 copy.168
  227.0 2.2 fusion.19
  229.3 1.1 copy.169
  230.4 2.5 stack_reshape.10
  232.9 1.0 fusion.18
  234.0 1.3 stack_reshape.9
  235.3 1.7 copy.171
  238.1 1.3 stack_reshape.11
  239.3 2.2 pad_maximum_fusion
  241.6 2.1 copy.173
  243.8 4.6 all-to-all-start.3
  249.1 1.0 copy-done.21
  250.1 5.4 %multiply_convert_fusion = bf16[8,512,512]{1,2,0:T(8,128)(2,1)S(1)} fusion(f32[8,512,512]{1,2,0:T(8,128)} %get-tuple-element.22, f32[8,512]{1,0:T(8,128)S(1)} %copy-done.29, f32[8,512]{1,0:T(8,128)S(1)} %log_add_fusion.1, pred[512,512]{0,1:T(8,128)(4,1)S(1)} %copy-done.16, bf16[512,8,128]{0,2,1:T(8,128)(2,1)S(1)} %copy.177, bf16[512,8,128]{0,2,1:T(8,128)(2,1)S(1)} %bitcast.155), kind=kOutput, calls=%fused_computation | convolution fusion | flops 549453824 | bytes 14974976 | tf_op jit(solution)/shard_map/ihd,jhd->hij/dot_general | solution.py:44
  256.2 1.3 copy-done.11
  258.1 3.7 multiply_convert_fusion.1
  262.4 6.7 %fusion.14 = bf16[8,128,512]{2,1,0:T(8,128)(2,1)} fusion(bf16[512,8,128]{0,2,1:T(8,128)(2,1)} %copy-done.21, f32[8,512,512]{1,2,0:T(8,128)} %get-tuple-element.22, f32[8,512]{1,0:T(8,128)S(1)} %log_add_fusion.1, pred[512,512]{0,1:T(8,128)(4,1)S(1)} %copy-done.16), kind=kOutput, calls=%fused_computation.35 | convolution fusion | flops 545783808 | bytes 10764288 | tf_op jit(solution)/shard_map/hij,ihd->jhd/dot_general | solution.py:41
  269.1 2.3 copy.179
  271.4 9.6 %fusion.9 = bf16[1,1,512,2048]{3,2,1,0:T(8,128)(2,1)} fusion(bf16[2048,2048]{1,0:T(8,128)(2,1)} %all-gather.2.cloned.1.call-done, bf16[512,1024]{1,0:T(8,128)(2,1)} %bitcast.19, bf16[512,1024]{1,0:T(8,128)(2,1)S(1)} %copy-done.19), kind=kOutput, calls=%fused_computation.18 | convolution fusion | flops 4300210176 | bytes 12582912 | tf_op jit(solution)/shard_map/dot_general | solution.py:130
  280.9 82.1 %all-to-all-done.3 = bf16[3,8,64,1024]{3,2,0,1:T(8,128)(2,1)} async-done(((bf16[3,8,64,1024]{3,2,0,1:T(8,128)(2,1)}), bf16[3,8,64,1024]{3,2,0,1:T(8,128)(2,1)}, u32[]{:S(2)}, u32[]{:S(2)}) %all-to-all-start.3) | async-done | bytes 3145760 | tf_op jit(solution)/shard_map/all_to_all | solution.py:110
  363.0 2.2 fusion.39
  365.2 1.5 maximum_bitcast_fusion.1
  366.8 1.5 maximum_bitcast_fusion.2
  368.3 1.5 maximum_bitcast_fusion.3
  369.8 96.5 %reduce-scatter.2.cloned.1.call-done = f32[64,2048]{1,0:T(8,128)} async-done(((f32[2048,2048]{1,0:T(8,128)}), f32[64,2048]{1,0:T(8,128)}) %reduce-scatter.2.cloned.1.call-update) | async-done | bytes 524304 | tf_op jit(solution)/shard_map/reduce_scatter | solution.py:138
  466.3 1.9 broadcast_multiply_fusion
  (88 shorter events, 9.8 us)
Async XLA Ops:
  7.2 93.0 %copy-start = (bf16[1,1,512,2048]{3,2,1,0:T(8,128)(2,1)S(1)}, bf16[1,1,512,2048]{3,2,1,0:T(8,128)(2,1)}, u32[]{:S(2)}) copy-start(bf16[1,1,512,2048]{3,2,1,0:T(8,128)(2,1)} %param.10) | copy-start | bytes 6291460
  7.2 93.0 %all-gather.2.cloned.1.call-start = ((), (), s32[]{:S(2)}) async-start(), calls=%async_computation.5 | async-start | bytes 10485760 | tf_op jit(solution)/shard_map/all_gather | solution.py:82
  7.9 3.0 copy-start.17
  7.9 3.0 copy-start.18
  17.9 6.7 %copy-start.28 = (s32[4,4]{1,0:T(4,128)S(1)}, s32[4,4]{1,0:T(4,128)}, u32[]{:S(2)}) copy-start(s32[4,4]{1,0:T(4,128)} %param.12) | copy-start | bytes 196
  17.9 106.7 %all-to-all-start = ((bf16[1,3,512,1024]{3,1,0,2:T(4,128)(2,1)}), bf16[1,3,512,1024]{3,1,0,2:T(4,128)(2,1)}, u32[]{:S(2)}, u32[]{:S(2)}) async-start(bf16[1,3,512,1024]{3,1,0,2:T(4,128)(2,1)} %copy.147), calls=%async_computation | async-start | bytes 8388608 | tf_op jit(solution)/shard_map/all_to_all | solution.py:85
  24.9 104.7 %copy-start.15 = (pred[512,512]{0,1:T(8,128)(4,1)}, pred[512,512]{0,1:T(8,128)(4,1)S(1)}, u32[]{:S(2)}) copy-start(pred[512,512]{0,1:T(8,128)(4,1)S(1)} %fusion.20) | copy-start | bytes 786436
  26.5 103.1 %copy-start.9 = (bf16[1,1,512,1024]{2,3,1,0:T(8,128)(2,1)}, bf16[1,1,512,1024]{2,3,1,0:T(8,128)(2,1)S(1)}, u32[]{:S(2)}) copy-start(bf16[1,1,512,1024]{2,3,1,0:T(8,128)(2,1)S(1)} %copy.202) | copy-start | bytes 3145732
  113.0 16.5 %copy-start.27 = (s32[8,8]{1,0:T(8,128)S(1)}, s32[8,8]{1,0:T(8,128)}, u32[]{:S(2)}) copy-start(s32[8,8]{1,0:T(8,128)} %param.13) | copy-start | bytes 772
  124.6 31.5 %all-to-all-start.2 = ((bf16[8,2,32768]{2,1,0:T(2,128)(2,1)}), bf16[8,2,32768]{2,1,0:T(2,128)(2,1)}, u32[]{:S(2)}, u32[]{:S(2)}) async-start(bf16[8,2,32768]{2,1,0:T(2,128)(2,1)} %reshape.105), calls=%async_computation.2 | async-start | bytes 2097152 | tf_op jit(solution)/shard_map/all_to_all | solution.py:104
  129.5 18.4 %copy-start.25 = (pred[8,8]{1,0:T(8,128)(4,1)}, pred[8,8]{1,0:T(8,128)(4,1)S(1)}, u32[]{:S(2)}) copy-start(pred[8,8]{1,0:T(8,128)(4,1)S(1)} %broadcast_compare_fusion) | copy-start | bytes 196
  140.9 4.0 copy-start.4
  141.2 1.1 copy-start.6
  170.0 1.2 copy-start.7
  170.0 1.5 copy-start.13
  177.8 30.9 %all-to-all-start.1 = ((bf16[8,64,1024]{2,1,0:T(8,128)(2,1)}), bf16[8,64,1024]{2,1,0:T(8,128)(2,1)}, u32[]{:S(2)}, u32[]{:S(2)}) async-start(bf16[8,64,1024]{2,1,0:T(8,128)(2,1)} %reshape.92), calls=%async_computation.1 | async-start | bytes 2097152 | tf_op jit(solution)/shard_map/all_to_all | solution.py:91
  182.0 284.3 %reduce-scatter.2.cloned.1.call-start = ((), (), s32[]{:S(2)}) async-start(), calls=%async_computation.6 | async-start | bytes 17301504 | tf_op jit(solution)/shard_map/reduce_scatter | solution.py:138
  187.2 9.4 %copy-start.23 = (f32[8,512]{1,0:T(8,128)}, f32[8,512]{1,0:T(8,128)S(1)}, u32[]{:S(2)}) copy-start(f32[8,512]{1,0:T(8,128)S(1)} %fusion) | copy-start | bytes 49156
  191.1 1.0 copy-start.2
  218.3 0.9 copy-start.22
  218.3 1.3 copy-start.8
  219.7 5.5 %copy-start.26 = (pred[8,8]{1,0:T(8,128)(4,1)S(1)}, pred[8,8]{1,0:T(8,128)(4,1)}, u32[]{:S(2)}) copy-start(pred[8,8]{1,0:T(8,128)(4,1)} %copy-done.25) | copy-start | bytes 196
  227.0 5.9 %copy-start.5 = (bf16[64,8,8,128]{3,2,1,0:T(8,128)(2,1)S(1)}, bf16[64,8,8,128]{3,2,1,0:T(8,128)(2,1)}, u32[]{:S(2)}) copy-start(bf16[64,8,8,128]{3,2,1,0:T(8,128)(2,1)} %copy-done.4) | copy-start | bytes 3145732
  243.7 4.6 copy-start.24
  243.7 4.6 copy-start.3
  243.7 6.3 %copy-start.16 = (pred[512,512]{0,1:T(8,128)(4,1)S(1)}, pred[512,512]{0,1:T(8,128)(4,1)}, u32[]{:S(2)}) copy-start(pred[512,512]{0,1:T(8,128)(4,1)} %copy-done.15) | copy-start | bytes 786436
  243.8 6.3 %copy-start.20 = (bf16[1,1,512,1024]{2,3,1,0:T(8,128)(2,1)S(1)}, bf16[1,1,512,1024]{2,3,1,0:T(8,128)(2,1)}, u32[]{:S(2)}) copy-start(bf16[1,1,512,1024]{2,3,1,0:T(8,128)(2,1)} %copy.145) | copy-start | bytes 3145732
  243.8 6.3 %copy-start.29 = (f32[8,512]{1,0:T(8,128)S(1)}, f32[8,512]{1,0:T(8,128)}, u32[]{:S(2)}) copy-start(f32[8,512]{1,0:T(8,128)} %get-tuple-element.25) | copy-start | bytes 49156
  243.8 119.2 %all-to-all-start.3 = ((bf16[3,8,64,1024]{3,2,0,1:T(8,128)(2,1)}), bf16[3,8,64,1024]{3,2,0,1:T(8,128)(2,1)}, u32[]{:S(2)}, u32[]{:S(2)}) async-start(bf16[3,8,64,1024]{3,2,0,1:T(8,128)(2,1)} %copy.173), calls=%async_computation.3 | async-start | bytes 6291456 | tf_op jit(solution)/shard_map/all_to_all | solution.py:110
  249.1 1.0 copy-start.21
  250.1 5.4 %copy-start.10 = (bf16[1,1,512,1024]{2,3,1,0:T(8,128)(2,1)S(1)}, bf16[1,1,512,1024]{2,3,1,0:T(8,128)(2,1)}, u32[]{:S(2)}) copy-start(bf16[1,1,512,1024]{2,3,1,0:T(8,128)(2,1)} %copy-done.9) | copy-start | bytes 3145732
  255.5 2.1 copy-start.11
  255.5 2.6 copy-start.14
  262.4 9.0 %copy-start.19 = (bf16[512,1024]{1,0:T(8,128)(2,1)S(1)}, bf16[512,1024]{1,0:T(8,128)(2,1)}, u32[]{:S(2)}) copy-start(bf16[512,1024]{1,0:T(8,128)(2,1)} %copy.155) | copy-start | bytes 3145732
  366.8 1.5 copy-start.12
  366.8 101.4 %copy-start.1 = (bf16[1,1,512,2048]{3,2,1,0:T(8,128)(2,1)S(1)}, bf16[1,1,512,2048]{3,2,1,0:T(8,128)(2,1)}, u32[]{:S(2)}) copy-start(bf16[1,1,512,2048]{3,2,1,0:T(8,128)(2,1)} %param.10) | copy-start | bytes 6291460
Sparse Core Ops, SparseCore 0:
  9.9 90.2 all-gather.1
  218.5 247.7 reduce-scatter.1

commit v2 on v1

--- a/solution.py
+++ b/solution.py
@@ -78,8 +78,17 @@
     heads_half = half // DH
     rows = lax.axis_size("seq")
     cols_each = tokens // rows
+    core = lax.axis_index("seq") % 2
+    pairs = [(2 * m + j, 2 * m + 1 - j) for m in range(rows // 2) for j in range(2)]
 
-    weight = lax.all_gather(out_weight, "dp", axis=0, tiled=True)
+    local_rows = out_weight.shape[0]
+    mine = lax.dynamic_slice_in_dim(out_weight, core * (local_rows // 2), local_rows // 2)
+    gathered = lax.all_gather(mine, "dp", axis=0, tiled=False)
+    theirs = lax.ppermute(gathered, "seq", pairs)
+    weight = jnp.where(
+        core == 0, jnp.stack([gathered, theirs], axis=1), jnp.stack([theirs, gathered], axis=1)
+    ).reshape(features, features)
+    grad_mate = lax.ppermute(out_grad[0, 0], "seq", pairs)
 
     packed = jnp.stack([t[0, 0, :, half:] for t in (queries, keys, values)])
     shipped = lax.all_to_all(packed[None], "seq", split_axis=2, concat_axis=0, tiled=True)
@@ -131,13 +140,25 @@
         jnp.bfloat16
     )
 
-    devices_all = lax.axis_size(("dp", "seq"))
+    block = local_rows // rows
+    by_parity = attention.reshape(tokens, features // (2 * block), 2, block)
+    own_rows = jnp.where(core == 0, by_parity[:, :, 0], by_parity[:, :, 1])
+    mate_rows = lax.ppermute(
+        jnp.where(core == 0, by_parity[:, :, 1], by_parity[:, :, 0]), "seq", pairs
+    )
+    pair_attn = jnp.concatenate([own_rows, mate_rows], axis=0).reshape(2 * tokens, features // 2)
+    pair_grad = jnp.concatenate([flat_grad, grad_mate], axis=0)
     partial = lax.dot_general(
-        attention, flat_grad, (((0,), (0,)), ((), ())), preferred_element_type=jnp.float32
+        pair_attn, pair_grad, (((0,), (0,)), ((), ())), preferred_element_type=jnp.float32
     )
-    wo_grad = lax.psum_scatter(partial, ("dp", "seq"), scatter_dimension=0, tiled=True) * (
-        1.0 / math.sqrt(tokens * devices_all)
-    )
+    dp_size = lax.axis_size("dp")
+    devices_all = dp_size * rows
+    groups = [
+        [d * rows + 2 * m + c for d in range(dp_size) for m in range(rows // 2)] for c in range(2)
+    ]
+    wo_grad = lax.psum_scatter(
+        partial, ("dp", "seq"), scatter_dimension=0, tiled=True, axis_index_groups=groups
+    ) * (1.0 / math.sqrt(tokens * devices_all))
 
     grads = [
         jnp.concatenate([row_grads[i].reshape(tokens, half), col_grads_back[i, 0]], axis=1)[

time: 482 us -> 527 us (1.093)
  waiting for transfers between devices: 257 us -> 308 us
  other arithmetic: 25.5 us -> 35.3 us
  matrix products: 70.7 us -> 64 us
  local copies, waits for them, and re-layouts: 86.6 us -> 81 us
    all_to_all x1, waiting for transfers between devices: 0.01 us -> 61.1 us  [on_device(): lax.all_to_all(packed[None], 'seq', split_axis=2, concat_axis=0, tiled=True)]
    reduce_scatter x1, waiting for transfers between devices: 96.5 us -> 53.5 us  [on_device(): lax.psum_scatter(partial, ('dp', 'seq'), scatter_dimension=0, tiled=True,...]
    all_to_all x1, waiting for transfers between devices: 82.1 us -> 115 us  [on_device(): lax.all_to_all(jnp.stack([g.reshape(rows, cols_each, half) for g in col_g...]
    all_gather x1, waiting for transfers between devices: 71.1 us -> 56 us  [on_device(): gathered = lax.all_gather(mine, 'dp', axis=0, tiled=False)]
    all_to_all x1, waiting for transfers between devices: 1.21 us -> 15.2 us  [on_device(): lax.all_to_all(col_out.reshape(rows, cols_each, half), 'seq', split_axis=...]
    unnamed x74 -> x77, local copies, waits for them, and re-layouts: 27.9 us -> 16.7 us
    select_n x0 -> x3, other arithmetic: none -> 8.71 us  [the longest x1 8.38 us: on_device(): jnp.where(core == 0, jnp.stack([gathered, theirs], axis=1), jnp.stack([th...]
    concatenate x0 -> x2, local copies, waits for them, and re-layouts: none -> 7.3 us  [on_device(): jnp.concatenate([row_out.reshape(tokens, half), col_back[0]], axis=1)]
  transfers between devices with their start and end apart: 6 -> 9, of which waited for: 5 -> 7; matrix products, arithmetic and copies ran while one was open for 30% -> 31% of each run, Pallas kernels for 0% -> 0%
where the time goes in v2:
time: 527 us; the launch traced here: 522 us
  waiting for transfers between devices  308 us (58%)
  local copies, waits for them, and re-layouts  81 us (15%)
  matrix products  64 us (12%)
  other arithmetic  35.3 us (7%)
  starting transfers between devices  18.1 us (3%)
  between operations  14.9 us (3%)
    all_to_all x1, waiting for transfers between devices, on_device(): lax.all_to_all(jnp.stack([g.reshape(rows, cols_each, half) for g in col_g...  115 us
    all_to_all x1, waiting for transfers between devices, on_device(): lax.all_to_all(packed[None], 'seq', split_axis=2, concat_axis=0, tiled=True)  61.1 us
    all_gather x1, waiting for transfers between devices, on_device(): gathered = lax.all_gather(mine, 'dp', axis=0, tiled=False)  56 us
    reduce_scatter x1, waiting for transfers between devices, on_device(): lax.psum_scatter(partial, ('dp', 'seq'), scatter_dimension=0, tiled=True,...  53.5 us
    unnamed x77, local copies, waits for them, and re-layouts  16.7 us
    all_to_all x1, waiting for transfers between devices, on_device(): lax.all_to_all(col_out.reshape(rows, cols_each, half), 'seq', split_axis=...  15.2 us
  transfers between devices with their start and end apart: 9, of which 7 were waited for; matrix products, arithmetic and copies ran while one was open for 31% of the time, Pallas kernels for 0%

profile of v2, /device:TPU:0, one launch (start us, length us, event | category | flops | bytes accessed | tf_op | source)
XLA Modules:
  0.0 521.6 jit_solution(14986426976849858004)
XLA Ops:
  7.2 1.5 copy-done
  9.9 56.0 %all-gather.3.cloned.1.call-done = bf16[1024,2048]{1,0:T(8,128)(2,1)} async-done(((bf16[256,2048]{1,0:T(8,128)(2,1)}), bf16[1024,2048]{1,0:T(8,128)(2,1)}) %all-gather.3.cloned.1.call-update) | async-done | bytes 4194320 | tf_op jit(solution)/shard_map/all_gather | solution.py:86
  65.9 1.9 fusion.53
  68.7 1.6 fusion.51
  70.6 4.7 copy.165
  75.3 5.1 all-to-all-start
  81.0 1.3 copy.163
  82.6 1.3 copy.226
  84.5 8.4 %maximum_select_fusion = bf16[4,2,256,2048]{3,2,1,0:T(8,128)(2,1)S(1)} fusion(bf16[4,1,256,2048]{3,2,1,0:T(8,128)(2,1)} %bitcast.22, bf16[4,1,256,2048]{3,2,1,0:T(8,128)(2,1)} %bitcast.168, pred[]{:T(512)S(6)} %eq.37), kind=kLoop, calls=%fused_computation | loop fusion | flops 12582912 | bytes 16777216 | tf_op jit(solution)/shard_map/jit(_where)/select_n | solution.py:88
  92.9 5.0 fusion.14
  98.0 1.3 copy-done.20
  99.4 3.8 copy.178
  103.7 8.0 %reduce.6 = bf16[512,1024]{1,0:T(8,128)(2,1)S(1)} reduce(bf16[512,1,1024]{2,1,0:T(2,128)(2,1)} %bitcast.166, bf16[]{:T(256)} %broadcast.51), dimensions={1}, to_apply=%bitcast.126.reduce_sub_computation | reduce | bytes 2097154
  111.7 1.6 reshape.136
  113.3 61.1 %all-to-all-done = bf16[1,3,512,1024]{3,1,0,2:T(4,128)(2,1)} async-done(((bf16[1,3,512,1024]{3,1,0,2:T(4,128)(2,1)}), bf16[1,3,512,1024]{3,1,0,2:T(4,128)(2,1)}, u32[]{:S(2)}, u32[]{:S(2)}) %all-to-all-start) | async-done | bytes 3145760 | tf_op jit(solution)/shard_map/all_to_all | solution.py:94
  174.5 4.1 all-to-all-start.2
  178.6 6.1 %select_reduce_fusion = (f32[8,512]{1,0:T(8,128)S(1)}, f32[8,512,512]{1,2,0:T(8,128)}) fusion(pred[512,512]{0,1:T(8,128)(4,1)S(1)} %fusion.29, bf16[512,8,128]{0,2,1:T(8,128)(2,1)} %bitcast.179, bf16[512,8,128]{0,2,1:T(8,128)(2,1)S(1)} %bitcast.162), kind=kOutput, calls=%fused_computation.5 | convolution fusion | flops 543158272 | bytes 10764288 | tf_op jit(solution)/shard_map/ihd,jhd->hij/dot_general | solution.py:32
  184.7 3.4 copy.255
  188.1 1.3 fusion.50
  190.0 2.6 fusion.36
  192.6 2.7 copy.169
  195.7 2.5 copy.171
  198.2 1.5 copy.230
  199.7 5.4 %all-to-all-done.2 = bf16[8,2,32768]{2,1,0:T(2,128)(2,1)S(1)} async-done(((bf16[8,2,32768]{2,1,0:T(2,128)(2,1)}), bf16[8,2,32768]{2,1,0:T(2,128)(2,1)S(1)}, u32[]{:S(2)}, u32[]{:S(2)}) %all-to-all-start.2) | async-done | bytes 1048608 | tf_op jit(solution)/shard_map/all_to_all | solution.py:113
  205.1 3.6 reshape.137
  208.7 7.8 %bitcast_reduce_fusion = bf16[512,1024]{1,0:T(8,128)(2,1)S(1)} fusion(bf16[512,1,1024]{2,1,0:T(2,128)(2,1)} %reshape.137), kind=kLoop, calls=%fused_computation.98 | loop fusion | bytes 2097152 | tf_op jit(solution)/shard_map/all_to_all | solution.py:113
  216.9 2.8 multiply_reduce_fusion
  219.9 1.3 reshape.119
  221.1 3.6 all-to-all-start.1
  224.8 5.2 fusion
  230.0 6.0 %fusion.19 = bf16[8,512,128]{1,2,0:T(8,128)(2,1)S(1)} fusion(bf16[512,8,128]{0,2,1:T(8,128)(2,1)S(1)} %bitcast.184, f32[8,512,512]{1,2,0:T(8,128)} %get-tuple-element.22, f32[8,512]{1,0:T(8,128)S(1)} %fusion, f32[8,512]{1,0:T(8,128)S(1)} %get-tuple-element.21, pred[512,512]{0,1:T(8,128)(4,1)S(1)} %copy-done.18), kind=kOutput, calls=%fused_computation.44 | convolution fusion | flops 547880960 | bytes 10780672 | tf_op jit(solution)/shard_map/hij,jhd->ihd/dot_general | solution.py:34
  236.0 15.2 %all-to-all-done.1 = bf16[8,64,1024]{2,1,0:T(8,128)(2,1)S(1)} async-done(((bf16[8,64,1024]{2,1,0:T(8,128)(2,1)}), bf16[8,64,1024]{2,1,0:T(8,128)(2,1)S(1)}, u32[]{:S(2)}, u32[]{:S(2)}) %all-to-all-start.1) | async-done | bytes 1048608 | tf_op jit(solution)/shard_map/all_to_all | solution.py:100
  252.2 2.7 reshape.134
  254.9 4.6 copy.225
  259.9 2.5 collective-permute-done.1
  262.7 8.4 %fusion.4 = f32[1024,2048]{1,0:T(8,128)} fusion(bf16[1024,1024]{0,1:T(8,128)(2,1)S(1)} %bitcast.181, bf16[512,2048]{1,0:T(8,128)(2,1)} %collective-permute-done.2, bf16[512,2048]{1,0:T(8,128)(2,1)S(1)} %bitcast.190), kind=kOutput, calls=%fused_computation.9 | convolution fusion | flops 4303355904 | bytes 14680064 | tf_op jit(solution)/shard_map/dot_general | solution.py:151
  272.3 2.6 fusion.31
  274.9 2.7 copy.181
  278.7 1.6 multiply_convert_fusion.5
  280.2 2.7 copy.189
  283.9 1.3 stack_reshape.11
  285.2 1.7 copy.186
  287.0 2.2 fusion.25
  289.1 1.1 copy.187
  290.3 2.4 stack_reshape.10
  293.8 1.3 stack_reshape.9
  295.1 1.9 pad_maximum_fusion
  297.0 2.1 copy.191
  299.1 4.6 all-to-all-start.3
  303.7 1.3 copy.173
  305.1 1.6 fusion.18
  306.7 5.6 %multiply_convert_fusion = bf16[8,512,512]{1,2,0:T(8,128)(2,1)S(1)} fusion(f32[8,512,512]{1,2,0:T(8,128)} %get-tuple-element.22, f32[8,512]{1,0:T(8,128)S(1)} %get-tuple-element.5, f32[8,512]{1,0:T(8,128)S(1)} %log_add_fusion.1, pred[512,512]{0,1:T(8,128)(4,1)S(1)} %copy-done.19, bf16[512,8,128]{0,2,1:T(8,128)(2,1)S(1)} %bitcast.182, ...), kind=kOutput, calls=%fused_computation.1 | convolution fusion | flops 549453824 | bytes 14974976 | tf_op jit(solution)/shard_map/ihd,jhd->hij/dot_general | solution.py:44
  313.1 1.2 copy-done.12
  314.8 4.0 multiply_convert_fusion.1
  319.4 6.7 %fusion.20 = bf16[8,128,512]{2,1,0:T(8,128)(2,1)} fusion(bf16[512,8,128]{0,2,1:T(8,128)(2,1)} %bitcast.183, f32[8,512,512]{1,2,0:T(8,128)} %get-tuple-element.22, f32[8,512]{1,0:T(8,128)S(1)} %log_add_fusion.1, pred[512,512]{0,1:T(8,128)(4,1)S(1)} %copy-done.19), kind=kOutput, calls=%fused_computation.45 | convolution fusion | flops 545783808 | bytes 10764288 | tf_op jit(solution)/shard_map/hij,ihd->jhd/dot_general | solution.py:41
  326.1 2.3 copy.196
  328.3 9.6 %fusion.13 = bf16[1,1,512,2048]{3,2,1,0:T(8,128)(2,1)} fusion(bf16[2048,2048]{1,0:T(8,128)(2,1)} %bitcast.165, bf16[512,1024]{1,0:T(8,128)(2,1)S(1)} %bitcast.169, bf16[512,1024]{1,0:T(8,128)(2,1)} %copy.173), kind=kOutput, calls=%fused_computation.23 | convolution fusion | flops 4300210176 | bytes 12582912 | tf_op jit(solution)/shard_map/dot_general | solution.py:139
  337.9 114.5 %all-to-all-done.3 = bf16[3,8,64,1024]{3,2,0,1:T(8,128)(2,1)} async-done(((bf16[3,8,64,1024]{3,2,0,1:T(8,128)(2,1)}), bf16[3,8,64,1024]{3,2,0,1:T(8,128)(2,1)}, u32[]{:S(2)}, u32[]{:S(2)}) %all-to-all-start.3) | async-done | bytes 3145760 | tf_op jit(solution)/shard_map/all_to_all | solution.py:119
  452.4 2.2 fusion.49
  454.6 1.5 maximum_bitcast_fusion.1
  456.2 1.5 maximum_bitcast_fusion.2
  457.7 1.5 maximum_bitcast_fusion.3
  459.2 53.5 %reduce-scatter.2.cloned.1.call-done = f32[64,2048]{1,0:T(8,128)} async-done(((f32[1024,2048]{1,0:T(8,128)}), f32[64,2048]{1,0:T(8,128)}) %reduce-scatter.2.cloned.1.call-update) | async-done | bytes 524304 | tf_op jit(solution)/shard_map/reduce_scatter | solution.py:159
  512.7 1.9 broadcast_multiply_fusion
  (104 shorter events, 13.9 us)
Async XLA Ops:
  7.2 1.6 copy-start
  7.2 58.7 %all-gather.3.cloned.1.call-start = ((), (), s32[]{:S(2)}) async-start(), calls=%async_computation.6 | async-start | bytes 5242880 | tf_op jit(solution)/shard_map/all_gather | solution.py:86
  65.9 2.2 copy-start.21
  65.9 2.9 copy-start.22
  65.9 18.6 %collective-permute-start = (bf16[4,256,2048]{2,1,0:T(8,128)(2,1)}, bf16[4,256,2048]{2,1,0:T(8,128)(2,1)}, u32[]{:S(2)}, u32[]{:S(2)}) collective-permute-start(bf16[4,256,2048]{2,1,0:T(8,128)(2,1)} %bitcast.167), channel_id=1, source_target_pairs={{0,1},{1,0},{2,3},{3,2},{4,5},{5,4},{6,7},{7,6},{8,9},{9,8},{10,11... | collective-permute-start | bytes 12582920 | tf_op jit(solution)/shard_map/ppermute | solution.py:87
  75.3 7.0 %copy-start.30 = (s32[4,4]{1,0:T(4,128)S(1)}, s32[4,4]{1,0:T(4,128)}, u32[]{:S(2)}) copy-start(s32[4,4]{1,0:T(4,128)} %param.12) | copy-start | bytes 196
  75.3 7.3 %copy-start.16 = (bf16[1,1,512,1024]{3,2,1,0:T(8,128)(2,1)S(1)}, bf16[1,1,512,1024]{3,2,1,0:T(8,128)(2,1)}, u32[]{:S(2)}) copy-start(bf16[1,1,512,1024]{3,2,1,0:T(8,128)(2,1)} %get-tuple-element.26) | copy-start | bytes 3145732
  75.3 99.1 %all-to-all-start = ((bf16[1,3,512,1024]{3,1,0,2:T(4,128)(2,1)}), bf16[1,3,512,1024]{3,1,0,2:T(4,128)(2,1)}, u32[]{:S(2)}, u32[]{:S(2)}) async-start(bf16[1,3,512,1024]{3,1,0,2:T(4,128)(2,1)} %copy.165), calls=%async_computation | async-start | bytes 8388608 | tf_op jit(solution)/shard_map/all_to_all | solution.py:94
  80.4 182.3 %collective-permute-start.2 = (bf16[512,2048]{1,0:T(8,128)(2,1)}, bf16[512,2048]{1,0:T(8,128)(2,1)}, u32[]{:S(2)}, u32[]{:S(2)}) collective-permute-start(bf16[512,2048]{1,0:T(8,128)(2,1)} %bitcast.189), channel_id=1, source_target_pairs={{0,1},{1,0},{2,3},{3,2},{4,5},{5,4},{6,7},{7,6},{8,9},{9,8},{10,11... | collective-permute-start | bytes 6291464 | tf_op jit(solution)/shard_map/ppermute | solution.py:91
  82.6 96.0 %copy-start.17 = (pred[512,512]{0,1:T(8,128)(4,1)}, pred[512,512]{0,1:T(8,128)(4,1)S(1)}, u32[]{:S(2)}) copy-start(pred[512,512]{0,1:T(8,128)(4,1)S(1)} %fusion.29) | copy-start | bytes 786436
  84.5 94.1 %copy-start.7 = (bf16[1,1,512,1024]{2,3,1,0:T(8,128)(2,1)}, bf16[1,1,512,1024]{2,3,1,0:T(8,128)(2,1)S(1)}, u32[]{:S(2)}) copy-start(bf16[1,1,512,1024]{2,3,1,0:T(8,128)(2,1)S(1)} %copy.227) | copy-start | bytes 3145732
  84.5 8.4 %copy-start.31 = (bf16[1,1,512,2048]{3,2,1,0:T(8,128)(2,1)S(1)}, bf16[1,1,512,2048]{3,2,1,0:T(8,128)(2,1)}, u32[]{:S(2)}) copy-start(bf16[1,1,512,2048]{3,2,1,0:T(8,128)(2,1)} %param.10) | copy-start | bytes 6291460
  92.9 5.1 copy-start.9
  98.0 1.3 copy-start.20
  103.2 75.4 %copy-start.29 = (s32[8,8]{1,0:T(8,128)S(1)}, s32[8,8]{1,0:T(8,128)}, u32[]{:S(2)}) copy-start(s32[8,8]{1,0:T(8,128)} %param.13) | copy-start | bytes 772
  174.5 30.6 %all-to-all-start.2 = ((bf16[8,2,32768]{2,1,0:T(2,128)(2,1)}), bf16[8,2,32768]{2,1,0:T(2,128)(2,1)S(1)}, u32[]{:S(2)}, u32[]{:S(2)}) async-start(bf16[8,2,32768]{2,1,0:T(2,128)(2,1)} %reshape.136), calls=%async_computation.2 | async-start | bytes 2097152 | tf_op jit(solution)/shard_map/all_to_all | solution.py:113
  178.6 17.0 %copy-start.28 = (pred[8,8]{1,0:T(8,128)(4,1)}, pred[8,8]{1,0:T(8,128)(4,1)S(1)}, u32[]{:S(2)}) copy-start(pred[8,8]{1,0:T(8,128)(4,1)S(1)} %broadcast_compare_fusion) | copy-start | bytes 196
  189.7 5.6 %copy-start.2 = (bf16[64,8,8,128]{3,2,1,0:T(8,128)(2,1)}, bf16[64,8,8,128]{3,2,1,0:T(8,128)(2,1)S(1)}, u32[]{:S(2)}) copy-start(bf16[64,8,8,128]{3,2,1,0:T(8,128)(2,1)S(1)} %copy.232) | copy-start | bytes 3145732
  189.9 8.2 %copy-start.4 = (bf16[64,8,8,128]{3,2,1,0:T(8,128)(2,1)}, bf16[64,8,8,128]{3,2,1,0:T(8,128)(2,1)S(1)}, u32[]{:S(2)}) copy-start(bf16[64,8,8,128]{3,2,1,0:T(8,128)(2,1)S(1)} %copy.231) | copy-start | bytes 3145732
  199.7 17.2 %copy-start.5 = (bf16[64,8,8,128]{3,2,1,0:T(8,128)(2,1)}, bf16[64,8,8,128]{3,2,1,0:T(8,128)(2,1)S(1)}, u32[]{:S(2)}) copy-start(bf16[64,8,8,128]{3,2,1,0:T(8,128)(2,1)S(1)} %copy.230) | copy-start | bytes 3145732
  208.6 8.3 %copy-start.14 = (bf16[64,8,8,8]{3,2,1,0:T(8,128)(2,1)S(1)}, bf16[64,8,8,8]{3,2,1,0:T(8,128)(2,1)}, u32[]{:S(2)}) copy-start(bf16[64,8,8,8]{3,2,1,0:T(8,128)(2,1)} %copy.171) | copy-start | bytes 196612
  221.1 30.1 %all-to-all-start.1 = ((bf16[8,64,1024]{2,1,0:T(8,128)(2,1)}), bf16[8,64,1024]{2,1,0:T(8,128)(2,1)S(1)}, u32[]{:S(2)}, u32[]{:S(2)}) async-start(bf16[8,64,1024]{2,1,0:T(8,128)(2,1)} %reshape.119), calls=%async_computation.1 | async-start | bytes 2097152 | tf_op jit(solution)/shard_map/all_to_all | solution.py:100
  224.7 288.0 %reduce-scatter.2.cloned.1.call-start = ((), (), s32[]{:S(2)}) async-start(), calls=%async_computation.5 | async-start | bytes 8912896 | tf_op jit(solution)/shard_map/reduce_scatter | solution.py:159
  224.7 5.2 %copy-start.18 = (pred[512,512]{0,1:T(8,128)(4,1)S(1)}, pred[512,512]{0,1:T(8,128)(4,1)}, u32[]{:S(2)}) copy-start(pred[512,512]{0,1:T(8,128)(4,1)} %copy-done.17) | copy-start | bytes 786436
  224.8 5.2 %copy-start.24 = (bf16[1,1,512,1024]{2,3,1,0:T(8,128)(2,1)S(1)}, bf16[1,1,512,1024]{2,3,1,0:T(8,128)(2,1)}, u32[]{:S(2)}) copy-start(bf16[1,1,512,1024]{2,3,1,0:T(8,128)(2,1)} %copy.163) | copy-start | bytes 3145732
  230.0 6.0 %copy-start.26 = (f32[8,512]{1,0:T(8,128)}, f32[8,512]{1,0:T(8,128)S(1)}, u32[]{:S(2)}) copy-start(f32[8,512]{1,0:T(8,128)S(1)} %fusion) | copy-start | bytes 49156
  251.2 1.0 copy-start.10
  259.7 3.0 copy-start.32
  259.7 2.7 collective-permute-start.1
  271.1 1.2 copy-start.6
  285.2 7.5 %copy-start.3 = (bf16[64,8,8,128]{3,2,1,0:T(8,128)(2,1)S(1)}, bf16[64,8,8,128]{3,2,1,0:T(8,128)(2,1)}, u32[]{:S(2)}) copy-start(bf16[64,8,8,128]{3,2,1,0:T(8,128)(2,1)} %copy-done.2) | copy-start | bytes 3145732
  293.7 1.4 copy-start.15
  299.1 6.0 %copy-start.27 = (f32[8,512]{1,0:T(8,128)S(1)}, f32[8,512]{1,0:T(8,128)}, u32[]{:S(2)}) copy-start(f32[8,512]{1,0:T(8,128)} %copy-done.26) | copy-start | bytes 49156
  299.1 153.3 %all-to-all-start.3 = ((bf16[3,8,64,1024]{3,2,0,1:T(8,128)(2,1)}), bf16[3,8,64,1024]{3,2,0,1:T(8,128)(2,1)}, u32[]{:S(2)}, u32[]{:S(2)}) async-start(bf16[3,8,64,1024]{3,2,0,1:T(8,128)(2,1)} %copy.191), calls=%async_computation.3 | async-start | bytes 6291456 | tf_op jit(solution)/shard_map/all_to_all | solution.py:119
  303.7 2.9 copy-start.19
  303.7 2.9 copy-start.25
  306.6 5.7 %copy-start.23 = (bf16[512,1024]{0,1:T(8,128)(2,1)}, bf16[512,1024]{0,1:T(8,128)(2,1)S(1)}, u32[]{:S(2)}) copy-start(bf16[512,1024]{0,1:T(8,128)(2,1)S(1)} %get-tuple-element.6) | copy-start | bytes 3145732
  306.7 5.6 %copy-start.8 = (bf16[1,1,512,1024]{2,3,1,0:T(8,128)(2,1)S(1)}, bf16[1,1,512,1024]{2,3,1,0:T(8,128)(2,1)}, u32[]{:S(2)}) copy-start(bf16[1,1,512,1024]{2,3,1,0:T(8,128)(2,1)} %copy-done.7) | copy-start | bytes 3145732
  312.3 2.0 copy-start.12
  319.4 9.0 %copy-start.11 = (bf16[8,64,1024]{2,1,0:T(8,128)(2,1)S(1)}, bf16[8,64,1024]{2,1,0:T(8,128)(2,1)}, u32[]{:S(2)}) copy-start(bf16[8,64,1024]{2,1,0:T(8,128)(2,1)} %copy-done.10) | copy-start | bytes 3145732
  454.6 3.0 copy-start.13
  456.1 58.4 %copy-start.1 = (bf16[512,2048]{1,0:T(8,128)(2,1)S(1)}, bf16[512,2048]{1,0:T(8,128)(2,1)}, u32[]{:S(2)}) copy-start(bf16[512,2048]{1,0:T(8,128)(2,1)} %param.11) | copy-start | bytes 6291460
Sparse Core Ops, SparseCore 0:
  10.4 55.3 all-gather.2
  271.2 241.4 reduce-scatter.1

commit v3 on v1

--- a/solution.py
+++ b/solution.py
@@ -98,6 +98,16 @@
     row_out, row_scores, row_total = row_forward(row_q, row_k, row_v, row_ok)
 
     flat_grad = out_grad[0, 0]
+    attention = jnp.concatenate([row_out.reshape(tokens, half), col_back[0]], axis=1)
+    partial = lax.dot_general(
+        attention, flat_grad, (((0,), (0,)), ((), ())), preferred_element_type=jnp.float32
+    )
+    partial, weight = lax.optimization_barrier((partial, weight))
+    devices_all = lax.axis_size(("dp", "seq"))
+    wo_grad = lax.psum_scatter(partial, ("dp", "seq"), scatter_dimension=0, tiled=True) * (
+        1.0 / math.sqrt(tokens * devices_all)
+    )
+
     attn_grad = lax.dot_general(
         flat_grad, weight, (((1,), (1,)), ((), ())), preferred_element_type=jnp.float32
     ).astype(jnp.bfloat16)
@@ -126,17 +136,8 @@
         row_ok,
     )
 
-    attention = jnp.concatenate([row_out.reshape(tokens, half), col_back[0]], axis=1)
     layer_out = jnp.dot(attention, weight, preferred_element_type=jnp.float32).astype(
         jnp.bfloat16
-    )
-
-    devices_all = lax.axis_size(("dp", "seq"))
-    partial = lax.dot_general(
-        attention, flat_grad, (((0,), (0,)), ((), ())), preferred_element_type=jnp.float32
-    )
-    wo_grad = lax.psum_scatter(partial, ("dp", "seq"), scatter_dimension=0, tiled=True) * (
-        1.0 / math.sqrt(tokens * devices_all)
     )
 
     grads = [

time: 482 us -> 466 us (0.967)
  local copies, waits for them, and re-layouts: 86.6 us -> 77.3 us
    all_to_all x1, waiting for transfers between devices: 0.01 us -> 82.1 us  [on_device(): lax.all_to_all(packed[None], 'seq', split_axis=2, concat_axis=0, tiled=True)]
    all_gather x1, waiting for transfers between devices: 71.1 us -> 0.01 us  [on_device(): weight = lax.all_gather(out_weight, 'dp', axis=0, tiled=True)]
    reduce_scatter x1, waiting for transfers between devices: 96.5 us -> 39.5 us  [on_device(): lax.psum_scatter(partial, ('dp', 'seq'), scatter_dimension=0, tiled=True)]
    all_to_all x1, waiting for transfers between devices: 5.66 us -> 43.4 us  [on_device(): lax.all_to_all(attn_grad[None, :, half:], 'seq', split_axis=1, concat_axi...]
    all_to_all x1, waiting for transfers between devices: 1.21 us -> 11.6 us  [on_device(): lax.all_to_all(col_out.reshape(rows, cols_each, half), 'seq', split_axis=...]
    unnamed x74 -> x71, local copies, waits for them, and re-layouts: 27.9 us -> 18.8 us
    all_to_all x1, waiting for transfers between devices: 82.1 us -> 75.9 us  [on_device(): lax.all_to_all(jnp.stack([g.reshape(rows, cols_each, half) for g in col_g...]
  transfers between devices with their start and end apart: 6 -> 6, of which waited for: 5 -> 5; matrix products, arithmetic and copies ran while one was open for 30% -> 36% of each run, Pallas kernels for 0% -> 0%
where the time goes in v3:
time: 466 us; the launch traced here: 459 us
  waiting for transfers between devices  253 us (54%)
  local copies, waits for them, and re-layouts  77.3 us (17%)
  matrix products  68.8 us (15%)
  other arithmetic  25 us (5%)
  starting transfers between devices  19.7 us (4%)
  between operations  14.8 us (3%)
    all_to_all x1, waiting for transfers between devices, on_device(): lax.all_to_all(packed[None], 'seq', split_axis=2, concat_axis=0, tiled=True)  82.1 us
    all_to_all x1, waiting for transfers between devices, on_device(): lax.all_to_all(jnp.stack([g.reshape(rows, cols_each, half) for g in col_g...  75.9 us
    all_to_all x1, waiting for transfers between devices, on_device(): lax.all_to_all(attn_grad[None, :, half:], 'seq', split_axis=1, concat_axi...  43.4 us
    reduce_scatter x1, waiting for transfers between devices, on_device(): lax.psum_scatter(partial, ('dp', 'seq'), scatter_dimension=0, tiled=True)  39.5 us
    unnamed x71, local copies, waits for them, and re-layouts  18.8 us
    all_to_all x1, waiting for transfers between devices, on_device(): lax.all_to_all(col_out.reshape(rows, cols_each, half), 'seq', split_axis=...  11.6 us
    dot_general x1, matrix products, on_device(): lax.dot_general(attention, flat_grad, (((0,), (0,)), ((), ())), preferred...  9.75 us
    dot_general x1, matrix products, on_device(): jnp.dot(attention, weight, preferred_element_type=jnp.float32)  9.53 us
  transfers between devices with their start and end apart: 6, of which 5 were waited for; matrix products, arithmetic and copies ran while one was open for 36% of the time, Pallas kernels for 0%

profile of v3, /device:TPU:0, one launch (start us, length us, event | category | flops | bytes accessed | tf_op | source)
XLA Modules:
  0.0 458.8 jit_solution(7015009196396605582)
XLA Ops:
  7.9 1.9 fusion.45
  10.8 1.9 fusion.43
  13.0 4.7 %copy.146 = bf16[1,3,512,1024]{3,1,0,2:T(4,128)(2,1)} copy(bf16[1,3,512,1024]{3,2,1,0:T(8,128)(2,1)S(1)} %maximum_bitcast_fusion) | data formatting | bytes 6291456 | tf_op jit(solution)/shard_map/broadcast_in_dim | solution.py:85
  17.7 6.7 %all-to-all-start = ((bf16[1,3,512,1024]{3,1,0,2:T(4,128)(2,1)}), bf16[1,3,512,1024]{3,1,0,2:T(4,128)(2,1)}, u32[]{:S(2)}, u32[]{:S(2)}) async-start(bf16[1,3,512,1024]{3,1,0,2:T(4,128)(2,1)} %copy.146), calls=%async_computation | async-start | bytes 8388608 | tf_op jit(solution)/shard_map/all_to_all | solution.py:85
  24.7 1.3 copy.144
  26.1 1.5 copy.202
  27.6 2.7 copy.201
  30.3 6.1 %select_reduce_fusion = (f32[8,512]{1,0:T(8,128)S(1)}, f32[8,512,512]{1,2,0:T(8,128)}) fusion(pred[512,512]{0,1:T(8,128)(4,1)S(1)} %fusion.22, bf16[512,8,128]{0,2,1:T(8,128)(2,1)} %bitcast.150, bf16[512,8,128]{0,2,1:T(8,128)(2,1)S(1)} %bitcast.138), kind=kOutput, calls=%fused_computation.4 | convolution fusion | flops 543158272 | bytes 10764288 | tf_op jit(solution)/shard_map/ihd,jhd->hij/dot_general | solution.py:32
  36.4 82.1 %all-to-all-done = bf16[1,3,512,1024]{3,1,0,2:T(4,128)(2,1)} async-done(((bf16[1,3,512,1024]{3,1,0,2:T(4,128)(2,1)}), bf16[1,3,512,1024]{3,1,0,2:T(4,128)(2,1)}, u32[]{:S(2)}, u32[]{:S(2)}) %all-to-all-start) | async-done | bytes 3145760 | tf_op jit(solution)/shard_map/all_to_all | solution.py:85
  118.5 3.4 copy.227
  122.2 1.3 copy.204
  124.0 0.7 copy-done.2
  125.1 2.6 fusion.29
  127.7 2.7 copy.150
  130.9 2.4 copy.152
  133.3 2.4 convolution_convert_fusion.3
  135.7 1.1 copy.153
  136.8 2.3 reshape.92
  139.1 4.3 all-to-all-start.1
  143.9 5.2 %fusion = f32[8,512]{1,0:T(8,128)S(1)} fusion(f32[8,512,512]{1,2,0:T(8,128)} %get-tuple-element.26, f32[8,512]{1,0:T(8,128)S(1)} %get-tuple-element.25, pred[512,512]{0,1:T(8,128)(4,1)} %copy-done.11), kind=kLoop, calls=%fused_computation.5 | loop fusion | flops 8384512 | bytes 8683520 | tf_op jit(solution)/shard_map/reduce_sum | solution.py:26
  149.1 7.0 %fusion.15 = bf16[8,512,128]{1,2,0:T(8,128)(2,1)} fusion(bf16[512,8,128]{0,2,1:T(8,128)(2,1)S(1)} %bitcast.154, f32[8,512,512]{1,2,0:T(8,128)} %get-tuple-element.26, f32[8,512]{1,0:T(8,128)S(1)} %fusion, f32[8,512]{1,0:T(8,128)S(1)} %get-tuple-element.25, pred[512,512]{0,1:T(8,128)(4,1)S(1)} %copy-done.12), kind=kOutput, calls=%fused_computation.36 | convolution fusion | flops 547880960 | bytes 10780672 | tf_op jit(solution)/shard_map/hij,jhd->ihd/dot_general | solution.py:34
  156.1 2.3 copy.154
  158.4 11.6 %all-to-all-done.1 = bf16[8,64,1024]{2,1,0:T(8,128)(2,1)} async-done(((bf16[8,64,1024]{2,1,0:T(8,128)(2,1)}), bf16[8,64,1024]{2,1,0:T(8,128)(2,1)}, u32[]{:S(2)}, u32[]{:S(2)}) %all-to-all-start.1) | async-done | bytes 1048608 | tf_op jit(solution)/shard_map/all_to_all | solution.py:91
  170.0 9.8 %fusion.13 = f32[2048,2048]{1,0:T(8,128)} fusion(bf16[1,1,512,2048]{3,2,1,0:T(8,128)(2,1)S(1)} %copy-done, bf16[512,1024]{1,0:T(8,128)(2,1)} %bitcast.19, bf16[512,1024]{1,0:T(8,128)(2,1)} %copy.154), kind=kOutput, calls=%fused_computation.27 | convolution fusion | flops 4299161600 | bytes 20971520 | tf_op jit(solution)/shard_map/dot_general | solution.py:102
  179.8 8.2 %fusion.10 = bf16[512,2048]{0,1:T(8,128)(2,1)S(1)} fusion(bf16[2048,2048]{1,0:T(8,128)(2,1)} %all-gather.2.cloned.1.call-done, bf16[1,1,512,2048]{3,2,1,0:T(8,128)(2,1)S(1)} %copy-done), kind=kOutput, calls=%fused_computation.19 | convolution fusion | flops 4296015872 | bytes 12582912 | tf_op jit(solution)/shard_map/dot_general | solution.py:111
  188.0 1.3 copy-done.14
  189.3 1.0 slice_bitcast_fusion
  190.3 4.7 %copy.159 = bf16[1,512,1024]{2,0,1:T(2,128)(2,1)S(1)} copy(bf16[1,512,1024]{1,2,0:T(8,128)(2,1)} %slice_bitcast_fusion) | data formatting | bytes 2097152 | tf_op jit(solution)/shard_map/broadcast_in_dim | solution.py:115
  195.6 7.7 %reduce.6 = bf16[512,1024]{1,0:T(8,128)(2,1)} reduce(bf16[512,1,1024]{2,1,0:T(2,128)(2,1)S(1)} %bitcast.140, bf16[]{:T(256)} %broadcast.37), dimensions={1}, to_apply=%bitcast.105.reduce_sub_computation | reduce | bytes 2097154
  203.4 2.6 reshape.105
  206.0 3.6 all-to-all-start.2
  210.2 43.4 %all-to-all-done.2 = bf16[8,2,32768]{2,1,0:T(2,128)(2,1)S(1)} async-done(((bf16[8,2,32768]{2,1,0:T(2,128)(2,1)}), bf16[8,2,32768]{2,1,0:T(2,128)(2,1)S(1)}, u32[]{:S(2)}, u32[]{:S(2)}) %all-to-all-start.2) | async-done | bytes 1048608 | tf_op jit(solution)/shard_map/all_to_all | solution.py:114
  253.6 3.6 reshape.106
  257.2 7.8 %bitcast_reduce_fusion = bf16[512,1024]{1,0:T(8,128)(2,1)S(1)} fusion(bf16[512,1,1024]{2,1,0:T(2,128)(2,1)} %reshape.106), kind=kLoop, calls=%fused_computation.83 | loop fusion | bytes 2097152 | tf_op jit(solution)/shard_map/all_to_all | solution.py:114
  265.3 2.6 fusion.24
  267.9 2.6 copy.162
  270.7 1.3 multiply_reduce_fusion
  272.3 1.9 copy.167
  274.3 2.3 fusion.21
  276.5 1.1 copy.168
  277.7 2.3 stack_reshape.10
  280.0 1.0 fusion.20
  281.1 1.3 stack_reshape.9
  282.4 1.7 copy.170
  284.1 0.9 fusion.19
  285.1 1.3 stack_reshape.11
  286.4 2.2 pad_maximum_fusion
  288.6 2.2 copy.172
  290.8 4.7 %all-to-all-start.3 = ((bf16[3,8,64,1024]{3,2,0,1:T(8,128)(2,1)}), bf16[3,8,64,1024]{3,2,0,1:T(8,128)(2,1)}, u32[]{:S(2)}, u32[]{:S(2)}) async-start(bf16[3,8,64,1024]{3,2,0,1:T(8,128)(2,1)} %copy.172), calls=%async_computation.3 | async-start | bytes 6291456 | tf_op jit(solution)/shard_map/all_to_all | solution.py:120
  296.9 5.4 %multiply_convert_fusion = bf16[8,512,512]{1,2,0:T(8,128)(2,1)S(1)} fusion(f32[8,512,512]{1,2,0:T(8,128)} %get-tuple-element.26, f32[8,512]{1,0:T(8,128)S(1)} %get-tuple-element.9, f32[8,512]{1,0:T(8,128)S(1)} %log_add_fusion.1, pred[512,512]{0,1:T(8,128)(4,1)S(1)} %copy-done.13, bf16[512,8,128]{0,2,1:T(8,128)(2,1)S(1)} %bitcast.152, ...), kind=kOutput, calls=%fused_computation | convolution fusion | flops 549453824 | bytes 14974976 | tf_op jit(solution)/shard_map/ihd,jhd->hij/dot_general | solution.py:44
  302.3 0.7 multiply_convert_fusion.4
  303.0 1.3 copy-done.9
  304.9 4.1 multiply_convert_fusion.1
  309.0 1.3 copy.175
  310.3 6.3 %fusion.16 = bf16[8,128,512]{2,1,0:T(8,128)(2,1)} fusion(bf16[512,8,128]{0,2,1:T(8,128)(2,1)S(1)} %bitcast.153, f32[8,512,512]{1,2,0:T(8,128)} %get-tuple-element.26, f32[8,512]{1,0:T(8,128)S(1)} %log_add_fusion.1, pred[512,512]{0,1:T(8,128)(4,1)S(1)} %copy-done.13), kind=kOutput, calls=%fused_computation.37 | convolution fusion | flops 545783808 | bytes 10764288 | tf_op jit(solution)/shard_map/hij,ihd->jhd/dot_general | solution.py:41
  316.7 1.5 copy.177
  318.2 9.5 %fusion.9 = bf16[1,1,512,2048]{3,2,1,0:T(8,128)(2,1)} fusion(bf16[2048,2048]{1,0:T(8,128)(2,1)} %all-gather.2.cloned.1.call-done, bf16[512,1024]{1,0:T(8,128)(2,1)} %bitcast.19, bf16[512,1024]{1,0:T(8,128)(2,1)S(1)} %copy-done.22), kind=kOutput, calls=%fused_computation.18 | convolution fusion | flops 4300210176 | bytes 12582912 | tf_op jit(solution)/shard_map/dot_general | solution.py:139
  327.7 75.9 %all-to-all-done.3 = bf16[3,8,64,1024]{3,2,0,1:T(8,128)(2,1)} async-done(((bf16[3,8,64,1024]{3,2,0,1:T(8,128)(2,1)}), bf16[3,8,64,1024]{3,2,0,1:T(8,128)(2,1)}, u32[]{:S(2)}, u32[]{:S(2)}) %all-to-all-start.3) | async-done | bytes 3145760 | tf_op jit(solution)/shard_map/all_to_all | solution.py:120
  403.6 2.2 fusion.41
  405.9 1.5 maximum_bitcast_fusion.3
  407.4 1.5 maximum_bitcast_fusion.2
  408.9 1.5 maximum_bitcast_fusion.1
  410.4 39.5 %reduce-scatter.2.cloned.1.call-done = f32[64,2048]{1,0:T(8,128)} async-done(((f32[2048,2048]{1,0:T(8,128)}), f32[64,2048]{1,0:T(8,128)}) %reduce-scatter.2.cloned.1.call-update) | async-done | bytes 524304 | tf_op jit(solution)/shard_map/reduce_scatter | solution.py:107
  449.9 1.9 broadcast_multiply_fusion
  (86 shorter events, 8.5 us)
Async XLA Ops:
  7.2 162.8 %copy-start = (bf16[1,1,512,2048]{3,2,1,0:T(8,128)(2,1)S(1)}, bf16[1,1,512,2048]{3,2,1,0:T(8,128)(2,1)}, u32[]{:S(2)}) copy-start(bf16[1,1,512,2048]{3,2,1,0:T(8,128)(2,1)} %param.10) | copy-start | bytes 6291460
  7.2 172.6 %all-gather.2.cloned.1.call-start = ((), (), s32[]{:S(2)}) async-start(), calls=%async_computation.5 | async-start | bytes 10485760 | tf_op jit(solution)/shard_map/all_gather | solution.py:82
  7.9 2.2 copy-start.16
  7.9 2.8 copy-start.17
  17.7 6.7 %copy-start.29 = (s32[4,4]{1,0:T(4,128)S(1)}, s32[4,4]{1,0:T(4,128)}, u32[]{:S(2)}) copy-start(s32[4,4]{1,0:T(4,128)} %param.12) | copy-start | bytes 196
  17.7 100.7 %all-to-all-start = ((bf16[1,3,512,1024]{3,1,0,2:T(4,128)(2,1)}), bf16[1,3,512,1024]{3,1,0,2:T(4,128)(2,1)}, u32[]{:S(2)}, u32[]{:S(2)}) async-start(bf16[1,3,512,1024]{3,1,0,2:T(4,128)(2,1)} %copy.146), calls=%async_computation | async-start | bytes 8388608 | tf_op jit(solution)/shard_map/all_to_all | solution.py:85
  24.7 5.6 %copy-start.11 = (pred[512,512]{0,1:T(8,128)(4,1)}, pred[512,512]{0,1:T(8,128)(4,1)S(1)}, u32[]{:S(2)}) copy-start(pred[512,512]{0,1:T(8,128)(4,1)S(1)} %fusion.22) | copy-start | bytes 786436
  24.7 5.5 %copy-start.28 = (s32[8,8]{1,0:T(8,128)S(1)}, s32[8,8]{1,0:T(8,128)}, u32[]{:S(2)}) copy-start(s32[8,8]{1,0:T(8,128)} %param.13) | copy-start | bytes 772
  27.6 8.8 %copy-start.6 = (bf16[1,1,512,1024]{2,3,1,0:T(8,128)(2,1)}, bf16[1,1,512,1024]{2,3,1,0:T(8,128)(2,1)S(1)}, u32[]{:S(2)}) copy-start(bf16[1,1,512,1024]{2,3,1,0:T(8,128)(2,1)S(1)} %copy.202) | copy-start | bytes 3145732
  30.3 100.5 %copy-start.26 = (pred[8,8]{1,0:T(8,128)(4,1)}, pred[8,8]{1,0:T(8,128)(4,1)S(1)}, u32[]{:S(2)}) copy-start(pred[8,8]{1,0:T(8,128)(4,1)S(1)} %broadcast_compare_fusion) | copy-start | bytes 196
  123.7 1.0 copy-start.2
  124.0 1.1 copy-start.4
  139.1 30.9 %all-to-all-start.1 = ((bf16[8,64,1024]{2,1,0:T(8,128)(2,1)}), bf16[8,64,1024]{2,1,0:T(8,128)(2,1)}, u32[]{:S(2)}, u32[]{:S(2)}) async-start(bf16[8,64,1024]{2,1,0:T(8,128)(2,1)} %reshape.92), calls=%async_computation.1 | async-start | bytes 2097152 | tf_op jit(solution)/shard_map/all_to_all | solution.py:91
  143.4 306.5 %reduce-scatter.2.cloned.1.call-start = ((), (), s32[]{:S(2)}) async-start(), calls=%async_computation.6 | async-start | bytes 17301504 | tf_op jit(solution)/shard_map/reduce_scatter | solution.py:107
  143.9 5.2 %copy-start.12 = (pred[512,512]{0,1:T(8,128)(4,1)S(1)}, pred[512,512]{0,1:T(8,128)(4,1)}, u32[]{:S(2)}) copy-start(pred[512,512]{0,1:T(8,128)(4,1)} %copy-done.11) | copy-start | bytes 786436
  143.9 5.2 %copy-start.20 = (bf16[1,1,512,1024]{2,3,1,0:T(8,128)(2,1)S(1)}, bf16[1,1,512,1024]{2,3,1,0:T(8,128)(2,1)}, u32[]{:S(2)}) copy-start(bf16[1,1,512,1024]{2,3,1,0:T(8,128)(2,1)} %copy.144) | copy-start | bytes 3145732
  149.1 7.0 %copy-start.24 = (f32[8,512]{1,0:T(8,128)}, f32[8,512]{1,0:T(8,128)S(1)}, u32[]{:S(2)}) copy-start(f32[8,512]{1,0:T(8,128)S(1)} %fusion) | copy-start | bytes 49156
  188.0 1.3 copy-start.14
  206.0 47.6 %all-to-all-start.2 = ((bf16[8,2,32768]{2,1,0:T(2,128)(2,1)}), bf16[8,2,32768]{2,1,0:T(2,128)(2,1)S(1)}, u32[]{:S(2)}, u32[]{:S(2)}) async-start(bf16[8,2,32768]{2,1,0:T(2,128)(2,1)} %reshape.105), calls=%async_computation.2 | async-start | bytes 2097152 | tf_op jit(solution)/shard_map/all_to_all | solution.py:114
  257.1 8.1 %copy-start.5 = (bf16[64,8,8,128]{3,2,1,0:T(8,128)(2,1)S(1)}, bf16[64,8,8,128]{3,2,1,0:T(8,128)(2,1)}, u32[]{:S(2)}) copy-start(bf16[64,8,8,128]{3,2,1,0:T(8,128)(2,1)} %copy.204) | copy-start | bytes 3145732
  270.6 1.6 copy-start.23
  270.6 1.6 copy-start.27
  274.3 5.7 %copy-start.3 = (bf16[64,8,8,128]{3,2,1,0:T(8,128)(2,1)S(1)}, bf16[64,8,8,128]{3,2,1,0:T(8,128)(2,1)}, u32[]{:S(2)}) copy-start(bf16[64,8,8,128]{3,2,1,0:T(8,128)(2,1)} %copy-done.2) | copy-start | bytes 3145732
  290.8 4.7 %copy-start.25 = (f32[8,512]{1,0:T(8,128)S(1)}, f32[8,512]{1,0:T(8,128)}, u32[]{:S(2)}) copy-start(f32[8,512]{1,0:T(8,128)} %copy-done.24) | copy-start | bytes 49156
  290.8 4.8 %copy-start.8 = (bf16[8,512,128]{1,2,0:T(8,128)(2,1)S(1)}, bf16[8,512,128]{1,2,0:T(8,128)(2,1)}, u32[]{:S(2)}) copy-start(bf16[8,512,128]{1,2,0:T(8,128)(2,1)} %fusion.15) | copy-start | bytes 3145732
  290.8 4.8 %copy-start.15 = (bf16[512,2048]{0,1:T(8,128)(2,1)S(1)}, bf16[512,2048]{0,1:T(8,128)(2,1)}, u32[]{:S(2)}) copy-start(bf16[512,2048]{0,1:T(8,128)(2,1)} %copy-done.14) | copy-start | bytes 6291460
  290.8 112.8 %all-to-all-start.3 = ((bf16[3,8,64,1024]{3,2,0,1:T(8,128)(2,1)}), bf16[3,8,64,1024]{3,2,0,1:T(8,128)(2,1)}, u32[]{:S(2)}, u32[]{:S(2)}) async-start(bf16[3,8,64,1024]{3,2,0,1:T(8,128)(2,1)} %copy.172), calls=%async_computation.3 | async-start | bytes 6291456 | tf_op jit(solution)/shard_map/all_to_all | solution.py:120
  295.5 1.0 copy-start.13
  295.5 1.3 copy-start.21
  295.9 6.3 %copy-start.18 = (bf16[512,1024]{0,1:T(8,128)(2,1)}, bf16[512,1024]{0,1:T(8,128)(2,1)S(1)}, u32[]{:S(2)}) copy-start(bf16[512,1024]{0,1:T(8,128)(2,1)S(1)} %get-tuple-element.10) | copy-start | bytes 3145732
  296.9 5.4 %copy-start.7 = (bf16[1,1,512,1024]{2,3,1,0:T(8,128)(2,1)S(1)}, bf16[1,1,512,1024]{2,3,1,0:T(8,128)(2,1)}, u32[]{:S(2)}) copy-start(bf16[1,1,512,1024]{2,3,1,0:T(8,128)(2,1)} %copy-done.6) | copy-start | bytes 3145732
  302.3 2.1 copy-start.9
  304.9 5.5 %copy-start.19 = (bf16[512,1024]{0,1:T(8,128)(2,1)S(1)}, bf16[512,1024]{0,1:T(8,128)(2,1)}, u32[]{:S(2)}) copy-start(bf16[512,1024]{0,1:T(8,128)(2,1)} %copy-done.18) | copy-start | bytes 3145732
  310.3 7.8 %copy-start.22 = (bf16[512,1024]{1,0:T(8,128)(2,1)S(1)}, bf16[512,1024]{1,0:T(8,128)(2,1)}, u32[]{:S(2)}) copy-start(bf16[512,1024]{1,0:T(8,128)(2,1)} %copy.154) | copy-start | bytes 3145732
  405.9 1.5 copy-start.10
  407.4 44.4 %copy-start.1 = (bf16[1,1,512,2048]{3,2,1,0:T(8,128)(2,1)S(1)}, bf16[1,1,512,2048]{3,2,1,0:T(8,128)(2,1)}, u32[]{:S(2)}) copy-start(bf16[1,1,512,2048]{3,2,1,0:T(8,128)(2,1)} %param.10) | copy-start | bytes 6291460
Sparse Core Ops, SparseCore 0:
  9.9 90.2 all-gather.1
  179.9 269.9 reduce-scatter.1

commit v4 on v3

--- a/solution.py
+++ b/solution.py
@@ -78,8 +78,10 @@
     heads_half = half // DH
     rows = lax.axis_size("seq")
     cols_each = tokens // rows
-
     weight = lax.all_gather(out_weight, "dp", axis=0, tiled=True)
+    core = lax.axis_index("seq") % 2
+    pairs = [(2 * m + j, 2 * m + 1 - j) for m in range(rows // 2) for j in range(2)]
+    grad_mate = lax.ppermute(out_grad[0, 0], "seq", pairs)
 
     packed = jnp.stack([t[0, 0, :, half:] for t in (queries, keys, values)])
     shipped = lax.all_to_all(packed[None], "seq", split_axis=2, concat_axis=0, tiled=True)
@@ -99,14 +101,26 @@
 
     flat_grad = out_grad[0, 0]
     attention = jnp.concatenate([row_out.reshape(tokens, half), col_back[0]], axis=1)
+
+    dp_size = lax.axis_size("dp")
+    block = features // (dp_size * rows)
+    by_parity = attention.reshape(tokens, features // (2 * block), 2, block)
+    own_rows = jnp.where(core == 0, by_parity[:, :, 0], by_parity[:, :, 1])
+    mate_rows = lax.ppermute(
+        jnp.where(core == 0, by_parity[:, :, 1], by_parity[:, :, 0]), "seq", pairs
+    )
+    pair_attn = jnp.concatenate([own_rows, mate_rows], axis=0).reshape(2 * tokens, features // 2)
+    pair_grad = jnp.concatenate([flat_grad, grad_mate], axis=0)
     partial = lax.dot_general(
-        attention, flat_grad, (((0,), (0,)), ((), ())), preferred_element_type=jnp.float32
-    )
+        pair_attn, pair_grad, (((0,), (0,)), ((), ())), preferred_element_type=jnp.float32
+    ).reshape(dp_size, rows // 2, block, features)
     partial, weight = lax.optimization_barrier((partial, weight))
-    devices_all = lax.axis_size(("dp", "seq"))
-    wo_grad = lax.psum_scatter(partial, ("dp", "seq"), scatter_dimension=0, tiled=True) * (
-        1.0 / math.sqrt(tokens * devices_all)
-    )
+    over_dp = lax.all_to_all(partial, "dp", split_axis=0, concat_axis=0, tiled=True).sum(axis=0)
+    parity_groups = [[2 * m + c for m in range(rows // 2)] for c in range(2)]
+    over_z = lax.all_to_all(
+        over_dp, "seq", split_axis=0, concat_axis=0, tiled=True, axis_index_groups=parity_groups
+    ).sum(axis=0)
+    wo_grad = over_z * (1.0 / math.sqrt(tokens * dp_size * rows))
 
     attn_grad = lax.dot_general(
         flat_grad, weight, (((1,), (1,)), ((), ())), preferred_element_type=jnp.float32

time: 466 us -> 475 us (1.019)
  blocking collectives: 0 us -> 30.1 us
  waiting for transfers between devices: 253 us -> 226 us
  other arithmetic: 25 us -> 32.8 us
  matrix products: 68.8 us -> 62.5 us
  starting transfers between devices: 19.7 us -> 25.1 us
    reduce_scatter x1 -> x0, waiting for transfers between devices: 39.5 us -> none  [on_device(): lax.psum_scatter(partial, ('dp', 'seq'), scatter_dimension=0, tiled=True)]
    all_to_all x0 -> x1, blocking collectives: none -> 30.1 us  [on_device(): lax.all_to_all(attn_grad[None, :, half:], 'seq', split_axis=1, concat_axi...]
    all_to_all x1 -> x2, waiting for transfers between devices: 43.4 us -> 72.9 us  [the longest x1 49.9 us: on_device(): lax.all_to_all(partial, 'dp', split_axis=0, concat_axis=0, tiled=True)]
    all_to_all x1, waiting for transfers between devices: 75.9 us -> 49.6 us  [on_device(): lax.all_to_all(jnp.stack([g.reshape(rows, cols_each, half) for g in col_g...]
    concatenate x0 -> x2, local copies, waits for them, and re-layouts: none -> 6.91 us  [on_device(): jnp.concatenate([row_out.reshape(tokens, half), col_back[0]], axis=1)]
    reduce_sum x0 -> x2, other arithmetic: none -> 5.93 us  [the longest x1 5.78 us: on_device(): lax.all_to_all(partial, 'dp', split_axis=0, concat_axis=0, tiled=True)]
    all_to_all x1 -> x2, starting transfers between devices: 3.56 us -> 9.47 us  [the longest x1 5.61 us: on_device(): lax.all_to_all(partial, 'dp', split_axis=0, concat_axis=0, tiled=True)]
    unnamed x71 -> x77, local copies, waits for them, and re-layouts: 18.8 us -> 18.3 us
  transfers between devices with their start and end apart: 6 -> 8, of which waited for: 5 -> 6; matrix products, arithmetic and copies ran while one was open for 36% -> 30% of each run, Pallas kernels for 0% -> 0%
where the time goes in v4:
time: 475 us; the launch traced here: 470 us
  waiting for transfers between devices  226 us (48%)
  local copies, waits for them, and re-layouts  79 us (17%)
  matrix products  62.5 us (13%)
  other arithmetic  32.8 us (7%)
  blocking collectives  30.1 us (6%)
  starting transfers between devices  25.1 us (5%)
  between operations  14.9 us (3%)
    all_to_all x1, waiting for transfers between devices, on_device(): lax.all_to_all(packed[None], 'seq', split_axis=2, concat_axis=0, tiled=True)  84.8 us
    all_to_all x1, waiting for transfers between devices, on_device(): lax.all_to_all(partial, 'dp', split_axis=0, concat_axis=0, tiled=True)  49.9 us
    all_to_all x1, waiting for transfers between devices, on_device(): lax.all_to_all(jnp.stack([g.reshape(rows, cols_each, half) for g in col_g...  49.6 us
    all_to_all x1, blocking collectives, on_device(): lax.all_to_all(attn_grad[None, :, half:], 'seq', split_axis=1, concat_axi...  30.1 us
    all_to_all x1, waiting for transfers between devices, on_device(): lax.all_to_all(over_dp, 'seq', split_axis=0, concat_axis=0, tiled=True, a...  22.9 us
    unnamed x77, local copies, waits for them, and re-layouts  18.3 us
    all_to_all x1, waiting for transfers between devices, on_device(): lax.all_to_all(col_out.reshape(rows, cols_each, half), 'seq', split_axis=...  15.2 us
    unnamed x3, other arithmetic  10.2 us
  transfers between devices with their start and end apart: 8, of which 6 were waited for; matrix products, arithmetic and copies ran while one was open for 30% of the time, Pallas kernels for 0%

profile of v4, /device:TPU:0, one launch (start us, length us, event | category | flops | bytes accessed | tf_op | source)
XLA Modules:
  0.0 470.0 jit_solution(5689248221337039734)
XLA Ops:
  9.0 1.4 copy-done.22
  11.0 1.6 fusion.50
  12.9 4.7 copy.207
  17.6 6.7 %all-to-all-start = ((bf16[1,3,512,1024]{3,1,0,2:T(4,128)(2,1)}), bf16[1,3,512,1024]{3,1,0,2:T(4,128)(2,1)}, u32[]{:S(2)}, u32[]{:S(2)}) async-start(bf16[1,3,512,1024]{3,1,0,2:T(4,128)(2,1)} %copy.207), calls=%async_computation | async-start | bytes 8388608 | tf_op jit(solution)/shard_map/all_to_all | solution.py:87
  24.8 1.3 copy.205
  26.5 1.6 copy.269
  28.7 4.8 %select_reduce_fusion = (f32[8,512]{1,0:T(8,128)S(1)}, f32[8,512,512]{1,2,0:T(8,128)}) fusion(pred[512,512]{0,1:T(8,128)(4,1)S(1)} %fusion.28, bf16[512,8,128]{0,2,1:T(8,128)(2,1)S(1)} %bitcast.180, bf16[512,8,128]{0,2,1:T(8,128)(2,1)S(1)} %bitcast.168), kind=kOutput, calls=%fused_computation.4 | convolution fusion | flops 543158272 | bytes 10764288 | tf_op jit(solution)/shard_map/ihd,jhd->hij/dot_general | solution.py:32
  33.5 84.8 %all-to-all-done = bf16[1,3,512,1024]{3,1,0,2:T(4,128)(2,1)} async-done(((bf16[1,3,512,1024]{3,1,0,2:T(4,128)(2,1)}), bf16[1,3,512,1024]{3,1,0,2:T(4,128)(2,1)}, u32[]{:S(2)}, u32[]{:S(2)}) %all-to-all-start) | async-done | bytes 3145760 | tf_op jit(solution)/shard_map/all_to_all | solution.py:87
  118.3 3.4 copy.296
  123.7 1.3 fusion.35
  125.0 1.1 copy.211
  126.6 1.6 copy.213
  128.5 1.0 copy-done.3
  130.5 1.3 reshape.106
  131.8 3.8 all-to-all-start.1
  135.6 5.2 %fusion = f32[8,512]{1,0:T(8,128)S(1)} fusion(f32[8,512,512]{1,2,0:T(8,128)} %get-tuple-element.26, f32[8,512]{1,0:T(8,128)S(1)} %get-tuple-element.25, pred[512,512]{0,1:T(8,128)(4,1)} %copy-done.16), kind=kLoop, calls=%fused_computation.5 | loop fusion | flops 8384512 | bytes 8683520 | tf_op jit(solution)/shard_map/reduce_sum | solution.py:26
  140.9 6.0 %fusion.18 = bf16[8,512,128]{1,2,0:T(8,128)(2,1)S(1)} fusion(bf16[512,8,128]{0,2,1:T(8,128)(2,1)S(1)} %bitcast.185, f32[8,512,512]{1,2,0:T(8,128)} %get-tuple-element.26, f32[8,512]{1,0:T(8,128)S(1)} %fusion, f32[8,512]{1,0:T(8,128)S(1)} %get-tuple-element.25, pred[512,512]{0,1:T(8,128)(4,1)S(1)} %copy-done.17), kind=kOutput, calls=%fused_computation.43 | convolution fusion | flops 547880960 | bytes 10780672 | tf_op jit(solution)/shard_map/hij,jhd->ihd/dot_general | solution.py:34
  146.9 15.2 %all-to-all-done.1 = bf16[8,64,1024]{2,1,0:T(8,128)(2,1)S(1)} async-done(((bf16[8,64,1024]{2,1,0:T(8,128)(2,1)}), bf16[8,64,1024]{2,1,0:T(8,128)(2,1)S(1)}, u32[]{:S(2)}, u32[]{:S(2)}) %all-to-all-start.1) | async-done | bytes 1048608 | tf_op jit(solution)/shard_map/all_to_all | solution.py:93
  163.1 2.3 reshape.120
  165.4 4.6 copy.267
  170.4 2.5 collective-permute-done
  173.2 8.4 %fusion.4 = f32[4,4,64,2048]{3,2,1,0:T(8,128)} fusion(bf16[4,4,64,1024]{3,2,1,0:T(8,128)(2,1)S(1)} %bitcast.182, bf16[512,2048]{1,0:T(8,128)(2,1)} %collective-permute-done.1, bf16[512,2048]{1,0:T(8,128)(2,1)S(1)} %bitcast.191), kind=kOutput, calls=%fused_computation.9 | convolution fusion | flops 4303355904 | bytes 14680064 | tf_op jit(solution)/shard_map/dot_general | solution.py:114
  181.5 8.5 %fusion.13 = bf16[512,2048]{0,1:T(8,128)(2,1)S(1)} fusion(bf16[2048,2048]{1,0:T(8,128)(2,1)} %all-gather.2.cloned.1.call-done, bf16[1,1,512,2048]{3,2,1,0:T(8,128)(2,1)} %param.10), kind=kOutput, calls=%fused_computation.23 | convolution fusion | flops 4296015872 | bytes 12582912 | tf_op jit(solution)/shard_map/dot_general | solution.py:125
  190.1 1.3 copy-done.19
  191.5 4.2 copy.225
  196.3 8.0 %reduce.6 = bf16[512,1024]{1,0:T(8,128)(2,1)S(1)} reduce(bf16[512,1,1024]{2,1,0:T(2,128)(2,1)} %bitcast.170, bf16[]{:T(256)} %broadcast.41), dimensions={1}, to_apply=%bitcast.131.reduce_sub_computation | reduce | bytes 2097154
  204.3 1.6 reshape.122
  205.8 30.1 %all_to_all.55 = bf16[8,2,32768]{2,1,0:T(2,128)(2,1)S(1)} all-to-all(bf16[8,2,32768]{2,1,0:T(2,128)(2,1)} %reshape.122), channel_id=1, replica_groups=mesh['dp'=4,'seq'=8] {'seq'}, dimensions={0} | all-to-all | bytes 2097152 | tf_op jit(solution)/shard_map/all_to_all | solution.py:128
  235.9 5.6 %all-to-all-start.4 = ((f32[4,4,64,2048]{3,2,1,0:T(8,128)}), f32[4,4,64,2048]{3,2,1,0:T(8,128)}, u32[]{:S(2)}, u32[]{:S(2)}) async-start(f32[4,4,64,2048]{3,2,1,0:T(8,128)} %fusion.4), calls=%async_computation.4 | async-start | bytes 16777216 | tf_op jit(solution)/shard_map/all_to_all | solution.py:118
  242.1 3.6 reshape.123
  245.7 7.8 %bitcast_reduce_fusion = bf16[512,1024]{1,0:T(8,128)(2,1)S(1)} fusion(bf16[512,1,1024]{2,1,0:T(2,128)(2,1)} %reshape.123), kind=kLoop, calls=%fused_computation.96 | loop fusion | bytes 2097152 | tf_op jit(solution)/shard_map/all_to_all | solution.py:128
  253.8 2.6 fusion.30
  256.5 3.3 copy.228
  259.9 2.0 multiply_reduce_fusion
  261.9 1.1 copy.264
  263.0 1.8 multiply_convert_fusion.5
  264.7 2.9 copy.236
  268.7 1.3 stack_reshape.11
  269.9 1.7 copy.233
  271.7 2.2 fusion.24
  273.9 1.2 copy.234
  275.1 2.3 stack_reshape.10
  278.6 1.3 stack_reshape.9
  279.8 1.9 pad_maximum_fusion
  281.7 2.1 copy.238
  283.9 49.9 %all-to-all-done.4 = f32[4,4,64,2048]{3,2,1,0:T(8,128)} async-done(((f32[4,4,64,2048]{3,2,1,0:T(8,128)}), f32[4,4,64,2048]{3,2,1,0:T(8,128)}, u32[]{:S(2)}, u32[]{:S(2)}) %all-to-all-start.4) | async-done | bytes 8388640 | tf_op jit(solution)/shard_map/all_to_all | solution.py:118
  333.8 4.5 all-to-all-start.3
  338.3 1.3 copy.215
  340.8 5.3 %multiply_convert_fusion = bf16[8,512,512]{1,2,0:T(8,128)(2,1)S(1)} fusion(f32[8,512,512]{1,2,0:T(8,128)} %get-tuple-element.26, f32[8,512]{1,0:T(8,128)S(1)} %get-tuple-element.9, f32[8,512]{1,0:T(8,128)S(1)} %log_add_fusion.1, pred[512,512]{0,1:T(8,128)(4,1)S(1)} %copy-done.18, bf16[512,8,128]{0,2,1:T(8,128)(2,1)S(1)} %bitcast.183, ...), kind=kOutput, calls=%fused_computation | convolution fusion | flops 549453824 | bytes 14974976 | tf_op jit(solution)/shard_map/ihd,jhd->hij/dot_general | solution.py:44
  346.9 1.2 copy-done.9
  348.1 1.3 copy.239
  349.4 3.7 multiply_convert_fusion.1
  353.1 1.3 copy.241
  354.4 5.8 %reduce_sum.38 = f32[4,64,2048]{2,1,0:T(8,128)} reduce(f32[4,4,64,2048]{3,2,1,0:T(8,128)} %all-to-all-done.4, f32[]{:T(128)} %constant.13.clone.1), dimensions={0}, to_apply=%region_4.5 | reduce | flops 1572864 | bytes 10485764 | tf_op jit(solution)/shard_map/reduce_sum | solution.py:118
  360.2 49.6 %all-to-all-done.3 = bf16[3,8,64,1024]{3,2,0,1:T(8,128)(2,1)} async-done(((bf16[3,8,64,1024]{3,2,0,1:T(8,128)(2,1)}), bf16[3,8,64,1024]{3,2,0,1:T(8,128)(2,1)}, u32[]{:S(2)}, u32[]{:S(2)}) %all-to-all-start.3) | async-done | bytes 3145760 | tf_op jit(solution)/shard_map/all_to_all | solution.py:134
  409.8 3.9 all-to-all-start.5
  413.7 6.7 %fusion.19 = bf16[8,128,512]{2,1,0:T(8,128)(2,1)} fusion(bf16[512,8,128]{0,2,1:T(8,128)(2,1)} %bitcast.184, f32[8,512,512]{1,2,0:T(8,128)} %get-tuple-element.26, f32[8,512]{1,0:T(8,128)S(1)} %log_add_fusion.1, pred[512,512]{0,1:T(8,128)(4,1)S(1)} %copy-done.18), kind=kOutput, calls=%fused_computation.44 | convolution fusion | flops 545783808 | bytes 10764288 | tf_op jit(solution)/shard_map/hij,ihd->jhd/dot_general | solution.py:41
  420.3 2.3 copy.243
  422.6 9.5 %fusion.12 = bf16[1,1,512,2048]{3,2,1,0:T(8,128)(2,1)} fusion(bf16[2048,2048]{1,0:T(8,128)(2,1)} %all-gather.2.cloned.1.call-done, bf16[512,1024]{1,0:T(8,128)(2,1)S(1)} %bitcast.171, bf16[512,1024]{1,0:T(8,128)(2,1)} %copy.215), kind=kOutput, calls=%fused_computation.22 | convolution fusion | flops 4300210176 | bytes 12582912 | tf_op jit(solution)/shard_map/dot_general | solution.py:153
  432.1 2.3 fusion.48
  434.4 1.5 maximum_bitcast_fusion.3
  435.9 1.5 maximum_bitcast_fusion.4
  437.4 1.5 maximum_bitcast_fusion.5
  438.9 22.9 %all-to-all-done.5 = f32[4,64,2048]{2,1,0:T(8,128)S(1)} async-done(((f32[4,64,2048]{2,1,0:T(8,128)}), f32[4,64,2048]{2,1,0:T(8,128)S(1)}, u32[]{:S(2)}, u32[]{:S(2)}) %all-to-all-start.5) | async-done | bytes 2097184 | tf_op jit(solution)/shard_map/all_to_all | solution.py:120
  (103 shorter events, 16.2 us)
Async XLA Ops:
  7.2 1.6 copy-start.21
  7.2 174.4 %all-gather.2.cloned.1.call-start = ((), (), s32[]{:S(2)}) async-start(), calls=%async_computation.6 | async-start | bytes 10485760 | tf_op jit(solution)/shard_map/all_gather | solution.py:81
  8.8 1.6 copy-start.22
  8.8 2.2 copy-start.23
  17.6 8.6 %copy-start.31 = (s32[4,4]{1,0:T(4,128)S(1)}, s32[4,4]{1,0:T(4,128)}, u32[]{:S(2)}) copy-start(s32[4,4]{1,0:T(4,128)} %param.12) | copy-start | bytes 196
  17.6 100.7 %all-to-all-start = ((bf16[1,3,512,1024]{3,1,0,2:T(4,128)(2,1)}), bf16[1,3,512,1024]{3,1,0,2:T(4,128)(2,1)}, u32[]{:S(2)}, u32[]{:S(2)}) async-start(bf16[1,3,512,1024]{3,1,0,2:T(4,128)(2,1)} %copy.207), calls=%async_computation | async-start | bytes 8388608 | tf_op jit(solution)/shard_map/all_to_all | solution.py:87
  24.3 148.9 %collective-permute-start.1 = (bf16[512,2048]{1,0:T(8,128)(2,1)}, bf16[512,2048]{1,0:T(8,128)(2,1)}, u32[]{:S(2)}, u32[]{:S(2)}) collective-permute-start(bf16[512,2048]{1,0:T(8,128)(2,1)} %bitcast.190), channel_id=1, source_target_pairs={{0,1},{1,0},{2,3},{3,2},{4,5},{5,4},{6,7},{7,6},{8,9},{9,8},{10,11... | collective-permute-start | bytes 6291464 | tf_op jit(solution)/shard_map/ppermute | solution.py:84
  24.8 3.8 copy-start.30
  26.4 7.1 %copy-start.16 = (pred[512,512]{0,1:T(8,128)(4,1)}, pred[512,512]{0,1:T(8,128)(4,1)S(1)}, u32[]{:S(2)}) copy-start(pred[512,512]{0,1:T(8,128)(4,1)S(1)} %fusion.28) | copy-start | bytes 786436
  28.1 5.5 %copy-start.14 = (bf16[1,1,512,1024]{2,3,1,0:T(8,128)(2,1)}, bf16[1,1,512,1024]{2,3,1,0:T(8,128)(2,1)S(1)}, u32[]{:S(2)}) copy-start(bf16[1,1,512,1024]{2,3,1,0:T(8,128)(2,1)S(1)} %copy.269) | copy-start | bytes 3145732
  28.6 4.9 %copy-start.5 = (bf16[1,1,512,1024]{2,3,1,0:T(8,128)(2,1)}, bf16[1,1,512,1024]{2,3,1,0:T(8,128)(2,1)S(1)}, u32[]{:S(2)}) copy-start(bf16[1,1,512,1024]{2,3,1,0:T(8,128)(2,1)S(1)} %copy.270) | copy-start | bytes 3145732
  28.6 97.9 %copy-start.29 = (pred[8,8]{1,0:T(8,128)(4,1)}, pred[8,8]{1,0:T(8,128)(4,1)S(1)}, u32[]{:S(2)}) copy-start(pred[8,8]{1,0:T(8,128)(4,1)S(1)} %broadcast_compare_fusion) | copy-start | bytes 196
  122.3 1.0 copy-start
  122.6 1.1 copy-start.2
  128.5 1.0 copy-start.3
  131.8 30.3 %all-to-all-start.1 = ((bf16[8,64,1024]{2,1,0:T(8,128)(2,1)}), bf16[8,64,1024]{2,1,0:T(8,128)(2,1)S(1)}, u32[]{:S(2)}, u32[]{:S(2)}) async-start(bf16[8,64,1024]{2,1,0:T(8,128)(2,1)} %reshape.106), calls=%async_computation.1 | async-start | bytes 2097152 | tf_op jit(solution)/shard_map/all_to_all | solution.py:93
  135.6 5.2 %copy-start.17 = (pred[512,512]{0,1:T(8,128)(4,1)S(1)}, pred[512,512]{0,1:T(8,128)(4,1)}, u32[]{:S(2)}) copy-start(pred[512,512]{0,1:T(8,128)(4,1)} %copy-done.16) | copy-start | bytes 786436
  135.6 5.2 %copy-start.25 = (bf16[1,1,512,1024]{2,3,1,0:T(8,128)(2,1)S(1)}, bf16[1,1,512,1024]{2,3,1,0:T(8,128)(2,1)}, u32[]{:S(2)}) copy-start(bf16[1,1,512,1024]{2,3,1,0:T(8,128)(2,1)} %copy.205) | copy-start | bytes 3145732
  140.8 6.0 %copy-start.27 = (f32[8,512]{1,0:T(8,128)}, f32[8,512]{1,0:T(8,128)S(1)}, u32[]{:S(2)}) copy-start(f32[8,512]{1,0:T(8,128)S(1)} %fusion) | copy-start | bytes 49156
  162.1 1.0 copy-start.7
  170.2 3.0 copy-start.32
  170.2 2.7 collective-permute-start
  190.1 1.3 copy-start.19
  235.9 97.9 %all-to-all-start.4 = ((f32[4,4,64,2048]{3,2,1,0:T(8,128)}), f32[4,4,64,2048]{3,2,1,0:T(8,128)}, u32[]{:S(2)}, u32[]{:S(2)}) async-start(f32[4,4,64,2048]{3,2,1,0:T(8,128)} %fusion.4), calls=%async_computation.4 | async-start | bytes 16777216 | tf_op jit(solution)/shard_map/all_to_all | solution.py:118
  245.7 8.1 %copy-start.4 = (bf16[64,8,8,128]{3,2,1,0:T(8,128)(2,1)S(1)}, bf16[64,8,8,128]{3,2,1,0:T(8,128)(2,1)}, u32[]{:S(2)}) copy-start(bf16[64,8,8,128]{3,2,1,0:T(8,128)(2,1)} %copy-done.3) | copy-start | bytes 3145732
  271.7 5.8 %copy-start.1 = (bf16[64,8,8,128]{3,2,1,0:T(8,128)(2,1)S(1)}, bf16[64,8,8,128]{3,2,1,0:T(8,128)(2,1)}, u32[]{:S(2)}) copy-start(bf16[64,8,8,128]{3,2,1,0:T(8,128)(2,1)} %copy-done) | copy-start | bytes 3145732
  278.4 1.4 copy-start.12
  283.9 55.7 %copy-start.28 = (f32[8,512]{1,0:T(8,128)S(1)}, f32[8,512]{1,0:T(8,128)}, u32[]{:S(2)}) copy-start(f32[8,512]{1,0:T(8,128)} %copy-done.27) | copy-start | bytes 49156
  283.9 55.7 %copy-start.20 = (bf16[512,2048]{0,1:T(8,128)(2,1)S(1)}, bf16[512,2048]{0,1:T(8,128)(2,1)}, u32[]{:S(2)}) copy-start(bf16[512,2048]{0,1:T(8,128)(2,1)} %copy-done.19) | copy-start | bytes 6291460
  333.8 76.0 %all-to-all-start.3 = ((bf16[3,8,64,1024]{3,2,0,1:T(8,128)(2,1)}), bf16[3,8,64,1024]{3,2,0,1:T(8,128)(2,1)}, u32[]{:S(2)}, u32[]{:S(2)}) async-start(bf16[3,8,64,1024]{3,2,0,1:T(8,128)(2,1)} %copy.238), calls=%async_computation.3 | async-start | bytes 6291456 | tf_op jit(solution)/shard_map/all_to_all | solution.py:134
  338.2 1.7 copy-start.18
  339.6 1.2 copy-start.26
  339.9 6.2 %copy-start.24 = (bf16[512,1024]{0,1:T(8,128)(2,1)}, bf16[512,1024]{0,1:T(8,128)(2,1)S(1)}, u32[]{:S(2)}) copy-start(bf16[512,1024]{0,1:T(8,128)(2,1)S(1)} %get-tuple-element.10) | copy-start | bytes 3145732
  340.8 5.3 %copy-start.6 = (bf16[1,1,512,1024]{2,3,1,0:T(8,128)(2,1)S(1)}, bf16[1,1,512,1024]{2,3,1,0:T(8,128)(2,1)}, u32[]{:S(2)}) copy-start(bf16[1,1,512,1024]{2,3,1,0:T(8,128)(2,1)} %copy-done.5) | copy-start | bytes 3145732
  346.1 1.9 copy-start.9
  346.1 3.2 copy-start.15
  409.8 52.1 %all-to-all-start.5 = ((f32[4,64,2048]{2,1,0:T(8,128)}), f32[4,64,2048]{2,1,0:T(8,128)S(1)}, u32[]{:S(2)}, u32[]{:S(2)}) async-start(f32[4,64,2048]{2,1,0:T(8,128)} %reduce_sum.38), calls=%async_computation.5 | async-start | bytes 4194304 | tf_op jit(solution)/shard_map/all_to_all | solution.py:120
  413.6 8.9 %copy-start.8 = (bf16[8,64,1024]{2,1,0:T(8,128)(2,1)S(1)}, bf16[8,64,1024]{2,1,0:T(8,128)(2,1)}, u32[]{:S(2)}) copy-start(bf16[8,64,1024]{2,1,0:T(8,128)(2,1)} %copy-done.7) | copy-start | bytes 3145732
  432.1 2.3 copy-start.10
  434.4 1.5 copy-start.11
  435.9 1.5 copy-start.13
Sparse Core Ops, SparseCore 0:
  9.9 90.2 all-gather.1

commit v5 on v3

--- a/solution.py
+++ b/solution.py
@@ -79,7 +79,15 @@
     rows = lax.axis_size("seq")
     cols_each = tokens // rows
 
-    weight = lax.all_gather(out_weight, "dp", axis=0, tiled=True)
+    dp_size = lax.axis_size("dp")
+    dp_index = lax.axis_index("dp")
+    shifted = [out_weight] + [
+        lax.ppermute(out_weight, "dp", [(i, (i + k) % dp_size) for i in range(dp_size)])
+        for k in range(1, dp_size)
+    ]
+    weight = jnp.take(
+        jnp.stack(shifted), (dp_index - jnp.arange(dp_size)) % dp_size, axis=0
+    ).reshape(features, features)
 
     packed = jnp.stack([t[0, 0, :, half:] for t in (queries, keys, values)])
     shipped = lax.all_to_all(packed[None], "seq", split_axis=2, concat_axis=0, tiled=True)
@@ -98,15 +106,34 @@
     row_out, row_scores, row_total = row_forward(row_q, row_k, row_v, row_ok)
 
     flat_grad = out_grad[0, 0]
-    attention = jnp.concatenate([row_out.reshape(tokens, half), col_back[0]], axis=1)
-    partial = lax.dot_general(
-        attention, flat_grad, (((0,), (0,)), ((), ())), preferred_element_type=jnp.float32
+    half_dp = dp_size // 2
+    order = [
+        member
+        for d in range(half_dp)
+        for s in range(rows)
+        for member in (d * rows + s, (d + half_dp) * rows + s)
+    ]
+    row_attn = row_out.reshape(tokens, half)
+    row_partial = lax.dot_general(
+        row_attn, flat_grad, (((0,), (0,)), ((), ())), preferred_element_type=jnp.float32
     )
-    partial, weight = lax.optimization_barrier((partial, weight))
-    devices_all = lax.axis_size(("dp", "seq"))
-    wo_grad = lax.psum_scatter(partial, ("dp", "seq"), scatter_dimension=0, tiled=True) * (
-        1.0 / math.sqrt(tokens * devices_all)
+    row_piece = lax.psum_scatter(
+        row_partial, ("dp", "seq"), scatter_dimension=0, tiled=True, axis_index_groups=[order]
     )
+    attention = jnp.concatenate([row_attn, col_back[0]], axis=1)
+    col_partial = lax.dot_general(
+        col_back[0], flat_grad, (((0,), (0,)), ((), ())), preferred_element_type=jnp.float32
+    )
+    col_partial, weight = lax.optimization_barrier((col_partial, weight))
+    col_piece = lax.psum_scatter(
+        col_partial, ("dp", "seq"), scatter_dimension=0, tiled=True, axis_index_groups=[order]
+    )
+    is_x = dp_index < half_dp
+    swap = [(d, d + half_dp) for d in range(half_dp)] + [(d + half_dp, d) for d in range(half_dp)]
+    received = lax.ppermute(jnp.where(is_x, col_piece, row_piece), "dp", swap)
+    wo_grad = jnp.concatenate(
+        [jnp.where(is_x, row_piece, received), jnp.where(is_x, received, col_piece)], axis=0
+    ) * (1.0 / math.sqrt(tokens * dp_size * rows))
 
     attn_grad = lax.dot_general(
         flat_grad, weight, (((1,), (1,)), ((), ())), preferred_element_type=jnp.float32

time: 466 us -> 551 us (1.18)
  the two profiles are of different devices: /device:TPU:0 before, /device:TPU:12 now
where the time goes in v5:
time: 551 us; the launch traced here: 541 us
  waiting for transfers between devices  282 us (51%)
  local copies, waits for them, and re-layouts  102 us (19%)
  matrix products  65 us (12%)
  other arithmetic  49.5 us (9%)
  starting transfers between devices  27.6 us (5%)
  between operations  14.9 us (3%)
    ppermute x3, waiting for transfers between devices, on_device(): lax.ppermute(out_weight, 'dp', [(i, (i + k) % dp_size) for i in range(dp_...  134 us
    reduce_scatter x1, waiting for transfers between devices, on_device(): lax.psum_scatter(col_partial, ('dp', 'seq'), scatter_dimension=0, tiled=T...  70.7 us
    all_to_all x1, waiting for transfers between devices, on_device(): lax.all_to_all(jnp.stack([g.reshape(rows, cols_each, half) for g in col_g...  46.3 us
    all_to_all x1, waiting for transfers between devices, on_device(): lax.all_to_all(attn_grad[None, :, half:], 'seq', split_axis=1, concat_axi...  26.4 us
    unnamed x77, local copies, waits for them, and re-layouts  21.4 us
    unnamed x4, other arithmetic  17.5 us
    gather x3, local copies, waits for them, and re-layouts, on_device(): jnp.take(jnp.stack(shifted), (dp_index - jnp.arange(dp_size)) % dp_size,...  16.1 us
  transfers between devices with their start and end apart: 10, of which 7 were waited for; matrix products, arithmetic and copies ran while one was open for 33% of the time, Pallas kernels for 0%

profile of v5, /device:TPU:12, one launch (start us, length us, event | category | flops | bytes accessed | tf_op | source)
XLA Modules:
  0.0 541.2 jit_solution(5930569096140347842)
XLA Ops:
  8.3 2.8 fusion.53
  11.1 1.3 copy.144
  12.4 4.3 fusion.51
  16.7 1.5 copy.202
  18.2 2.7 copy.201
  20.9 2.9 select_reduce_fusion
  23.8 1.7 fusion
  25.6 1.4 copy-done.2
  27.0 2.7 fusion.20
  30.7 5.6 %fusion.15 = f32[1024,2048]{1,0:T(8,128)} fusion(bf16[512,1024]{0,1:T(8,128)(2,1)S(1)} %bitcast.156, bf16[1,1,512,2048]{3,2,1,0:T(8,128)(2,1)S(1)} %copy-done), kind=kOutput, calls=%fused_computation.33 | convolution fusion | flops 2147483648 | bytes 11534336 | tf_op jit(solution)/shard_map/dot_general | solution.py:117
  37.5 1.9 maximum_bitcast_fusion
  39.4 4.7 copy.146
  44.1 5.5 %all-to-all-start = ((bf16[1,3,512,1024]{3,1,0,2:T(4,128)(2,1)}), bf16[1,3,512,1024]{3,1,0,2:T(4,128)(2,1)}, u32[]{:S(2)}, u32[]{:S(2)}) async-start(bf16[1,3,512,1024]{3,1,0,2:T(4,128)(2,1)} %copy.146), calls=%async_computation | async-start | bytes 8388608 | tf_op jit(solution)/shard_map/all_to_all | solution.py:93
  49.6 1.5 collective-permute-start
  51.0 1.6 collective-permute-start.2
  53.3 46.7 %collective-permute-done = bf16[512,2048]{1,0:T(8,128)(2,1)} collective-permute-done((bf16[512,2048]{1,0:T(8,128)(2,1)}, bf16[512,2048]{1,0:T(8,128)(2,1)}, u32[]{:S(2)}, u32[]{:S(2)}) %collective-permute-start) | collective-permute-done | bytes 2097184 | tf_op jit(solution)/shard_map/ppermute | solution.py:85
  100.0 43.5 %collective-permute-done.2 = bf16[512,2048]{1,0:T(8,128)(2,1)} collective-permute-done((bf16[512,2048]{1,0:T(8,128)(2,1)}, bf16[512,2048]{1,0:T(8,128)(2,1)}, u32[]{:S(2)}, u32[]{:S(2)}) %collective-permute-start.2) | collective-permute-done | bytes 2097184 | tf_op jit(solution)/shard_map/ppermute | solution.py:85
  143.5 43.6 %collective-permute-done.1 = bf16[512,2048]{1,0:T(8,128)(2,1)} collective-permute-done((bf16[512,2048]{1,0:T(8,128)(2,1)}, bf16[512,2048]{1,0:T(8,128)(2,1)}, u32[]{:S(2)}, u32[]{:S(2)}) %collective-permute-start.1) | collective-permute-done | bytes 2097184 | tf_op jit(solution)/shard_map/ppermute | solution.py:85
  187.1 7.2 %pad_maximum_fusion = bf16[4,512,2048]{2,1,0:T(8,128)(2,1)} fusion(bf16[1,512,2048]{2,1,0:T(8,128)(2,1)} %bitcast.24, bf16[1,512,2048]{2,1,0:T(8,128)(2,1)} %bitcast.23, bf16[1,512,2048]{2,1,0:T(8,128)(2,1)} %bitcast.22, bf16[1,512,2048]{2,1,0:T(8,128)(2,1)} %bitcast.168), kind=kLoop, calls=%fused_computation.2 | loop fusion | flops 12582912 | bytes 16777216 | tf_op jit(solution)/shard_map/stack | solution.py:89
  194.3 3.4 copy.228
  200.9 2.6 fusion.34
  203.5 2.7 copy.150
  206.7 2.4 copy.152
  209.1 2.4 convolution_convert_fusion.3
  212.7 2.3 reshape.149
  215.0 5.3 all-to-all-start.1
  220.5 6.0 %fusion.48 = (bf16[4,512,1024]{2,1,0:T(8,128)(2,1)}, bf16[4,512,1024]{2,1,0:T(8,128)(2,1)}) fusion(bf16[4,512,2048]{2,1,0:T(8,128)(2,1)} %pad_maximum_fusion), kind=kLoop, calls=%fused_computation.103 | loop fusion | bytes 16777216 | tf_op jit(solution)/shard_map/jit(_take)/gather | solution.py:88
  226.6 5.0 gather_fusion
  231.6 5.1 gather_fusion.1
  236.6 8.2 %pad_maximum_fusion.1 = bf16[4,512,2048]{2,1,0:T(8,128)(2,1)} fusion(bf16[4,512,1024]{2,1,0:T(8,128)(2,1)} %gather_fusion.1, bf16[4,512,1024]{2,1,0:T(8,128)(2,1)} %gather_fusion), kind=kLoop, calls=%fused_computation.3 | loop fusion | flops 16777216 | bytes 16777216
  244.9 7.5 %bitcast_select_fusion = bf16[2048,2048]{1,0:T(8,128)(2,1)} fusion(bf16[4,512,2048]{2,1,0:T(8,128)(2,1)} %pad_maximum_fusion.1, pred[2048]{0:T(1024)(128)(4,1)S(1)} %bitcast.175), kind=kLoop, calls=%fused_computation.4 | loop fusion | flops 4194304 | bytes 16779264 | tf_op jit(solution)/shard_map/jit(_take)/select_n | solution.py:88
  252.4 6.9 %fusion.18 = f32[1024,2048]{1,0:T(8,128)} fusion(bf16[512,1024]{1,0:T(8,128)(2,1)} %bitcast.19, bf16[1,1,512,2048]{3,2,1,0:T(8,128)(2,1)S(1)} %copy-done), kind=kOutput, calls=%fused_computation.36 | convolution fusion | flops 2147483648 | bytes 11534336 | tf_op jit(solution)/shard_map/dot_general | solution.py:124
  259.3 8.3 %fusion.10 = bf16[512,2048]{0,1:T(8,128)(2,1)S(1)} fusion(bf16[2048,2048]{1,0:T(8,128)(2,1)} %bitcast_select_fusion, bf16[1,1,512,2048]{3,2,1,0:T(8,128)(2,1)S(1)} %copy-done), kind=kOutput, calls=%fused_computation.24 | convolution fusion | flops 4296015872 | bytes 12582912 | tf_op jit(solution)/shard_map/dot_general | solution.py:138
  269.9 5.2 copy.159
  275.7 7.8 %reduce.6 = bf16[512,1024]{1,0:T(8,128)(2,1)} reduce(bf16[512,1,1024]{2,1,0:T(2,128)(2,1)S(1)} %bitcast.155, bf16[]{:T(256)} %broadcast.143), dimensions={1}, to_apply=%bitcast.118.reduce_sub_computation | reduce | bytes 2097154
  283.4 2.6 reshape.178
  286.0 5.4 all-to-all-start.2
  292.1 26.4 %all-to-all-done.2 = bf16[8,2,32768]{2,1,0:T(2,128)(2,1)S(1)} async-done(((bf16[8,2,32768]{2,1,0:T(2,128)(2,1)}), bf16[8,2,32768]{2,1,0:T(2,128)(2,1)S(1)}, u32[]{:S(2)}, u32[]{:S(2)}) %all-to-all-start.2) | async-done | bytes 1048608 | tf_op jit(solution)/shard_map/all_to_all | solution.py:141
  318.5 3.6 reshape.179
  322.1 7.8 %bitcast_reduce_fusion = bf16[512,1024]{1,0:T(8,128)(2,1)S(1)} fusion(bf16[512,1,1024]{2,1,0:T(2,128)(2,1)} %reshape.179), kind=kLoop, calls=%fused_computation.109 | loop fusion | bytes 2097152 | tf_op jit(solution)/shard_map/all_to_all | solution.py:141
  330.1 2.6 fusion.29
  332.8 2.6 copy.162
  335.5 1.3 multiply_reduce_fusion
  337.8 3.0 copy.167
  340.8 2.2 fusion.26
  344.1 2.3 stack_reshape.10
  348.8 1.7 copy.170
  352.8 1.6 pad_maximum_fusion.2
  354.4 2.2 copy.172
  356.6 7.5 %all-to-all-start.3 = ((bf16[3,8,64,1024]{3,2,0,1:T(8,128)(2,1)}), bf16[3,8,64,1024]{3,2,0,1:T(8,128)(2,1)}, u32[]{:S(2)}, u32[]{:S(2)}) async-start(bf16[3,8,64,1024]{3,2,0,1:T(8,128)(2,1)} %copy.172), calls=%async_computation.3 | async-start | bytes 6291456 | tf_op jit(solution)/shard_map/all_to_all | solution.py:147
  365.4 1.6 fusion.14
  368.0 5.3 multiply_convert_fusion
  375.9 4.8 multiply_convert_fusion.1
  380.7 2.3 copy.175
  383.0 6.3 %fusion.21 = bf16[8,128,512]{2,1,0:T(8,128)(2,1)} fusion(bf16[512,8,128]{0,2,1:T(8,128)(2,1)S(1)} %bitcast.170, f32[8,512,512]{1,2,0:T(8,128)} %copy-done.2, f32[8,512]{1,0:T(8,128)S(1)} %log_add_fusion.1, pred[512,512]{0,1:T(8,128)(4,1)S(1)} %copy-done.18), kind=kOutput, calls=%fused_computation.46 | convolution fusion | flops 545783808 | bytes 10764288 | tf_op jit(solution)/shard_map/hij,ihd->jhd/dot_general | solution.py:41
  389.3 1.5 copy.177
  390.7 9.9 %fusion.9 = bf16[1,1,512,2048]{3,2,1,0:T(8,128)(2,1)} fusion(bf16[2048,2048]{1,0:T(8,128)(2,1)} %bitcast_select_fusion, bf16[512,1024]{1,0:T(8,128)(2,1)} %bitcast.19, bf16[512,1024]{1,0:T(8,128)(2,1)} %copy.154), kind=kOutput, calls=%fused_computation.23 | convolution fusion | flops 4300210176 | bytes 12582912 | tf_op jit(solution)/shard_map/dot_general | solution.py:166
  400.6 46.3 %all-to-all-done.3 = bf16[3,8,64,1024]{3,2,0,1:T(8,128)(2,1)} async-done(((bf16[3,8,64,1024]{3,2,0,1:T(8,128)(2,1)}), bf16[3,8,64,1024]{3,2,0,1:T(8,128)(2,1)}, u32[]{:S(2)}, u32[]{:S(2)}) %all-to-all-start.3) | async-done | bytes 3145760 | tf_op jit(solution)/shard_map/all_to_all | solution.py:147
  447.0 3.3 fusion.49
  450.3 1.5 maximum_bitcast_fusion.1
  451.8 1.5 maximum_bitcast_fusion.2
  453.3 70.7 %reduce-scatter.5.cloned.1.call-done = f32[32,2048]{1,0:T(8,128)} async-done(((f32[1024,2048]{1,0:T(8,128)}), f32[32,2048]{1,0:T(8,128)}) %reduce-scatter.5.cloned.1.call-update) | async-done | bytes 262160 | tf_op jit(solution)/shard_map/reduce_scatter | solution.py:128
  525.1 2.8 maximum_bitcast_fusion.3
  527.9 5.2 collective-permute-done.3
  (112 shorter events, 26.5 us)
Async XLA Ops:
  7.2 23.5 %copy-start = (bf16[1,1,512,2048]{3,2,1,0:T(8,128)(2,1)S(1)}, bf16[1,1,512,2048]{3,2,1,0:T(8,128)(2,1)}, u32[]{:S(2)}) copy-start(bf16[1,1,512,2048]{3,2,1,0:T(8,128)(2,1)} %param.10) | copy-start | bytes 6291460
  7.2 446.1 %reduce-scatter.3.cloned.1.call-start = ((), (), s32[]{:S(2)}) async-start(), calls=%async_computation.6 | async-start | bytes 8650752 | tf_op jit(solution)/shard_map/reduce_scatter | solution.py:120
  8.3 17.2 %copy-start.17 = (pred[512,512]{0,1:T(8,128)(4,1)}, pred[512,512]{0,1:T(8,128)(4,1)S(1)}, u32[]{:S(2)}) copy-start(pred[512,512]{0,1:T(8,128)(4,1)S(1)} %fusion.27) | copy-start | bytes 786436
  18.2 5.5 %copy-start.7 = (bf16[1,1,512,1024]{2,3,1,0:T(8,128)(2,1)}, bf16[1,1,512,1024]{2,3,1,0:T(8,128)(2,1)S(1)}, u32[]{:S(2)}) copy-start(bf16[1,1,512,1024]{2,3,1,0:T(8,128)(2,1)S(1)} %copy.202) | copy-start | bytes 3145732
  23.8 3.2 copy-start.2
  23.8 3.2 copy-start.22
  25.5 4.2 copy-start.27
  29.7 1.0 copy-start.9
  36.3 1.2 copy-start.15
  44.1 9.2 %copy-start.31 = (s32[8,8]{1,0:T(8,128)S(1)}, s32[8,8]{1,0:T(8,128)}, u32[]{:S(2)}) copy-start(s32[8,8]{1,0:T(8,128)} %param.13) | copy-start | bytes 772
  44.1 150.2 %all-to-all-start = ((bf16[1,3,512,1024]{3,1,0,2:T(4,128)(2,1)}), bf16[1,3,512,1024]{3,1,0,2:T(4,128)(2,1)}, u32[]{:S(2)}, u32[]{:S(2)}) async-start(bf16[1,3,512,1024]{3,1,0,2:T(4,128)(2,1)} %copy.146), calls=%async_computation | async-start | bytes 8388608 | tf_op jit(solution)/shard_map/all_to_all | solution.py:93
  49.6 50.4 %collective-permute-start = (bf16[512,2048]{1,0:T(8,128)(2,1)}, bf16[512,2048]{1,0:T(8,128)(2,1)}, u32[]{:S(2)}, u32[]{:S(2)}) collective-permute-start(bf16[512,2048]{1,0:T(8,128)(2,1)} %param.11), channel_id=1, source_target_pairs={{0,8},{8,16},{16,24},{24,0},{1,9},{9,17},{17,25},{25,1},{2,10},{10... | collective-permute-start | bytes 6291464 | tf_op jit(solution)/shard_map/ppermute | solution.py:85
  51.0 92.4 %collective-permute-start.2 = (bf16[512,2048]{1,0:T(8,128)(2,1)}, bf16[512,2048]{1,0:T(8,128)(2,1)}, u32[]{:S(2)}, u32[]{:S(2)}) collective-permute-start(bf16[512,2048]{1,0:T(8,128)(2,1)} %param.11), channel_id=1, source_target_pairs={{0,24},{8,0},{16,8},{24,16},{1,25},{9,1},{17,9},{25,17},{2,26},{10... | collective-permute-start | bytes 6291464 | tf_op jit(solution)/shard_map/ppermute | solution.py:85
  52.7 134.4 %collective-permute-start.1 = (bf16[512,2048]{1,0:T(8,128)(2,1)}, bf16[512,2048]{1,0:T(8,128)(2,1)}, u32[]{:S(2)}, u32[]{:S(2)}) collective-permute-start(bf16[512,2048]{1,0:T(8,128)(2,1)} %param.11), channel_id=1, source_target_pairs={{0,16},{8,24},{16,0},{24,8},{1,17},{9,25},{17,1},{25,9},{2,18},{10... | collective-permute-start | bytes 6291464 | tf_op jit(solution)/shard_map/ppermute | solution.py:85
  53.3 153.2 %copy-start.29 = (pred[8,8]{1,0:T(8,128)(4,1)}, pred[8,8]{1,0:T(8,128)(4,1)S(1)}, u32[]{:S(2)}) copy-start(pred[8,8]{1,0:T(8,128)(4,1)S(1)} %broadcast_compare_fusion) | copy-start | bytes 196
  199.6 1.0 copy-start.3
  199.9 1.0 copy-start.5
  215.0 37.4 %all-to-all-start.1 = ((bf16[8,64,1024]{2,1,0:T(8,128)(2,1)}), bf16[8,64,1024]{2,1,0:T(8,128)(2,1)}, u32[]{:S(2)}, u32[]{:S(2)}) async-start(bf16[8,64,1024]{2,1,0:T(8,128)(2,1)} %reshape.149), calls=%async_computation.1 | async-start | bytes 2097152 | tf_op jit(solution)/shard_map/all_to_all | solution.py:99
  220.2 303.8 %reduce-scatter.5.cloned.1.call-start = ((), (), s32[]{:S(2)}) async-start(), calls=%async_computation.7 | async-start | bytes 8650752 | tf_op jit(solution)/shard_map/reduce_scatter | solution.py:128
  267.6 1.3 copy-start.19
  286.0 32.5 %all-to-all-start.2 = ((bf16[8,2,32768]{2,1,0:T(2,128)(2,1)}), bf16[8,2,32768]{2,1,0:T(2,128)(2,1)S(1)}, u32[]{:S(2)}, u32[]{:S(2)}) async-start(bf16[8,2,32768]{2,1,0:T(2,128)(2,1)} %reshape.178), calls=%async_computation.2 | async-start | bytes 2097152 | tf_op jit(solution)/shard_map/all_to_all | solution.py:141
  292.1 38.1 %copy-start.6 = (bf16[64,8,8,128]{3,2,1,0:T(8,128)(2,1)S(1)}, bf16[64,8,8,128]{3,2,1,0:T(8,128)(2,1)}, u32[]{:S(2)}) copy-start(bf16[64,8,8,128]{3,2,1,0:T(8,128)(2,1)} %copy.204) | copy-start | bytes 3145732
  332.8 4.2 copy-start.26
  332.8 4.2 copy-start.30
  337.8 8.6 %copy-start.4 = (bf16[64,8,8,128]{3,2,1,0:T(8,128)(2,1)S(1)}, bf16[64,8,8,128]{3,2,1,0:T(8,128)(2,1)}, u32[]{:S(2)}) copy-start(bf16[64,8,8,128]{3,2,1,0:T(8,128)(2,1)} %copy-done.3) | copy-start | bytes 3145732
  348.8 4.0 copy-start.13
  351.4 1.4 copy-start.14
  356.6 7.5 %copy-start.10 = (bf16[8,512,128]{1,2,0:T(8,128)(2,1)S(1)}, bf16[8,512,128]{1,2,0:T(8,128)(2,1)}, u32[]{:S(2)}) copy-start(bf16[8,512,128]{1,2,0:T(8,128)(2,1)} %copy-done.9) | copy-start | bytes 3145732
  356.6 8.8 %copy-start.28 = (f32[8,512]{1,0:T(8,128)S(1)}, f32[8,512]{1,0:T(8,128)}, u32[]{:S(2)}) copy-start(f32[8,512]{1,0:T(8,128)} %copy-done.27) | copy-start | bytes 49156
  356.6 90.4 %all-to-all-start.3 = ((bf16[3,8,64,1024]{3,2,0,1:T(8,128)(2,1)}), bf16[3,8,64,1024]{3,2,0,1:T(8,128)(2,1)}, u32[]{:S(2)}, u32[]{:S(2)}) async-start(bf16[3,8,64,1024]{3,2,0,1:T(8,128)(2,1)} %copy.172), calls=%async_computation.3 | async-start | bytes 6291456 | tf_op jit(solution)/shard_map/all_to_all | solution.py:147
  364.1 3.9 copy-start.18
  364.1 3.9 copy-start.23
  367.0 1.0 copy-start.20
  368.0 5.3 copy-start.8
  373.3 2.1 copy-start.11
  373.3 2.6 copy-start.16
  375.9 7.0 %copy-start.21 = (bf16[512,1024]{0,1:T(8,128)(2,1)S(1)}, bf16[512,1024]{0,1:T(8,128)(2,1)}, u32[]{:S(2)}) copy-start(bf16[512,1024]{0,1:T(8,128)(2,1)} %copy-done.20) | copy-start | bytes 3145732
  447.0 4.8 copy-start.12
  451.8 82.2 %copy-start.1 = (bf16[1,1,512,2048]{3,2,1,0:T(8,128)(2,1)S(1)}, bf16[1,1,512,2048]{3,2,1,0:T(8,128)(2,1)}, u32[]{:S(2)}) copy-start(bf16[1,1,512,2048]{3,2,1,0:T(8,128)(2,1)} %param.10) | copy-start | bytes 6291460
  453.3 79.8 %copy-start.24 = (f32[32,2048]{1,0:T(8,128)S(1)}, f32[32,2048]{1,0:T(8,128)}, u32[]{:S(2)}) copy-start(f32[32,2048]{1,0:T(8,128)} %reduce-scatter.3.cloned.1.call-done) | copy-start | bytes 786436
  524.0 9.1 %copy-start.25 = (f32[32,2048]{1,0:T(8,128)S(1)}, f32[32,2048]{1,0:T(8,128)}, u32[]{:S(2)}) copy-start(f32[32,2048]{1,0:T(8,128)} %reduce-scatter.5.cloned.1.call-done) | copy-start | bytes 786436
  525.1 8.0 %collective-permute-start.3 = (f32[32,2048]{1,0:T(8,128)S(1)}, f32[32,2048]{1,0:T(8,128)S(1)}, u32[]{:S(2)}, u32[]{:S(2)}) collective-permute-start(f32[32,2048]{1,0:T(8,128)S(1)} %broadcast_select_fusion.2), channel_id=1, source_target_pairs={{0,16},{8,24},{16,0},{24,8},{1,17},{9,25},{17,1},{25,9},{2,18},{10... | collective-permute-start | bytes 786440 | tf_op jit(solution)/shard_map/ppermute | solution.py:133
Sparse Core Ops, SparseCore 0:
  36.5 274.7 reduce-scatter.2
  313.5 210.4 reduce-scatter.4

commit v6 on v3

--- a/solution.py
+++ b/solution.py
@@ -104,9 +104,9 @@
     )
     partial, weight = lax.optimization_barrier((partial, weight))
     devices_all = lax.axis_size(("dp", "seq"))
-    wo_grad = lax.psum_scatter(partial, ("dp", "seq"), scatter_dimension=0, tiled=True) * (
-        1.0 / math.sqrt(tokens * devices_all)
-    )
+    wo_grad = lax.psum_scatter(
+        partial.astype(jnp.bfloat16), ("dp", "seq"), scatter_dimension=0, tiled=True
+    ).astype(jnp.float32) * (1.0 / math.sqrt(tokens * devices_all))
 
     attn_grad = lax.dot_general(
         flat_grad, weight, (((1,), (1,)), ((), ())), preferred_element_type=jnp.float32

time: 466 us -> 403 us (0.86)
  waiting for transfers between devices: 253 us -> 193 us
    reduce_scatter x1, waiting for transfers between devices: 39.5 us -> 0.01 us  [on_device(): lax.psum_scatter(partial.astype(jnp.bfloat16), ('dp', 'seq'), scatter_dim...]
    all_to_all x1, waiting for transfers between devices: 75.9 us -> 57 us  [on_device(): lax.all_to_all(jnp.stack([g.reshape(rows, cols_each, half) for g in col_g...]
  transfers between devices with their start and end apart: 6 -> 6, of which waited for: 5 -> 4; matrix products, arithmetic and copies ran while one was open for 36% -> 41% of each run, Pallas kernels for 0% -> 0%
where the time goes in v6:
time: 403 us; the launch traced here: 397 us
  waiting for transfers between devices  193 us (48%)
  local copies, waits for them, and re-layouts  77 us (19%)
  matrix products  67.5 us (17%)
  other arithmetic  25 us (6%)
  starting transfers between devices  19.7 us (5%)
  between operations  14.8 us (4%)
    all_to_all x1, waiting for transfers between devices, on_device(): lax.all_to_all(packed[None], 'seq', split_axis=2, concat_axis=0, tiled=True)  82.1 us
    all_to_all x1, waiting for transfers between devices, on_device(): lax.all_to_all(jnp.stack([g.reshape(rows, cols_each, half) for g in col_g...  57 us
    all_to_all x1, waiting for transfers between devices, on_device(): lax.all_to_all(attn_grad[None, :, half:], 'seq', split_axis=1, concat_axi...  41.7 us
    unnamed x71, local copies, waits for them, and re-layouts  18.7 us
    all_to_all x1, waiting for transfers between devices, on_device(): lax.all_to_all(col_out.reshape(rows, cols_each, half), 'seq', split_axis=...  11.6 us
    dot_general x1, matrix products, on_device(): jnp.dot(attention, weight, preferred_element_type=jnp.float32)  9.58 us
    unnamed x3, other arithmetic  9.25 us
    dot_general x1, matrix products, on_device(): lax.dot_general(attention, flat_grad, (((0,), (0,)), ((), ())), preferred...  8.38 us
  transfers between devices with their start and end apart: 6, of which 4 were waited for; matrix products, arithmetic and copies ran while one was open for 41% of the time, Pallas kernels for 0%

profile of v6, /device:TPU:0, one launch (start us, length us, event | category | flops | bytes accessed | tf_op | source)
XLA Modules:
  0.0 397.1 jit_solution(11882130805455135017)
XLA Ops:
  7.2 0.7 all-gather.2.cloned.1.call-update
  7.9 1.9 fusion.45
  10.8 1.9 fusion.43
  13.0 4.7 %copy.146 = bf16[1,3,512,1024]{3,1,0,2:T(4,128)(2,1)} copy(bf16[1,3,512,1024]{3,2,1,0:T(8,128)(2,1)S(1)} %maximum_bitcast_fusion) | data formatting | bytes 6291456 | tf_op jit(solution)/shard_map/broadcast_in_dim | solution.py:85
  17.7 6.7 %all-to-all-start = ((bf16[1,3,512,1024]{3,1,0,2:T(4,128)(2,1)}), bf16[1,3,512,1024]{3,1,0,2:T(4,128)(2,1)}, u32[]{:S(2)}, u32[]{:S(2)}) async-start(bf16[1,3,512,1024]{3,1,0,2:T(4,128)(2,1)} %copy.146), calls=%async_computation | async-start | bytes 8388608 | tf_op jit(solution)/shard_map/all_to_all | solution.py:85
  24.7 1.3 copy.144
  26.1 1.5 copy.202
  27.6 2.7 copy.201
  30.3 6.1 %select_reduce_fusion = (f32[8,512]{1,0:T(8,128)S(1)}, f32[8,512,512]{1,2,0:T(8,128)}) fusion(pred[512,512]{0,1:T(8,128)(4,1)S(1)} %fusion.22, bf16[512,8,128]{0,2,1:T(8,128)(2,1)} %bitcast.150, bf16[512,8,128]{0,2,1:T(8,128)(2,1)S(1)} %bitcast.138), kind=kOutput, calls=%fused_computation.4 | convolution fusion | flops 543158272 | bytes 10764288 | tf_op jit(solution)/shard_map/ihd,jhd->hij/dot_general | solution.py:32
  36.4 82.1 %all-to-all-done = bf16[1,3,512,1024]{3,1,0,2:T(4,128)(2,1)} async-done(((bf16[1,3,512,1024]{3,1,0,2:T(4,128)(2,1)}), bf16[1,3,512,1024]{3,1,0,2:T(4,128)(2,1)}, u32[]{:S(2)}, u32[]{:S(2)}) %all-to-all-start) | async-done | bytes 3145760 | tf_op jit(solution)/shard_map/all_to_all | solution.py:85
  118.5 3.4 copy.227
  122.2 1.3 copy.204
  124.0 0.7 copy-done.2
  125.1 2.6 fusion.29
  127.7 2.7 copy.150
  130.8 2.4 copy.152
  133.3 2.4 convolution_convert_fusion.3
  135.7 1.1 copy.153
  136.8 2.3 reshape.92
  139.1 4.2 %all-to-all-start.1 = ((bf16[8,64,1024]{2,1,0:T(8,128)(2,1)}), bf16[8,64,1024]{2,1,0:T(8,128)(2,1)}, u32[]{:S(2)}, u32[]{:S(2)}) async-start(bf16[8,64,1024]{2,1,0:T(8,128)(2,1)} %reshape.92), calls=%async_computation.1 | async-start | bytes 2097152 | tf_op jit(solution)/shard_map/all_to_all | solution.py:91
  143.8 5.2 %fusion = f32[8,512]{1,0:T(8,128)S(1)} fusion(f32[8,512,512]{1,2,0:T(8,128)} %get-tuple-element.26, f32[8,512]{1,0:T(8,128)S(1)} %get-tuple-element.25, pred[512,512]{0,1:T(8,128)(4,1)} %copy-done.11), kind=kLoop, calls=%fused_computation.5 | loop fusion | flops 8384512 | bytes 8683520 | tf_op jit(solution)/shard_map/reduce_sum | solution.py:26
  149.1 7.0 %fusion.15 = bf16[8,512,128]{1,2,0:T(8,128)(2,1)} fusion(bf16[512,8,128]{0,2,1:T(8,128)(2,1)S(1)} %bitcast.154, f32[8,512,512]{1,2,0:T(8,128)} %get-tuple-element.26, f32[8,512]{1,0:T(8,128)S(1)} %fusion, f32[8,512]{1,0:T(8,128)S(1)} %get-tuple-element.25, pred[512,512]{0,1:T(8,128)(4,1)S(1)} %copy-done.12), kind=kOutput, calls=%fused_computation.36 | convolution fusion | flops 547880960 | bytes 10780672 | tf_op jit(solution)/shard_map/hij,jhd->ihd/dot_general | solution.py:34
  156.0 2.3 copy.154
  158.3 11.6 %all-to-all-done.1 = bf16[8,64,1024]{2,1,0:T(8,128)(2,1)} async-done(((bf16[8,64,1024]{2,1,0:T(8,128)(2,1)}), bf16[8,64,1024]{2,1,0:T(8,128)(2,1)}, u32[]{:S(2)}, u32[]{:S(2)}) %all-to-all-start.1) | async-done | bytes 1048608 | tf_op jit(solution)/shard_map/all_to_all | solution.py:91
  169.9 8.4 %fusion.13 = bf16[2048,2048]{1,0:T(8,128)(2,1)} fusion(bf16[1,1,512,2048]{3,2,1,0:T(8,128)(2,1)S(1)} %copy-done, bf16[512,1024]{1,0:T(8,128)(2,1)} %bitcast.19, bf16[512,1024]{1,0:T(8,128)(2,1)} %copy.154), kind=kOutput, calls=%fused_computation.27 | convolution fusion | flops 4299161600 | bytes 12582912 | tf_op jit(solution)/shard_map/dot_general | solution.py:102
  178.3 8.2 %fusion.10 = bf16[512,2048]{0,1:T(8,128)(2,1)S(1)} fusion(bf16[2048,2048]{1,0:T(8,128)(2,1)} %all-gather.2.cloned.1.call-done, bf16[1,1,512,2048]{3,2,1,0:T(8,128)(2,1)S(1)} %copy-done), kind=kOutput, calls=%fused_computation.19 | convolution fusion | flops 4296015872 | bytes 12582912 | tf_op jit(solution)/shard_map/dot_general | solution.py:111
  186.6 1.3 copy-done.14
  187.9 1.0 slice_bitcast_fusion
  188.9 4.7 %copy.159 = bf16[1,512,1024]{2,0,1:T(2,128)(2,1)S(1)} copy(bf16[1,512,1024]{1,2,0:T(8,128)(2,1)} %slice_bitcast_fusion) | data formatting | bytes 2097152 | tf_op jit(solution)/shard_map/broadcast_in_dim | solution.py:115
  194.3 7.8 %reduce.6 = bf16[512,1024]{1,0:T(8,128)(2,1)} reduce(bf16[512,1,1024]{2,1,0:T(2,128)(2,1)S(1)} %bitcast.140, bf16[]{:T(256)} %broadcast.37), dimensions={1}, to_apply=%bitcast.105.reduce_sub_computation | reduce | bytes 2097154
  202.0 2.6 reshape.105
  204.7 3.6 all-to-all-start.2
  208.8 41.7 %all-to-all-done.2 = bf16[8,2,32768]{2,1,0:T(2,128)(2,1)S(1)} async-done(((bf16[8,2,32768]{2,1,0:T(2,128)(2,1)}), bf16[8,2,32768]{2,1,0:T(2,128)(2,1)S(1)}, u32[]{:S(2)}, u32[]{:S(2)}) %all-to-all-start.2) | async-done | bytes 1048608 | tf_op jit(solution)/shard_map/all_to_all | solution.py:114
  250.5 3.6 reshape.106
  254.1 7.9 %bitcast_reduce_fusion = bf16[512,1024]{1,0:T(8,128)(2,1)S(1)} fusion(bf16[512,1,1024]{2,1,0:T(2,128)(2,1)} %reshape.106), kind=kLoop, calls=%fused_computation.83 | loop fusion | bytes 2097152 | tf_op jit(solution)/shard_map/all_to_all | solution.py:114
  262.3 2.6 fusion.24
  264.9 2.6 copy.162
  267.7 1.3 multiply_reduce_fusion
  269.3 1.9 copy.167
  271.2 2.3 fusion.21
  273.5 1.1 copy.168
  274.6 2.3 stack_reshape.10
  276.9 1.0 fusion.20
  278.0 1.3 stack_reshape.9
  279.3 1.7 copy.170
  281.1 0.9 fusion.19
  282.1 1.3 stack_reshape.11
  283.3 2.2 pad_maximum_fusion
  285.6 2.1 copy.172
  287.7 4.8 %all-to-all-start.3 = ((bf16[3,8,64,1024]{3,2,0,1:T(8,128)(2,1)}), bf16[3,8,64,1024]{3,2,0,1:T(8,128)(2,1)}, u32[]{:S(2)}, u32[]{:S(2)}) async-start(bf16[3,8,64,1024]{3,2,0,1:T(8,128)(2,1)} %copy.172), calls=%async_computation.3 | async-start | bytes 6291456 | tf_op jit(solution)/shard_map/all_to_all | solution.py:120
  293.8 5.3 %multiply_convert_fusion = bf16[8,512,512]{1,2,0:T(8,128)(2,1)S(1)} fusion(f32[8,512,512]{1,2,0:T(8,128)} %get-tuple-element.26, f32[8,512]{1,0:T(8,128)S(1)} %get-tuple-element.9, f32[8,512]{1,0:T(8,128)S(1)} %log_add_fusion.1, pred[512,512]{0,1:T(8,128)(4,1)S(1)} %copy-done.13, bf16[512,8,128]{0,2,1:T(8,128)(2,1)S(1)} %bitcast.152, ...), kind=kOutput, calls=%fused_computation | convolution fusion | flops 549453824 | bytes 14974976 | tf_op jit(solution)/shard_map/ihd,jhd->hij/dot_general | solution.py:44
  299.1 0.7 multiply_convert_fusion.4
  299.9 1.3 copy-done.9
  301.7 4.1 %multiply_convert_fusion.1 = bf16[8,512,128]{1,2,0:T(8,128)(2,1)S(1)} fusion(bf16[8,512,512]{1,2,0:T(8,128)(2,1)} %copy-done.9, bf16[512,8,128]{0,2,1:T(8,128)(2,1)} %bitcast.151), kind=kOutput, calls=%fused_computation.30 | convolution fusion | flops 537919488 | bytes 6291456 | tf_op jit(solution)/shard_map/hij,ihd->jhd/dot_general | solution.py:47
  305.8 1.3 copy.175
  307.1 6.4 %fusion.16 = bf16[8,128,512]{2,1,0:T(8,128)(2,1)} fusion(bf16[512,8,128]{0,2,1:T(8,128)(2,1)S(1)} %bitcast.153, f32[8,512,512]{1,2,0:T(8,128)} %get-tuple-element.26, f32[8,512]{1,0:T(8,128)S(1)} %log_add_fusion.1, pred[512,512]{0,1:T(8,128)(4,1)S(1)} %copy-done.13), kind=kOutput, calls=%fused_computation.37 | convolution fusion | flops 545783808 | bytes 10764288 | tf_op jit(solution)/shard_map/hij,ihd->jhd/dot_general | solution.py:41
  313.5 1.5 copy.177
  315.0 9.6 %fusion.9 = bf16[1,1,512,2048]{3,2,1,0:T(8,128)(2,1)} fusion(bf16[2048,2048]{1,0:T(8,128)(2,1)} %all-gather.2.cloned.1.call-done, bf16[512,1024]{1,0:T(8,128)(2,1)} %bitcast.19, bf16[512,1024]{1,0:T(8,128)(2,1)S(1)} %copy-done.22), kind=kOutput, calls=%fused_computation.18 | convolution fusion | flops 4300210176 | bytes 12582912 | tf_op jit(solution)/shard_map/dot_general | solution.py:139
  324.5 57.0 %all-to-all-done.3 = bf16[3,8,64,1024]{3,2,0,1:T(8,128)(2,1)} async-done(((bf16[3,8,64,1024]{3,2,0,1:T(8,128)(2,1)}), bf16[3,8,64,1024]{3,2,0,1:T(8,128)(2,1)}, u32[]{:S(2)}, u32[]{:S(2)}) %all-to-all-start.3) | async-done | bytes 3145760 | tf_op jit(solution)/shard_map/all_to_all | solution.py:120
  381.5 2.2 fusion.41
  383.7 1.5 maximum_bitcast_fusion.3
  385.2 1.5 maximum_bitcast_fusion.2
  386.7 1.5 maximum_bitcast_fusion.1
  388.3 1.8 convert_multiply_fusion.1
  (86 shorter events, 7.8 us)
Async XLA Ops:
  7.2 162.8 %copy-start = (bf16[1,1,512,2048]{3,2,1,0:T(8,128)(2,1)S(1)}, bf16[1,1,512,2048]{3,2,1,0:T(8,128)(2,1)}, u32[]{:S(2)}) copy-start(bf16[1,1,512,2048]{3,2,1,0:T(8,128)(2,1)} %param.10) | copy-start | bytes 6291460
  7.2 171.1 %all-gather.2.cloned.1.call-start = ((), (), s32[]{:S(2)}) async-start(), calls=%async_computation.5 | async-start | bytes 10485760 | tf_op jit(solution)/shard_map/all_gather | solution.py:82
  7.9 2.2 copy-start.16
  7.9 2.8 copy-start.17
  17.7 6.7 %copy-start.29 = (s32[4,4]{1,0:T(4,128)S(1)}, s32[4,4]{1,0:T(4,128)}, u32[]{:S(2)}) copy-start(s32[4,4]{1,0:T(4,128)} %param.12) | copy-start | bytes 196
  17.7 100.7 %all-to-all-start = ((bf16[1,3,512,1024]{3,1,0,2:T(4,128)(2,1)}), bf16[1,3,512,1024]{3,1,0,2:T(4,128)(2,1)}, u32[]{:S(2)}, u32[]{:S(2)}) async-start(bf16[1,3,512,1024]{3,1,0,2:T(4,128)(2,1)} %copy.146), calls=%async_computation | async-start | bytes 8388608 | tf_op jit(solution)/shard_map/all_to_all | solution.py:85
  24.7 5.6 %copy-start.11 = (pred[512,512]{0,1:T(8,128)(4,1)}, pred[512,512]{0,1:T(8,128)(4,1)S(1)}, u32[]{:S(2)}) copy-start(pred[512,512]{0,1:T(8,128)(4,1)S(1)} %fusion.22) | copy-start | bytes 786436
  24.7 5.5 %copy-start.28 = (s32[8,8]{1,0:T(8,128)S(1)}, s32[8,8]{1,0:T(8,128)}, u32[]{:S(2)}) copy-start(s32[8,8]{1,0:T(8,128)} %param.13) | copy-start | bytes 772
  27.6 8.8 %copy-start.6 = (bf16[1,1,512,1024]{2,3,1,0:T(8,128)(2,1)}, bf16[1,1,512,1024]{2,3,1,0:T(8,128)(2,1)S(1)}, u32[]{:S(2)}) copy-start(bf16[1,1,512,1024]{2,3,1,0:T(8,128)(2,1)S(1)} %copy.202) | copy-start | bytes 3145732
  30.3 100.5 %copy-start.26 = (pred[8,8]{1,0:T(8,128)(4,1)}, pred[8,8]{1,0:T(8,128)(4,1)S(1)}, u32[]{:S(2)}) copy-start(pred[8,8]{1,0:T(8,128)(4,1)S(1)} %broadcast_compare_fusion) | copy-start | bytes 196
  123.7 1.0 copy-start.2
  124.0 1.1 copy-start.4
  139.1 30.8 %all-to-all-start.1 = ((bf16[8,64,1024]{2,1,0:T(8,128)(2,1)}), bf16[8,64,1024]{2,1,0:T(8,128)(2,1)}, u32[]{:S(2)}, u32[]{:S(2)}) async-start(bf16[8,64,1024]{2,1,0:T(8,128)(2,1)} %reshape.92), calls=%async_computation.1 | async-start | bytes 2097152 | tf_op jit(solution)/shard_map/all_to_all | solution.py:91
  143.3 244.9 %reduce-scatter.2.cloned.1.call-start = ((), (), s32[]{:S(2)}) async-start(), calls=%async_computation.6 | async-start | bytes 8650752 | tf_op jit(solution)/shard_map/reduce_scatter | solution.py:107
  143.8 5.2 %copy-start.12 = (pred[512,512]{0,1:T(8,128)(4,1)S(1)}, pred[512,512]{0,1:T(8,128)(4,1)}, u32[]{:S(2)}) copy-start(pred[512,512]{0,1:T(8,128)(4,1)} %copy-done.11) | copy-start | bytes 786436
  143.8 5.2 %copy-start.20 = (bf16[1,1,512,1024]{2,3,1,0:T(8,128)(2,1)S(1)}, bf16[1,1,512,1024]{2,3,1,0:T(8,128)(2,1)}, u32[]{:S(2)}) copy-start(bf16[1,1,512,1024]{2,3,1,0:T(8,128)(2,1)} %copy.144) | copy-start | bytes 3145732
  149.0 7.0 %copy-start.24 = (f32[8,512]{1,0:T(8,128)}, f32[8,512]{1,0:T(8,128)S(1)}, u32[]{:S(2)}) copy-start(f32[8,512]{1,0:T(8,128)S(1)} %fusion) | copy-start | bytes 49156
  186.6 1.3 copy-start.14
  204.7 45.9 %all-to-all-start.2 = ((bf16[8,2,32768]{2,1,0:T(2,128)(2,1)}), bf16[8,2,32768]{2,1,0:T(2,128)(2,1)S(1)}, u32[]{:S(2)}, u32[]{:S(2)}) async-start(bf16[8,2,32768]{2,1,0:T(2,128)(2,1)} %reshape.105), calls=%async_computation.2 | async-start | bytes 2097152 | tf_op jit(solution)/shard_map/all_to_all | solution.py:114
  254.1 8.1 %copy-start.5 = (bf16[64,8,8,128]{3,2,1,0:T(8,128)(2,1)S(1)}, bf16[64,8,8,128]{3,2,1,0:T(8,128)(2,1)}, u32[]{:S(2)}) copy-start(bf16[64,8,8,128]{3,2,1,0:T(8,128)(2,1)} %copy.204) | copy-start | bytes 3145732
  267.5 1.6 copy-start.23
  267.5 1.6 copy-start.27
  271.2 5.7 %copy-start.3 = (bf16[64,8,8,128]{3,2,1,0:T(8,128)(2,1)S(1)}, bf16[64,8,8,128]{3,2,1,0:T(8,128)(2,1)}, u32[]{:S(2)}) copy-start(bf16[64,8,8,128]{3,2,1,0:T(8,128)(2,1)} %copy-done.2) | copy-start | bytes 3145732
  287.7 4.8 %copy-start.25 = (f32[8,512]{1,0:T(8,128)S(1)}, f32[8,512]{1,0:T(8,128)}, u32[]{:S(2)}) copy-start(f32[8,512]{1,0:T(8,128)} %copy-done.24) | copy-start | bytes 49156
  287.7 4.8 %copy-start.8 = (bf16[8,512,128]{1,2,0:T(8,128)(2,1)S(1)}, bf16[8,512,128]{1,2,0:T(8,128)(2,1)}, u32[]{:S(2)}) copy-start(bf16[8,512,128]{1,2,0:T(8,128)(2,1)} %fusion.15) | copy-start | bytes 3145732
  287.7 4.8 %copy-start.15 = (bf16[512,2048]{0,1:T(8,128)(2,1)S(1)}, bf16[512,2048]{0,1:T(8,128)(2,1)}, u32[]{:S(2)}) copy-start(bf16[512,2048]{0,1:T(8,128)(2,1)} %copy-done.14) | copy-start | bytes 6291460
  287.7 93.9 %all-to-all-start.3 = ((bf16[3,8,64,1024]{3,2,0,1:T(8,128)(2,1)}), bf16[3,8,64,1024]{3,2,0,1:T(8,128)(2,1)}, u32[]{:S(2)}, u32[]{:S(2)}) async-start(bf16[3,8,64,1024]{3,2,0,1:T(8,128)(2,1)} %copy.172), calls=%async_computation.3 | async-start | bytes 6291456 | tf_op jit(solution)/shard_map/all_to_all | solution.py:120
  292.4 1.0 copy-start.13
  292.4 1.3 copy-start.21
  292.8 6.3 %copy-start.18 = (bf16[512,1024]{0,1:T(8,128)(2,1)}, bf16[512,1024]{0,1:T(8,128)(2,1)S(1)}, u32[]{:S(2)}) copy-start(bf16[512,1024]{0,1:T(8,128)(2,1)S(1)} %get-tuple-element.10) | copy-start | bytes 3145732
  293.8 5.4 %copy-start.7 = (bf16[1,1,512,1024]{2,3,1,0:T(8,128)(2,1)S(1)}, bf16[1,1,512,1024]{2,3,1,0:T(8,128)(2,1)}, u32[]{:S(2)}) copy-start(bf16[1,1,512,1024]{2,3,1,0:T(8,128)(2,1)} %copy-done.6) | copy-start | bytes 3145732
  299.1 2.0 copy-start.9
  301.7 5.4 %copy-start.19 = (bf16[512,1024]{0,1:T(8,128)(2,1)S(1)}, bf16[512,1024]{0,1:T(8,128)(2,1)}, u32[]{:S(2)}) copy-start(bf16[512,1024]{0,1:T(8,128)(2,1)} %copy-done.18) | copy-start | bytes 3145732
  307.1 7.9 %copy-start.22 = (bf16[512,1024]{1,0:T(8,128)(2,1)S(1)}, bf16[512,1024]{1,0:T(8,128)(2,1)}, u32[]{:S(2)}) copy-start(bf16[512,1024]{1,0:T(8,128)(2,1)} %copy.154) | copy-start | bytes 3145732
  383.7 1.5 copy-start.10
  385.2 4.8 %copy-start.1 = (bf16[1,1,512,2048]{3,2,1,0:T(8,128)(2,1)S(1)}, bf16[1,1,512,2048]{3,2,1,0:T(8,128)(2,1)}, u32[]{:S(2)}) copy-start(bf16[1,1,512,2048]{3,2,1,0:T(8,128)(2,1)} %param.10) | copy-start | bytes 6291460
Sparse Core Ops, SparseCore 0:
  9.9 90.2 all-gather.1
  178.5 178.6 reduce-scatter.1

commit v7 on v6

--- a/solution.py
+++ b/solution.py
@@ -102,17 +102,17 @@
     partial = lax.dot_general(
         attention, flat_grad, (((0,), (0,)), ((), ())), preferred_element_type=jnp.float32
     )
-    partial, weight = lax.optimization_barrier((partial, weight))
+
+    attn_grad = lax.dot_general(
+        flat_grad, weight, (((1,), (1,)), ((), ())), preferred_element_type=jnp.float32
+    ).astype(jnp.bfloat16)
+    partial, grad_col_part = lax.optimization_barrier((partial, attn_grad[None, :, half:]))
     devices_all = lax.axis_size(("dp", "seq"))
     wo_grad = lax.psum_scatter(
         partial.astype(jnp.bfloat16), ("dp", "seq"), scatter_dimension=0, tiled=True
     ).astype(jnp.float32) * (1.0 / math.sqrt(tokens * devices_all))
-
-    attn_grad = lax.dot_general(
-        flat_grad, weight, (((1,), (1,)), ((), ())), preferred_element_type=jnp.float32
-    ).astype(jnp.bfloat16)
     grad_cols = lax.all_to_all(
-        attn_grad[None, :, half:], "seq", split_axis=1, concat_axis=0, tiled=True
+        grad_col_part, "seq", split_axis=1, concat_axis=0, tiled=True
     ).reshape(rows, cols_each, heads_half, DH)
     col_grads = column_backward(
         col_q, col_k, col_v, col_out, grad_cols, col_scores, col_total, col_ok

time: 403 us -> 401 us (level)
  waiting for transfers between devices: 193 us -> 186 us
  local copies, waits for them, and re-layouts: 77 us -> 82.5 us
    all_to_all x1, waiting for transfers between devices: 11.6 us -> 1.61 us  [on_device(): lax.all_to_all(col_out.reshape(rows, cols_each, half), 'seq', split_axis=...]
    broadcast_in_dim x2 -> x0, local copies, waits for them, and re-layouts: 5.79 us -> none  [on_device(): attn_grad[None, :, half:]]
    unnamed x71 -> x68, local copies, waits for them, and re-layouts: 18.7 us -> 24 us
    all_to_all x1, waiting for transfers between devices: 57 us -> 61.3 us  [on_device(): lax.all_to_all(jnp.stack([g.reshape(rows, cols_each, half) for g in col_g...]
    unnamed x3 -> x4, other arithmetic: 9.25 us -> 11.4 us
  transfers between devices with their start and end apart: 6 -> 6, of which waited for: 4 -> 4; matrix products, arithmetic and copies ran while one was open for 41% -> 40% of each run, Pallas kernels for 0% -> 0%
where the time goes in v7:
time: 401 us; the launch traced here: 395 us
  waiting for transfers between devices  186 us (46%)
  local copies, waits for them, and re-layouts  82.5 us (21%)
  matrix products  67.5 us (17%)
  other arithmetic  25.3 us (6%)
  starting transfers between devices  19.4 us (5%)
  between operations  14.8 us (4%)
    all_to_all x1, waiting for transfers between devices, on_device(): lax.all_to_all(packed[None], 'seq', split_axis=2, concat_axis=0, tiled=True)  80.3 us
    all_to_all x1, waiting for transfers between devices, on_device(): lax.all_to_all(jnp.stack([g.reshape(rows, cols_each, half) for g in col_g...  61.3 us
    all_to_all x1, waiting for transfers between devices, on_device(): lax.all_to_all(grad_col_part, 'seq', split_axis=1, concat_axis=0, tiled=T...  42 us
    unnamed x68, local copies, waits for them, and re-layouts  24 us
    unnamed x4, other arithmetic  11.4 us
    dot_general x1, matrix products, on_device(): jnp.dot(attention, weight, preferred_element_type=jnp.float32)  9.58 us
    dot_general x1, matrix products, on_device(): lax.dot_general(attention, flat_grad, (((0,), (0,)), ((), ())), preferred...  8.75 us
    dot_general x1, matrix products, row_forward(): jnp.einsum('hij,jhd->ihd', probs, v, preferred_element_type=jnp.float32)  8.59 us
  transfers between devices with their start and end apart: 6, of which 4 were waited for; matrix products, arithmetic and copies ran while one was open for 40% of the time, Pallas kernels for 0%

profile of v7, /device:TPU:0, one launch (start us, length us, event | category | flops | bytes accessed | tf_op | source)
XLA Modules:
  0.0 395.3 jit_solution(15468860958145844283)
XLA Ops:
  7.9 1.9 fusion.43
  10.8 1.9 fusion.41
  13.0 4.7 %copy.147 = bf16[1,3,512,1024]{3,1,0,2:T(4,128)(2,1)} copy(bf16[1,3,512,1024]{3,2,1,0:T(8,128)(2,1)S(1)} %maximum_bitcast_fusion) | data formatting | bytes 6291456 | tf_op jit(solution)/shard_map/broadcast_in_dim | solution.py:85
  17.7 6.7 %all-to-all-start = ((bf16[1,3,512,1024]{3,1,0,2:T(4,128)(2,1)}), bf16[1,3,512,1024]{3,1,0,2:T(4,128)(2,1)}, u32[]{:S(2)}, u32[]{:S(2)}) async-start(bf16[1,3,512,1024]{3,1,0,2:T(4,128)(2,1)} %copy.147), calls=%async_computation | async-start | bytes 8388608 | tf_op jit(solution)/shard_map/all_to_all | solution.py:85
  24.7 1.4 copy.145
  26.1 1.5 copy.202
  27.6 2.7 copy.201
  30.3 2.9 select_reduce_fusion
  33.2 3.2 copy-done.2
  36.4 1.7 fusion
  38.1 80.3 %all-to-all-done = bf16[1,3,512,1024]{3,1,0,2:T(4,128)(2,1)} async-done(((bf16[1,3,512,1024]{3,1,0,2:T(4,128)(2,1)}), bf16[1,3,512,1024]{3,1,0,2:T(4,128)(2,1)}, u32[]{:S(2)}, u32[]{:S(2)}) %all-to-all-start) | async-done | bytes 3145760 | tf_op jit(solution)/shard_map/all_to_all | solution.py:85
  118.5 3.4 copy.229
  124.2 2.6 fusion.27
  126.9 2.7 copy.151
  130.7 3.3 copy.153
  134.0 2.1 convolution_convert_fusion.3
  136.0 1.0 copy-done.3
  137.2 1.3 reshape.92
  138.4 4.5 %all-to-all-start.1 = ((bf16[8,64,1024]{2,1,0:T(8,128)(2,1)}), bf16[8,64,1024]{2,1,0:T(8,128)(2,1)}, u32[]{:S(2)}, u32[]{:S(2)}) async-start(bf16[8,64,1024]{2,1,0:T(8,128)(2,1)} %reshape.92), calls=%async_computation.1 | async-start | bytes 2097152 | tf_op jit(solution)/shard_map/all_to_all | solution.py:91
  143.0 8.1 %convolution_convert_fusion = bf16[512,2048]{1,0:T(8,128)(2,1)S(1)} fusion(bf16[2048,2048]{1,0:T(8,128)(2,1)} %all-gather.2.cloned.1.call-done, bf16[1,1,512,2048]{3,2,1,0:T(8,128)(2,1)S(1)} %copy-done), kind=kOutput, calls=%fused_computation.16 | convolution fusion | flops 4296015872 | bytes 12582912 | tf_op jit(solution)/shard_map/dot_general | solution.py:106
  151.1 1.2 slice_bitcast_fusion.1
  152.6 1.5 bitcast_convert_fusion.1
  154.1 2.9 copy.190
  157.0 8.6 %multiply_reduce_fusion.1 = (f32[8,512]{1,0:T(8,128)}, bf16[8,512,128]{1,2,0:T(8,128)(2,1)}) fusion(f32[8,512,128]{1,2,0:T(8,128)} %copy.190, bf16[512,8,128]{0,2,1:T(8,128)(2,1)} %bitcast.154, f32[8,512,512]{1,2,0:T(8,128)} %copy-done.2, f32[8,512]{1,0:T(8,128)S(1)} %fusion, f32[8,512]{1,0:T(8,128)S(1)} %get-tuple-element.25, pred[512,512]{0,1:T(8,128)(4,1)} %copy-done.14), kind=kOutput, calls=%fused_computation.27 | convolution fusion | flops 549449728 | bytes 12894208 | tf_op jit(solution)/shard_map/hij,jhd->ihd/dot_general | solution.py:34
  165.6 2.3 copy.155
  167.9 1.6 all-to-all-done.1
  169.5 8.8 %fusion.10 = bf16[2048,2048]{1,0:T(8,128)(2,1)} fusion(bf16[1,1,512,2048]{3,2,1,0:T(8,128)(2,1)S(1)} %copy-done, bf16[512,1024]{1,0:T(8,128)(2,1)} %bitcast.19, bf16[512,1024]{1,0:T(8,128)(2,1)} %copy.155), kind=kOutput, calls=%fused_computation.23 | convolution fusion | flops 4299161600 | bytes 12582912 | tf_op jit(solution)/shard_map/dot_general | solution.py:102
  178.3 2.8 copy.231
  181.6 7.8 %reduce.6 = bf16[512,1024]{1,0:T(8,128)(2,1)} reduce(bf16[512,1,1024]{2,1,0:T(2,128)(2,1)S(1)} %bitcast.143, bf16[]{:T(256)} %broadcast.37), dimensions={1}, to_apply=%bitcast.127.reduce_sub_computation | reduce | bytes 2097154
  189.4 2.6 reshape.105
  192.0 3.6 all-to-all-start.2
  196.2 42.0 %all-to-all-done.2 = bf16[8,2,32768]{2,1,0:T(2,128)(2,1)S(1)} async-done(((bf16[8,2,32768]{2,1,0:T(2,128)(2,1)}), bf16[8,2,32768]{2,1,0:T(2,128)(2,1)S(1)}, u32[]{:S(2)}, u32[]{:S(2)}) %all-to-all-start.2) | async-done | bytes 1048608 | tf_op jit(solution)/shard_map/all_to_all | solution.py:114
  238.2 3.6 reshape.106
  241.8 7.8 %bitcast_reduce_fusion = bf16[512,1024]{1,0:T(8,128)(2,1)S(1)} fusion(bf16[512,1,1024]{2,1,0:T(2,128)(2,1)} %reshape.106), kind=kLoop, calls=%fused_computation.83 | loop fusion | bytes 2097152 | tf_op jit(solution)/shard_map/all_to_all | solution.py:114
  249.9 2.6 fusion.22
  252.5 3.4 copy.163
  256.1 2.0 multiply_reduce_fusion
  258.1 1.1 copy.198
  259.2 1.8 multiply_convert_fusion.5
  261.0 2.9 copy.168
  263.9 2.2 fusion.19
  266.1 1.1 copy.169
  267.2 2.3 stack_reshape.10
  269.5 2.2 fusion.18
  271.8 1.3 stack_reshape.9
  273.1 1.7 copy.171
  275.9 1.3 stack_reshape.11
  277.1 1.9 pad_maximum_fusion
  279.0 2.1 copy.173
  281.1 4.6 %all-to-all-start.3 = ((bf16[3,8,64,1024]{3,2,0,1:T(8,128)(2,1)}), bf16[3,8,64,1024]{3,2,0,1:T(8,128)(2,1)}, u32[]{:S(2)}, u32[]{:S(2)}) async-start(bf16[3,8,64,1024]{3,2,0,1:T(8,128)(2,1)} %copy.173), calls=%async_computation.3 | async-start | bytes 6291456 | tf_op jit(solution)/shard_map/all_to_all | solution.py:120
  285.8 1.5 copy.177
  287.3 5.8 %multiply_convert_fusion = bf16[8,512,512]{1,2,0:T(8,128)(2,1)S(1)} fusion(f32[8,512,512]{1,2,0:T(8,128)} %copy-done.2, f32[8,512]{1,0:T(8,128)S(1)} %copy-done.26, f32[8,512]{1,0:T(8,128)S(1)} %log_add_fusion.1, pred[512,512]{0,1:T(8,128)(4,1)S(1)} %copy-done.15, bf16[512,8,128]{0,2,1:T(8,128)(2,1)} %copy.177, bf16[512,8,128]{0,2,1:T(8,128)(2,1)S(1)} %bitcast.155), kind=kOutput, calls=%fused_computation | convolution fusion | flops 549453824 | bytes 14974976 | tf_op jit(solution)/shard_map/ihd,jhd->hij/dot_general | solution.py:44
  293.8 1.2 copy-done.11
  295.6 4.1 %multiply_convert_fusion.1 = bf16[8,512,128]{1,2,0:T(8,128)(2,1)S(1)} fusion(bf16[8,512,512]{1,2,0:T(8,128)(2,1)} %copy-done.11, bf16[512,8,128]{0,2,1:T(8,128)(2,1)} %bitcast.153), kind=kOutput, calls=%fused_computation.28 | convolution fusion | flops 537919488 | bytes 6291456 | tf_op jit(solution)/shard_map/hij,ihd->jhd/dot_general | solution.py:47
  299.7 1.3 copy.176
  301.0 6.4 %fusion.14 = bf16[8,128,512]{2,1,0:T(8,128)(2,1)} fusion(bf16[512,8,128]{0,2,1:T(8,128)(2,1)S(1)} %copy-done.20, f32[8,512,512]{1,2,0:T(8,128)} %copy-done.2, f32[8,512]{1,0:T(8,128)S(1)} %log_add_fusion.1, pred[512,512]{0,1:T(8,128)(4,1)S(1)} %copy-done.15), kind=kOutput, calls=%fused_computation.35 | convolution fusion | flops 545783808 | bytes 10764288 | tf_op jit(solution)/shard_map/hij,ihd->jhd/dot_general | solution.py:41
  307.4 1.5 copy.179
  308.9 9.6 %fusion.9 = bf16[1,1,512,2048]{3,2,1,0:T(8,128)(2,1)} fusion(bf16[2048,2048]{1,0:T(8,128)(2,1)} %all-gather.2.cloned.1.call-done, bf16[512,1024]{1,0:T(8,128)(2,1)} %bitcast.19, bf16[512,1024]{1,0:T(8,128)(2,1)S(1)} %copy-done.19), kind=kOutput, calls=%fused_computation.18 | convolution fusion | flops 4300210176 | bytes 12582912 | tf_op jit(solution)/shard_map/dot_general | solution.py:139
  318.4 61.3 %all-to-all-done.3 = bf16[3,8,64,1024]{3,2,0,1:T(8,128)(2,1)} async-done(((bf16[3,8,64,1024]{3,2,0,1:T(8,128)(2,1)}), bf16[3,8,64,1024]{3,2,0,1:T(8,128)(2,1)}, u32[]{:S(2)}, u32[]{:S(2)}) %all-to-all-start.3) | async-done | bytes 3145760 | tf_op jit(solution)/shard_map/all_to_all | solution.py:120
  379.8 2.2 fusion.39
  382.0 1.5 maximum_bitcast_fusion.3
  383.5 1.5 maximum_bitcast_fusion.2
  385.0 1.5 maximum_bitcast_fusion.1
  386.5 1.8 convert_multiply_fusion
  (83 shorter events, 10.2 us)
Async XLA Ops:
  7.2 135.8 %copy-start = (bf16[1,1,512,2048]{3,2,1,0:T(8,128)(2,1)S(1)}, bf16[1,1,512,2048]{3,2,1,0:T(8,128)(2,1)}, u32[]{:S(2)}) copy-start(bf16[1,1,512,2048]{3,2,1,0:T(8,128)(2,1)} %param.10) | copy-start | bytes 6291460
  7.2 135.8 %all-gather.2.cloned.1.call-start = ((), (), s32[]{:S(2)}) async-start(), calls=%async_computation.5 | async-start | bytes 10485760 | tf_op jit(solution)/shard_map/all_gather | solution.py:82
  7.9 2.2 copy-start.16
  7.9 2.8 copy-start.17
  17.7 6.7 %copy-start.25 = (s32[4,4]{1,0:T(4,128)S(1)}, s32[4,4]{1,0:T(4,128)}, u32[]{:S(2)}) copy-start(s32[4,4]{1,0:T(4,128)} %param.12) | copy-start | bytes 196
  17.7 100.7 %all-to-all-start = ((bf16[1,3,512,1024]{3,1,0,2:T(4,128)(2,1)}), bf16[1,3,512,1024]{3,1,0,2:T(4,128)(2,1)}, u32[]{:S(2)}, u32[]{:S(2)}) async-start(bf16[1,3,512,1024]{3,1,0,2:T(4,128)(2,1)} %copy.147), calls=%async_computation | async-start | bytes 8388608 | tf_op jit(solution)/shard_map/all_to_all | solution.py:85
  24.7 8.5 %copy-start.14 = (pred[512,512]{0,1:T(8,128)(4,1)}, pred[512,512]{0,1:T(8,128)(4,1)S(1)}, u32[]{:S(2)}) copy-start(pred[512,512]{0,1:T(8,128)(4,1)S(1)} %fusion.20) | copy-start | bytes 786436
  24.7 5.5 %copy-start.24 = (s32[8,8]{1,0:T(8,128)S(1)}, s32[8,8]{1,0:T(8,128)}, u32[]{:S(2)}) copy-start(s32[8,8]{1,0:T(8,128)} %param.13) | copy-start | bytes 772
  27.6 5.6 %copy-start.9 = (bf16[1,1,512,1024]{2,3,1,0:T(8,128)(2,1)}, bf16[1,1,512,1024]{2,3,1,0:T(8,128)(2,1)S(1)}, u32[]{:S(2)}) copy-start(bf16[1,1,512,1024]{2,3,1,0:T(8,128)(2,1)S(1)} %copy.202) | copy-start | bytes 3145732
  30.3 99.6 %copy-start.23 = (pred[8,8]{1,0:T(8,128)(4,1)}, pred[8,8]{1,0:T(8,128)(4,1)S(1)}, u32[]{:S(2)}) copy-start(pred[8,8]{1,0:T(8,128)(4,1)S(1)} %broadcast_compare_fusion) | copy-start | bytes 196
  33.2 3.2 copy-start.2
  38.1 118.9 %copy-start.21 = (f32[8,512]{1,0:T(8,128)}, f32[8,512]{1,0:T(8,128)S(1)}, u32[]{:S(2)}) copy-start(f32[8,512]{1,0:T(8,128)S(1)} %fusion) | copy-start | bytes 49156
  122.5 11.5 %copy-start.7 = (bf16[64,8,8,128]{3,2,1,0:T(8,128)(2,1)}, bf16[64,8,8,128]{3,2,1,0:T(8,128)(2,1)S(1)}, u32[]{:S(2)}) copy-start(bf16[64,8,8,128]{3,2,1,0:T(8,128)(2,1)S(1)} %copy.204) | copy-start | bytes 3145732
  122.8 1.1 copy-start.5
  123.0 1.2 copy-start.6
  136.0 1.0 copy-start.3
  138.4 31.1 %all-to-all-start.1 = ((bf16[8,64,1024]{2,1,0:T(8,128)(2,1)}), bf16[8,64,1024]{2,1,0:T(8,128)(2,1)}, u32[]{:S(2)}, u32[]{:S(2)}) async-start(bf16[8,64,1024]{2,1,0:T(8,128)(2,1)} %reshape.92), calls=%async_computation.1 | async-start | bytes 2097152 | tf_op jit(solution)/shard_map/all_to_all | solution.py:91
  142.9 243.6 %reduce-scatter.2.cloned.1.call-start = ((), (), s32[]{:S(2)}) async-start(), calls=%async_computation.6 | async-start | bytes 8650752 | tf_op jit(solution)/shard_map/reduce_scatter | solution.py:111
  192.0 46.2 %all-to-all-start.2 = ((bf16[8,2,32768]{2,1,0:T(2,128)(2,1)}), bf16[8,2,32768]{2,1,0:T(2,128)(2,1)S(1)}, u32[]{:S(2)}, u32[]{:S(2)}) async-start(bf16[8,2,32768]{2,1,0:T(2,128)(2,1)} %reshape.105), calls=%async_computation.2 | async-start | bytes 2097152 | tf_op jit(solution)/shard_map/all_to_all | solution.py:114
  241.7 8.1 %copy-start.8 = (bf16[64,8,8,128]{3,2,1,0:T(8,128)(2,1)S(1)}, bf16[64,8,8,128]{3,2,1,0:T(8,128)(2,1)}, u32[]{:S(2)}) copy-start(bf16[64,8,8,128]{3,2,1,0:T(8,128)(2,1)} %copy-done.7) | copy-start | bytes 3145732
  252.5 3.6 copy-start.4
  275.7 1.4 copy-start.13
  281.1 4.6 %copy-start.22 = (f32[8,512]{1,0:T(8,128)S(1)}, f32[8,512]{1,0:T(8,128)}, u32[]{:S(2)}) copy-start(f32[8,512]{1,0:T(8,128)} %copy-done.21) | copy-start | bytes 49156
  281.1 6.1 %copy-start.15 = (pred[512,512]{0,1:T(8,128)(4,1)S(1)}, pred[512,512]{0,1:T(8,128)(4,1)}, u32[]{:S(2)}) copy-start(pred[512,512]{0,1:T(8,128)(4,1)} %copy-done.14) | copy-start | bytes 786436
  281.1 6.1 %copy-start.18 = (bf16[1,1,512,1024]{2,3,1,0:T(8,128)(2,1)S(1)}, bf16[1,1,512,1024]{2,3,1,0:T(8,128)(2,1)}, u32[]{:S(2)}) copy-start(bf16[1,1,512,1024]{2,3,1,0:T(8,128)(2,1)} %copy.145) | copy-start | bytes 3145732
  281.1 6.1 %copy-start.26 = (f32[8,512]{1,0:T(8,128)S(1)}, f32[8,512]{1,0:T(8,128)}, u32[]{:S(2)}) copy-start(f32[8,512]{1,0:T(8,128)} %get-tuple-element.27) | copy-start | bytes 49156
  281.1 98.6 %all-to-all-start.3 = ((bf16[3,8,64,1024]{3,2,0,1:T(8,128)(2,1)}), bf16[3,8,64,1024]{3,2,0,1:T(8,128)(2,1)}, u32[]{:S(2)}, u32[]{:S(2)}) async-start(bf16[3,8,64,1024]{3,2,0,1:T(8,128)(2,1)} %copy.173), calls=%async_computation.3 | async-start | bytes 6291456 | tf_op jit(solution)/shard_map/all_to_all | solution.py:120
  287.2 5.8 %copy-start.10 = (bf16[1,1,512,1024]{2,3,1,0:T(8,128)(2,1)S(1)}, bf16[1,1,512,1024]{2,3,1,0:T(8,128)(2,1)}, u32[]{:S(2)}) copy-start(bf16[1,1,512,1024]{2,3,1,0:T(8,128)(2,1)} %copy-done.9) | copy-start | bytes 3145732
  293.0 2.0 copy-start.11
  295.6 5.4 %copy-start.20 = (bf16[512,8,128]{0,2,1:T(8,128)(2,1)S(1)}, bf16[512,8,128]{0,2,1:T(8,128)(2,1)}, u32[]{:S(2)}) copy-start(bf16[512,8,128]{0,2,1:T(8,128)(2,1)} %copy.177) | copy-start | bytes 3145732
  301.0 7.9 %copy-start.19 = (bf16[512,1024]{1,0:T(8,128)(2,1)S(1)}, bf16[512,1024]{1,0:T(8,128)(2,1)}, u32[]{:S(2)}) copy-start(bf16[512,1024]{1,0:T(8,128)(2,1)} %copy.155) | copy-start | bytes 3145732
  382.0 1.5 copy-start.12
  383.5 4.8 %copy-start.1 = (bf16[1,1,512,2048]{3,2,1,0:T(8,128)(2,1)S(1)}, bf16[1,1,512,2048]{3,2,1,0:T(8,128)(2,1)}, u32[]{:S(2)}) copy-start(bf16[1,1,512,2048]{3,2,1,0:T(8,128)(2,1)} %param.10) | copy-start | bytes 6291460
Sparse Core Ops, SparseCore 0:
  9.9 90.2 all-gather.1
  178.4 182.5 reduce-scatter.1
